TPU v7x, 32 devices: a whole 2x2x4 slice. The times are simulated.
32 devices in a mesh: wide: 8 (over z, x), narrow: 4 (over y, core).
Axes of the slice: x: 2, y: 2, z: 4, core: 2. Of those that a mesh axis runs over, the one named last changes fastest.
Arguments:
- stream: bfloat16 [64, 1048576], P(None, ('wide', 'narrow')), may hold values from -96 to 96
- target: bfloat16 [1048576], P(('wide', 'narrow')), may hold values from -400 to 400
- depthwise_taps: float32 [4, 16, 64], replicated, may hold values from -1.5 to 1.5
Outputs:
- coefficients: float32 [256], replicated
- residual: float32 [1048576], P(('wide', 'narrow'))
All inputs are finite; a program needn't handle non-finite values.
Results may differ from a plain program's by a relative error of at most 0.0004.
The roundings to bfloat16 on the way count: a program that leaves them out, or rounds other values in their place, can miss the bound.
Values may be sent and summed in bfloat16 or wider, within the bound.
No kernel may reach another device: no remote copies, remote signals or barrier semaphores. Data moves between devices by JAX's collectives and lax.ppermute only.
A program may use at most 128 MiB of HBM per device.

v0:
```python
import functools

import jax
import jax.numpy as jnp
from jax import lax
from jax.sharding import PartitionSpec as P
from jax.experimental import pallas as pl
from jax.experimental.pallas import tpu as pltpu

ridge_share = 0.05


def shifted(array, axis, by):
    size = lax.axis_size(axis)
    pairs = [(i, i + by) for i in range(size) if 0 <= i + by < size]
    return lax.ppermute(array, axis, pairs)


def dilation_list(top_dilation):
    return (1, top_dilation // 16, top_dilation // 4, top_dilation)


def filter_bank(window, depthwise_taps, top_dilation, history_len, length):
    row_list = []
    for j, d in enumerate(dilation_list(top_dilation)):
        total = jnp.zeros((window.shape[0], length), jnp.float32)
        for k in range(depthwise_taps.shape[1]):
            start_offset = history_len - 1 - k * d
            total = (
                total
                + depthwise_taps[j, k][:, None] * window[:, start_offset : start_offset + length]
            )
        row_list.append(total.astype(jnp.bfloat16))
    return jnp.concatenate(row_list, 0)


TIME_BLOCK = 2048
CHUNK = 256


def feature_kernel(dilations, span, taps_per_filter, chunk, w_ref, taps_ref, tgt_ref, f_ref, g_ref, c_ref):
    block = pl.program_id(0)
    block_len = f_ref.shape[1]
    channels = w_ref.shape[0]

    @pl.when(block == 0)
    def _():
        g_ref[...] = jnp.zeros_like(g_ref)
        c_ref[...] = jnp.zeros_like(c_ref)

    for j, d in enumerate(dilations):
        def chunk_body(i, carry, j=j, d=d):
            start = pl.multiple_of(block * block_len + i * chunk, 128)
            slabs = {}
            acc = None
            for k in range(taps_per_filter):
                offset = span - k * d
                r = offset % 128
                a = offset - r
                if r == 0:
                    x = w_ref[:, pl.ds(pl.multiple_of(start + a, 128), chunk)].astype(jnp.float32)
                else:
                    if a not in slabs:
                        slabs[a] = w_ref[:, pl.ds(pl.multiple_of(start + a, 128), chunk + 128)].astype(jnp.float32)
                    x = slabs[a][:, r:r + chunk]
                w = jnp.tile(taps_ref[j * taps_per_filter + k], (1, chunk // 128))
                acc = w * x if acc is None else acc + w * x
            f_ref[j * channels:(j + 1) * channels, pl.ds(pl.multiple_of(i * chunk, 128), chunk)] = acc.astype(f_ref.dtype)
            return carry

        lax.fori_loop(0, block_len // chunk, chunk_body, 0)

    feats = f_ref[...]
    g_ref[...] += lax.dot_general(feats, feats, (((1,), (1,)), ((), ())), preferred_element_type=jnp.float32)
    c_ref[...] += lax.dot_general(tgt_ref[...], feats, (((1,), (1,)), ((), ())), preferred_element_type=jnp.float32)


def features_and_sums(window, depthwise_taps, target, top_dilation, length, interpret=False):
    channels = window.shape[0]
    dilations = dilation_list(top_dilation)
    n_filters, taps_per_filter = len(dilations), depthwise_taps.shape[1]
    span = (taps_per_filter - 1) * top_dilation
    rows = n_filters * channels
    block_len = min(TIME_BLOCK, length)
    taps = jnp.broadcast_to(
        depthwise_taps.reshape(n_filters * taps_per_filter, channels, 1),
        (n_filters * taps_per_filter, channels, 128),
    )
    kernel = functools.partial(feature_kernel, dilations, span, taps_per_filter, min(CHUNK, block_len))
    return pl.pallas_call(
        kernel,
        grid=(length // block_len,),
        in_specs=[
            pl.BlockSpec(memory_space=pltpu.VMEM),
            pl.BlockSpec(memory_space=pltpu.VMEM),
            pl.BlockSpec((1, block_len), lambda b: (0, b)),
        ],
        out_specs=[
            pl.BlockSpec((rows, block_len), lambda b: (0, b)),
            pl.BlockSpec((rows, rows), lambda b: (0, 0)),
            pl.BlockSpec((1, rows), lambda b: (0, 0)),
        ],
        out_shape=[
            jax.ShapeDtypeStruct((rows, length), jnp.bfloat16),
            jax.ShapeDtypeStruct((rows, rows), jnp.float32),
            jax.ShapeDtypeStruct((1, rows), jnp.float32),
        ],
        compiler_params=pltpu.CompilerParams(
            dimension_semantics=("arbitrary",), vmem_limit_bytes=48 * 1024 * 1024
        ),
        interpret=interpret,
    )(window, taps, target.reshape(1, length))


def ridge_solve(system, cross_sum):
    factor = jnp.linalg.cholesky(system)
    middle = lax.linalg.triangular_solve(factor, cross_sum[:, None], left_side=True, lower=True)
    answer = lax.linalg.triangular_solve(
        factor, middle, left_side=True, lower=True, transpose_a=True
    )
    return answer[:, 0]


def butterfly_sum(x, axes):
    size = 1
    for name in axes:
        size *= lax.axis_size(name)
    if size & (size - 1):
        return lax.psum(x, axes)
    step = 1
    while step < size:
        x = x + lax.ppermute(x, axes, [(i, i ^ step) for i in range(size)])
        step *= 2
    return x


def reduce_system(gram_sum, cross_sum, axes):
    n = gram_sum.shape[0]
    h = n // 2
    rows = lax.broadcasted_iota(jnp.int32, (h, h), 0)
    cols = lax.broadcasted_iota(jnp.int32, (h, h), 1)
    lead, off, trail = gram_sum[:h, :h], gram_sum[:h, h:], gram_sum[h:, h:]
    folded = jnp.where(rows <= cols, lead, trail)
    extra = jnp.stack([cross_sum, jnp.concatenate([jnp.diagonal(trail), jnp.zeros((n - h,), jnp.float32)])])
    packed = jnp.concatenate([jnp.concatenate([folded, off], 1), extra], 0)
    packed = butterfly_sum(packed, axes)
    folded, off = packed[:h, :h], packed[:h, h:]
    upper = jnp.where(rows <= cols, folded, 0.0)
    lead = upper + jnp.where(rows < cols, folded, 0.0).T
    strict = jnp.where(rows > cols, folded, 0.0)
    trail = strict + strict.T + jnp.diag(packed[h + 1, :h])
    gram_sum = jnp.concatenate(
        [jnp.concatenate([lead, off], 1), jnp.concatenate([off.T, trail], 1)], 0
    )
    return gram_sum, packed[h]


def local(stream, target, depthwise_taps):
    length = stream.shape[1]
    top_dilation = min(1024, length // 16)
    history_len = 15 * top_dilation + 1
    tail_end = stream[:, length - history_len :]
    previous = shifted(tail_end, ("wide", "narrow"), 1)
    window = jnp.concatenate([previous, stream], 1)[:, : history_len - 1 + length]
    features, gram_sum, cross_sum = features_and_sums(window, depthwise_taps, target, top_dilation, length)
    cross_sum = cross_sum[0]
    gram_sum, cross_sum = reduce_system(gram_sum, cross_sum, ("wide", "narrow"))
    total_rows = length * lax.axis_size("wide") * lax.axis_size("narrow")
    system = gram_sum + ridge_share * total_rows * jnp.eye(gram_sum.shape[0], dtype=jnp.float32)
    coefficients = ridge_solve(system, cross_sum)
    rounded = coefficients.astype(jnp.bfloat16)
    fitted = jnp.dot(rounded, features, preferred_element_type=jnp.float32)
    return (coefficients, target.astype(jnp.float32) - fitted)


def solution(mesh):
    in_specs = (P(None, ("wide", "narrow")), P(("wide", "narrow")), P())
    out_specs = (P(), P(("wide", "narrow")))
    return jax.shard_map(local, mesh=mesh, in_specs=in_specs, out_specs=out_specs, check_vma=False)
```

profile of v0, /device:TPU:0, one launch (start us, length us, event | category | flops | bytes accessed | tf_op | source)
XLA Modules:
  0.0 242.0 jit_solution(14997003552058133761)
XLA Ops:
  0.6 2.1 slice.81
  2.8 2.5 %collective-permute-start = (bf16[64,15361]{1,0:T(8,128)(2,1)S(1)}, bf16[64,15361]{1,0:T(8,128)(2,1)S(1)}, u32[]{:S(2)}, u32[]{:S(2)}) collective-permute-start(bf16[64,15361]{1,0:T(8,128)(2,1)S(1)} %slice.81), channel_id=1, source_target_pairs={{0,1},{1,2},{2,3},{3,4},{4,5},{5,6},{6,7},{7,8},{8,9},{9,10},{10,1... | collective-permute-start | bytes 5898632 | tf_op jit(solution)/shard_map/ppermute | solution.py:16
  5.3 0.9 reshape.57.tgt_ref
  6.2 2.5 %collective-permute-done = bf16[64,15361]{1,0:T(8,128)(2,1)S(1)} collective-permute-done((bf16[64,15361]{1,0:T(8,128)(2,1)S(1)}, bf16[64,15361]{1,0:T(8,128)(2,1)S(1)}, u32[]{:S(2)}, u32[]{:S(2)}) %collective-permute-start) | collective-permute-done | bytes 1966240 | tf_op jit(solution)/shard_map/ppermute | solution.py:16
  8.8 6.1 %pad_maximum_fusion.w_ref = bf16[64,48128]{1,0:T(8,128)(2,1)} fusion(bf16[64,32768]{1,0:T(8,128)(2,1)} %param.3, bf16[64,15361]{1,0:T(8,128)(2,1)S(1)} %collective-permute-done), kind=kLoop, calls=%fused_computation.3 | loop fusion | flops 12320768 | bytes 12320896 | tf_op jit(solution)/shard_map/concatenate | solution.py:164
  14.8 0.6 broadcast_in_dim.39.taps_ref
  15.4 105.1 %shard_map.50 = (bf16[256,32768]{1,0:T(8,128)(2,1)}, f32[256,256]{1,0:T(8,128)S(1)}, f32[1,256]{1,0:T(1,128)S(1)}) custom-call(bf16[64,48128]{1,0:T(8,128)(2,1)} %pad_maximum_fusion.w_ref, f32[64,64,128]{2,1,0:T(8,128)S(1)} %broadcast_in_dim.39.taps_ref, bf16[1,32768]{1,0:T(2,128)(2,1)S(1)} %reshape.57.tgt_ref), custom_call_target="tpu_custom_call" | custom-call | tf_op jit(solution)/shard_map/pallas_call | solution.py:90
  120.5 1.4 gather_fusion
  122.0 20.8 %collective-permute-start.1 = (f32[130,256]{1,0:T(8,128)S(1)}, f32[130,256]{1,0:T(8,128)S(1)}, u32[]{:S(2)}, u32[]{:S(2)}) collective-permute-start(f32[130,256]{1,0:T(8,128)S(1)} %pad_maximum_fusion.1), channel_id=1, source_target_pairs={{0,1},{1,0},{2,3},{3,2},{4,5},{5,4},{6,7},{7,6},{8,9},{9,8},{10,11... | collective-permute-start | bytes 399368 | tf_op jit(solution)/shard_map/ppermute | solution.py:132
  142.8 1.0 collective-permute-done.1
  143.8 2.8 %collective-permute-start.2 = (f32[130,256]{1,0:T(8,128)S(1)}, f32[130,256]{1,0:T(8,128)S(1)}, u32[]{:S(2)}, u32[]{:S(2)}) collective-permute-start(f32[130,256]{1,0:T(8,128)S(1)} %fusion.14), channel_id=1, source_target_pairs={{0,2},{1,3},{2,0},{3,1},{4,6},{5,7},{6,4},{7,5},{8,10},{9,11},{10,... | collective-permute-start | bytes 399368 | tf_op jit(solution)/shard_map/ppermute | solution.py:132
  146.6 4.0 %collective-permute-done.2 = f32[130,256]{1,0:T(8,128)S(1)} collective-permute-done((f32[130,256]{1,0:T(8,128)S(1)}, f32[130,256]{1,0:T(8,128)S(1)}, u32[]{:S(2)}, u32[]{:S(2)}) %collective-permute-start.2) | collective-permute-done | bytes 133152 | tf_op jit(solution)/shard_map/ppermute | solution.py:132
  150.6 2.7 %collective-permute-start.3 = (f32[130,256]{1,0:T(8,128)S(1)}, f32[130,256]{1,0:T(8,128)S(1)}, u32[]{:S(2)}, u32[]{:S(2)}) collective-permute-start(f32[130,256]{1,0:T(8,128)S(1)} %add.58), channel_id=1, source_target_pairs={{0,4},{1,5},{2,6},{3,7},{4,0},{5,1},{6,2},{7,3},{8,12},{9,13},{10,... | collective-permute-start | bytes 399368 | tf_op jit(solution)/shard_map/ppermute | solution.py:132
  153.3 3.1 %collective-permute-done.3 = f32[130,256]{1,0:T(8,128)S(1)} collective-permute-done((f32[130,256]{1,0:T(8,128)S(1)}, f32[130,256]{1,0:T(8,128)S(1)}, u32[]{:S(2)}, u32[]{:S(2)}) %collective-permute-start.3) | collective-permute-done | bytes 133152 | tf_op jit(solution)/shard_map/ppermute | solution.py:132
  156.5 3.0 %collective-permute-start.4 = (f32[130,256]{1,0:T(8,128)S(1)}, f32[130,256]{1,0:T(8,128)S(1)}, u32[]{:S(2)}, u32[]{:S(2)}) collective-permute-start(f32[130,256]{1,0:T(8,128)S(1)} %add.59), channel_id=1, source_target_pairs={{0,8},{1,9},{2,10},{3,11},{4,12},{5,13},{6,14},{7,15},{8,0},{9,1},... | collective-permute-start | bytes 399368 | tf_op jit(solution)/shard_map/ppermute | solution.py:132
  159.4 3.0 %collective-permute-done.4 = f32[130,256]{1,0:T(8,128)S(1)} collective-permute-done((f32[130,256]{1,0:T(8,128)S(1)}, f32[130,256]{1,0:T(8,128)S(1)}, u32[]{:S(2)}, u32[]{:S(2)}) %collective-permute-start.4) | collective-permute-done | bytes 133152 | tf_op jit(solution)/shard_map/ppermute | solution.py:132
  162.5 3.5 %collective-permute-start.5 = (f32[130,256]{1,0:T(8,128)S(1)}, f32[130,256]{1,0:T(8,128)S(1)}, u32[]{:S(2)}, u32[]{:S(2)}) collective-permute-start(f32[130,256]{1,0:T(8,128)S(1)} %add.60), channel_id=1, source_target_pairs={{0,16},{1,17},{2,18},{3,19},{4,20},{5,21},{6,22},{7,23},{8,24},{9,... | collective-permute-start | bytes 399368 | tf_op jit(solution)/shard_map/ppermute | solution.py:132
  166.0 4.5 %collective-permute-done.5 = f32[130,256]{1,0:T(8,128)S(1)} collective-permute-done((f32[130,256]{1,0:T(8,128)S(1)}, f32[130,256]{1,0:T(8,128)S(1)}, u32[]{:S(2)}, u32[]{:S(2)}) %collective-permute-start.5) | collective-permute-done | bytes 133152 | tf_op jit(solution)/shard_map/ppermute | solution.py:132
  171.2 11.7 %cholesky.58 = f32[128,128]{1,0:T(8,128)S(1)} custom-call(f32[128,128]{1,0:T(8,128)S(1)} %cholesky.129), custom_call_target="Cholesky" | custom-call | tf_op jit(solution)/shard_map/jit(cholesky)/cholesky | solution.py:116
  183.3 9.8 %custom-call.16 = f32[1,128,128]{1,2,0:T(8,128)S(1)} custom-call(f32[1,128,128]{2,1,0:T(8,128)S(1)} %copy.27), custom_call_target="InvertDiagBlocksLowerTriangular" | custom-call | tf_op jit(solution)/shard_map/jit(cholesky)/cholesky | solution.py:116
  193.4 0.3 convolution_subtract_fusion
  193.7 11.7 %cholesky.117 = f32[128,128]{1,0:T(8,128)S(1)} custom-call(f32[128,128]{1,0:T(8,128)S(1)} %convolution_subtract_fusion), custom_call_target="Cholesky" | custom-call | tf_op jit(solution)/shard_map/jit(cholesky)/cholesky | solution.py:116
  205.6 0.7 compare_reduce_fusion
  207.8 4.3 %while.1 = (s32[]{:T(128)}, f32[256,256]{0,1:T(8,128)S(1)}, s32[2,2]{1,0:T(2,128)S(1)}, f32[2,128,128]{2,1,0:T(8,128)S(1)}, s32[]{:T(128)}) while((s32[]{:T(128)}, f32[256,256]{0,1:T(8,128)S(1)}, s32[2,2]{1,0:T(2,128)S(1)}, f32[2,128,128]{2,1,0:T(8,128)S(1)}, s32[]{:T(128)}) %tuple.32), condition=%wide.while_cond, body=%wide.while_body.sunk | while | flops 2 | bytes 393321 | solution.py:118
  207.8 0.6 fusion.24
  208.4 1.4 dynamic-slice.7
  210.0 0.6 fusion.24
  210.6 1.4 dynamic-slice.7
  212.1 19.9 %custom-call.17 = f32[2,128,128]{1,2,0:T(8,128)S(1)} custom-call(f32[2,128,128]{2,1,0:T(8,128)S(1)} %get-tuple-element.15), custom_call_target="InvertDiagBlocksLowerTriangular" | custom-call | tf_op jit(solution)/shard_map/triangular_solve | solution.py:118
  232.7 0.2 convolution_bitcast_fusion.1
  233.3 8.1 %fusion.16 = f32[1,32768]{1,0:T(1,128)S(1)} fusion(bf16[256,1]{0,1:T(2,128)(2,1)S(1)} %reshape.96, bf16[256,32768]{1,0:T(8,128)(2,1)} %get-tuple-element.7), kind=kOutput, calls=%fused_computation.58 | convolution fusion | flops 16777216 | bytes 16908800 | tf_op jit(solution)/shard_map/dot_general | solution.py:172
  241.3 0.7 convert_subtract_fusion
  (55 shorter events, 2.8 us)
Async XLA Ops:
  2.8 6.0 %collective-permute-start = (bf16[64,15361]{1,0:T(8,128)(2,1)S(1)}, bf16[64,15361]{1,0:T(8,128)(2,1)S(1)}, u32[]{:S(2)}, u32[]{:S(2)}) collective-permute-start(bf16[64,15361]{1,0:T(8,128)(2,1)S(1)} %slice.81), channel_id=1, source_target_pairs={{0,1},{1,2},{2,3},{3,4},{4,5},{5,6},{6,7},{7,8},{8,9},{9,10},{10,1... | collective-permute-start | bytes 5898632 | tf_op jit(solution)/shard_map/ppermute | solution.py:16
  6.2 8.6 %copy-start.1 = (f32[4,16,64]{2,1,0:T(8,128)S(1)}, f32[4,16,64]{2,1,0:T(8,128)}, u32[]{:S(2)}) copy-start(f32[4,16,64]{2,1,0:T(8,128)} %param.5) | copy-start | bytes 49156
  122.0 21.8 %collective-permute-start.1 = (f32[130,256]{1,0:T(8,128)S(1)}, f32[130,256]{1,0:T(8,128)S(1)}, u32[]{:S(2)}, u32[]{:S(2)}) collective-permute-start(f32[130,256]{1,0:T(8,128)S(1)} %pad_maximum_fusion.1), channel_id=1, source_target_pairs={{0,1},{1,0},{2,3},{3,2},{4,5},{5,4},{6,7},{7,6},{8,9},{9,8},{10,11... | collective-permute-start | bytes 399368 | tf_op jit(solution)/shard_map/ppermute | solution.py:132
  143.8 6.8 %collective-permute-start.2 = (f32[130,256]{1,0:T(8,128)S(1)}, f32[130,256]{1,0:T(8,128)S(1)}, u32[]{:S(2)}, u32[]{:S(2)}) collective-permute-start(f32[130,256]{1,0:T(8,128)S(1)} %fusion.14), channel_id=1, source_target_pairs={{0,2},{1,3},{2,0},{3,1},{4,6},{5,7},{6,4},{7,5},{8,10},{9,11},{10,... | collective-permute-start | bytes 399368 | tf_op jit(solution)/shard_map/ppermute | solution.py:132
  150.6 5.8 %collective-permute-start.3 = (f32[130,256]{1,0:T(8,128)S(1)}, f32[130,256]{1,0:T(8,128)S(1)}, u32[]{:S(2)}, u32[]{:S(2)}) collective-permute-start(f32[130,256]{1,0:T(8,128)S(1)} %add.58), channel_id=1, source_target_pairs={{0,4},{1,5},{2,6},{3,7},{4,0},{5,1},{6,2},{7,3},{8,12},{9,13},{10,... | collective-permute-start | bytes 399368 | tf_op jit(solution)/shard_map/ppermute | solution.py:132
  156.5 6.0 %collective-permute-start.4 = (f32[130,256]{1,0:T(8,128)S(1)}, f32[130,256]{1,0:T(8,128)S(1)}, u32[]{:S(2)}, u32[]{:S(2)}) collective-permute-start(f32[130,256]{1,0:T(8,128)S(1)} %add.59), channel_id=1, source_target_pairs={{0,8},{1,9},{2,10},{3,11},{4,12},{5,13},{6,14},{7,15},{8,0},{9,1},... | collective-permute-start | bytes 399368 | tf_op jit(solution)/shard_map/ppermute | solution.py:132
  162.5 8.1 %collective-permute-start.5 = (f32[130,256]{1,0:T(8,128)S(1)}, f32[130,256]{1,0:T(8,128)S(1)}, u32[]{:S(2)}, u32[]{:S(2)}) collective-permute-start(f32[130,256]{1,0:T(8,128)S(1)} %add.60), channel_id=1, source_target_pairs={{0,16},{1,17},{2,18},{3,19},{4,20},{5,21},{6,22},{7,23},{8,24},{9,... | collective-permute-start | bytes 399368 | tf_op jit(solution)/shard_map/ppermute | solution.py:132
  233.2 8.2 %copy-start.2 = (f32[256,1]{0,1:T(1,128)}, f32[256,1]{0,1:T(1,128)S(1)}, u32[]{:S(2)}) copy-start(f32[256,1]{0,1:T(1,128)S(1)} %pad_maximum_fusion.3) | copy-start | bytes 3076
  233.2 8.1 %copy-start = (bf16[32768]{0:T(1024)(128)(2,1)S(1)}, bf16[32768]{0:T(1024)(128)(2,1)}, u32[]{:S(2)}) copy-start(bf16[32768]{0:T(1024)(128)(2,1)} %param.4) | copy-start | bytes 196612
where the time goes:
time: 242 us
  Pallas kernels  105 us (43%)
  other arithmetic  61.1 us (25%)
  starting transfers between devices  35.3 us (15%)
  waiting for transfers between devices  18.2 us (8%)
  local copies, waits for them, and re-layouts  10.3 us (4%)
  matrix products  9.69 us (4%)
    pallas_call x1, Pallas kernels, features_and_sums(): pl.pallas_call(kernel, grid=(length // block_len,), in_specs=[pl.BlockSpe...  105 us
    another operation x6, other arithmetic, ridge_solve(): factor = jnp.linalg.cholesky(system)  34.2 us
    ppermute x5, starting transfers between devices, butterfly_sum(): x = x + lax.ppermute(x, axes, [(i, i ^ step) for i in range(size)])  32.8 us
    another operation x4, other arithmetic, ridge_solve(): lax.linalg.triangular_solve(factor, middle, left_side=True, lower=True, t...  19.9 us
    ppermute x5, waiting for transfers between devices, butterfly_sum(): x = x + lax.ppermute(x, axes, [(i, i ^ step) for i in range(size)])  15.7 us
    dot_general x1, matrix products, local(): fitted = jnp.dot(rounded, features, preferred_element_type=jnp.float32)  8.07 us
    concatenate x1, other arithmetic, local(): jnp.concatenate([previous, stream], 1)[:, :history_len - 1 + length]  6.06 us
  transfers between devices with their start and end apart: 6, of which 6 were waited for; matrix products, arithmetic and copies ran while one was open for 0% of the time, Pallas kernels for 0%

commit v1 on v0

--- a/solution.py
+++ b/solution.py
@@ -112,6 +112,53 @@
     )(window, taps, target.reshape(1, length))
 
 
+def solve_kernel(system_ref, c_ref, x_ref, a_ref, lt_ref):
+    n = a_ref.shape[0]
+    a_ref[...] = system_ref[...]
+    lanes = lax.broadcasted_iota(jnp.int32, (1, n), 1)
+
+    def pick(vec, at):
+        return jnp.sum(jnp.where(at, vec, 0.0), axis=1, keepdims=True)
+
+    def factor_step(j, carry):
+        rhs, forward, diag = carry
+        at = lanes == j
+        row = a_ref[pl.ds(j, 1), :]
+        root = jnp.sqrt(pick(row, at))
+        col_j = jnp.where(lanes >= j, row / root, 0.0)
+        lt_ref[pl.ds(j, 1), :] = col_j
+        yj = pick(rhs, at) / root
+        rhs = rhs - yj * col_j
+        forward = jnp.where(at, yj, forward)
+        diag = jnp.where(at, root, diag)
+        column = jnp.transpose(jnp.broadcast_to(col_j, (8, n)))[:, 0:1]
+        a_ref[...] = a_ref[...] - column * col_j
+        return rhs, forward, diag
+
+    zeros = jnp.zeros((1, n), jnp.float32)
+    _, forward, diag = lax.fori_loop(0, n, factor_step, (c_ref[...], zeros, zeros))
+
+    def back_step(t, x):
+        j = n - 1 - t
+        at = lanes == j
+        partial = jnp.sum(lt_ref[pl.ds(j, 1), :] * x, axis=1, keepdims=True)
+        return jnp.where(at, (pick(forward, at) - partial) / pick(diag, at), x)
+
+    x_ref[...] = lax.fori_loop(0, n, back_step, zeros)
+
+
+def ridge_solve_kernel(system, cross_sum, interpret=False):
+    n = system.shape[0]
+    return pl.pallas_call(
+        solve_kernel,
+        in_specs=[pl.BlockSpec(memory_space=pltpu.VMEM), pl.BlockSpec(memory_space=pltpu.VMEM)],
+        out_specs=pl.BlockSpec(memory_space=pltpu.VMEM),
+        out_shape=jax.ShapeDtypeStruct((1, n), jnp.float32),
+        scratch_shapes=[pltpu.VMEM((n, n), jnp.float32), pltpu.VMEM((n, n), jnp.float32)],
+        interpret=interpret,
+    )(system, cross_sum.reshape(1, n))[0]
+
+
 def ridge_solve(system, cross_sum):
     factor = jnp.linalg.cholesky(system)
     middle = lax.linalg.triangular_solve(factor, cross_sum[:, None], left_side=True, lower=True)
@@ -167,7 +214,7 @@
     gram_sum, cross_sum = reduce_system(gram_sum, cross_sum, ("wide", "narrow"))
     total_rows = length * lax.axis_size("wide") * lax.axis_size("narrow")
     system = gram_sum + ridge_share * total_rows * jnp.eye(gram_sum.shape[0], dtype=jnp.float32)
-    coefficients = ridge_solve(system, cross_sum)
+    coefficients = ridge_solve_kernel(system, cross_sum)
     rounded = coefficients.astype(jnp.bfloat16)
     fitted = jnp.dot(rounded, features, preferred_element_type=jnp.float32)
     return (coefficients, target.astype(jnp.float32) - fitted)

time: 242 us -> 309 us (1.28)
  Pallas kernels: 105 us -> 219 us
  other arithmetic: 61.1 us -> 7.9 us
  waiting for transfers between devices: 18.2 us -> 30.7 us
    pallas_call x0 -> x1, Pallas kernels: none -> 114 us  [ridge_solve_kernel(): pl.pallas_call(solve_kernel, in_specs=[pl.BlockSpec(memory_space=pltpu.VM...]
    another operation x10 -> x0, other arithmetic: 54.1 us -> none  [the longest x6 34.2 us: ridge_solve(): factor = jnp.linalg.cholesky(system)]
    ppermute x5, waiting for transfers between devices: 15.7 us -> 28.1 us  [butterfly_sum(): x = x + lax.ppermute(x, axes, [(i, i ^ step) for i in range(size)])]
    another operation x18 -> x1, local copies, waits for them, and re-layouts: 4.72 us -> 0.13 us  [reduce_system(): jnp.stack([cross_sum, jnp.concatenate([jnp.diagonal(trail), jnp.zeros((n...]
where the time goes in v1:
time: 309 us; the launch traced here: 308 us
  Pallas kernels  219 us (71%)
  starting transfers between devices  34.4 us (11%)
  waiting for transfers between devices  30.7 us (10%)
  matrix products  8.07 us (3%)
  other arithmetic  7.9 us (3%)
  local copies, waits for them, and re-layouts  7.32 us (2%)
    pallas_call x1, Pallas kernels, ridge_solve_kernel(): pl.pallas_call(solve_kernel, in_specs=[pl.BlockSpec(memory_space=pltpu.VM...  114 us
    pallas_call x1, Pallas kernels, features_and_sums(): pl.pallas_call(kernel, grid=(length // block_len,), in_specs=[pl.BlockSpe...  105 us
    ppermute x5, starting transfers between devices, butterfly_sum(): x = x + lax.ppermute(x, axes, [(i, i ^ step) for i in range(size)])  31.9 us
    ppermute x5, waiting for transfers between devices, butterfly_sum(): x = x + lax.ppermute(x, axes, [(i, i ^ step) for i in range(size)])  28.1 us
    dot_general x1, matrix products, local(): fitted = jnp.dot(rounded, features, preferred_element_type=jnp.float32)  8.07 us
  transfers between devices with their start and end apart: 6, of which 6 were waited for; matrix products, arithmetic and copies ran while one was open for 0% of the time, Pallas kernels for 0%

profile of v1, /device:TPU:0, one launch (start us, length us, event | category | flops | bytes accessed | tf_op | source)
XLA Modules:
  0.0 308.3 jit_solution(15779251912548809827)
XLA Ops:
  0.6 2.1 slice.27
  2.8 2.5 collective-permute-start
  5.3 0.9 reshape.11.tgt_ref
  6.2 2.5 collective-permute-done
  8.8 6.0 %pad_maximum_fusion.w_ref = bf16[64,48128]{1,0:T(8,128)(2,1)} fusion(bf16[64,32768]{1,0:T(8,128)(2,1)} %param.3, bf16[64,15361]{1,0:T(8,128)(2,1)S(1)} %collective-permute-done), kind=kLoop, calls=%fused_computation.1 | loop fusion | flops 12320768 | bytes 12320896 | tf_op jit(solution)/shard_map/concatenate | solution.py:211
  14.8 0.6 broadcast_in_dim.37.taps_ref
  15.4 105.1 %shard_map.50 = (bf16[256,32768]{1,0:T(8,128)(2,1)}, f32[256,256]{1,0:T(8,128)S(1)}, f32[1,256]{1,0:T(1,128)S(1)}) custom-call(bf16[64,48128]{1,0:T(8,128)(2,1)} %pad_maximum_fusion.w_ref, f32[64,64,128]{2,1,0:T(8,128)S(1)} %broadcast_in_dim.37.taps_ref, bf16[1,32768]{1,0:T(2,128)(2,1)S(1)} %reshape.11.tgt_ref), custom_call_target="tpu_custom_call" | custom-call | tf_op jit(solution)/shard_map/pallas_call | solution.py:90
  120.5 0.1 copy.19
  120.7 1.3 gather_fusion
  122.0 0.1 copy.23
  122.1 0.1 copy.22
  122.2 0.1 pad_maximum_fusion.1
  122.4 20.8 %collective-permute-start.1 = (f32[130,256]{0,1:T(8,128)S(1)}, f32[130,256]{0,1:T(8,128)S(1)}, u32[]{:S(2)}, u32[]{:S(2)}) collective-permute-start(f32[130,256]{0,1:T(8,128)S(1)} %pad_maximum_fusion.1), channel_id=1, source_target_pairs={{0,1},{1,0},{2,3},{3,2},{4,5},{5,4},{6,7},{7,6},{8,9},{9,8},{10,11... | collective-permute-start | bytes 399368 | tf_op jit(solution)/shard_map/ppermute | solution.py:179
  143.2 1.2 collective-permute-done.1
  144.3 0.1 fusion.6
  144.4 2.8 collective-permute-start.2
  147.2 6.6 %collective-permute-done.2 = f32[130,256]{0,1:T(8,128)S(1)} collective-permute-done((f32[130,256]{0,1:T(8,128)S(1)}, f32[130,256]{0,1:T(8,128)S(1)}, u32[]{:S(2)}, u32[]{:S(2)}) %collective-permute-start.2) | collective-permute-done | bytes 133152 | tf_op jit(solution)/shard_map/ppermute | solution.py:179
  153.9 2.7 collective-permute-start.3
  156.6 5.8 %collective-permute-done.3 = f32[130,256]{0,1:T(8,128)S(1)} collective-permute-done((f32[130,256]{0,1:T(8,128)S(1)}, f32[130,256]{0,1:T(8,128)S(1)}, u32[]{:S(2)}, u32[]{:S(2)}) %collective-permute-start.3) | collective-permute-done | bytes 133152 | tf_op jit(solution)/shard_map/ppermute | solution.py:179
  162.4 2.8 collective-permute-start.4
  165.1 4.9 %collective-permute-done.4 = f32[130,256]{0,1:T(8,128)S(1)} collective-permute-done((f32[130,256]{0,1:T(8,128)S(1)}, f32[130,256]{0,1:T(8,128)S(1)}, u32[]{:S(2)}, u32[]{:S(2)}) %collective-permute-start.4) | collective-permute-done | bytes 133152 | tf_op jit(solution)/shard_map/ppermute | solution.py:179
  170.1 2.8 collective-permute-start.5
  172.9 0.1 copy.24
  173.0 9.7 %collective-permute-done.5 = f32[130,256]{0,1:T(8,128)S(1)} collective-permute-done((f32[130,256]{0,1:T(8,128)S(1)}, f32[130,256]{0,1:T(8,128)S(1)}, u32[]{:S(2)}, u32[]{:S(2)}) %collective-permute-start.5) | collective-permute-done | bytes 133152 | tf_op jit(solution)/shard_map/ppermute | solution.py:179
  182.7 0.1 copy.25
  182.9 0.6 slice.44.c_ref
  183.9 0.1 copy.29
  184.0 0.8 copy.33.system_ref
  184.8 114.0 %shard_map.51 = f32[1,256]{1,0:T(1,128)} custom-call(f32[256,256]{1,0:T(8,128)} %copy.33.system_ref, f32[1,256]{1,0:T(1,128)} %slice.44.c_ref), custom_call_target="tpu_custom_call" | custom-call | tf_op jit(solution)/shard_map/pallas_call | solution.py:152
  298.9 0.7 convert_element_type.8
  299.6 8.1 %fusion.3 = f32[1,32768]{1,0:T(1,128)S(1)} fusion(bf16[256,1]{0,1:T(2,128)(2,1)S(1)} %reshape.18, bf16[256,32768]{1,0:T(8,128)(2,1)} %get-tuple-element.7), kind=kOutput, calls=%fused_computation.19 | convolution fusion | flops 16777216 | bytes 16908800 | tf_op jit(solution)/shard_map/dot_general | solution.py:219
  307.7 0.7 convert_subtract_fusion
  (20 shorter events, 0.6 us)
Async XLA Ops:
  2.8 6.0 %collective-permute-start = (bf16[64,15361]{1,0:T(8,128)(2,1)S(1)}, bf16[64,15361]{1,0:T(8,128)(2,1)S(1)}, u32[]{:S(2)}, u32[]{:S(2)}) collective-permute-start(bf16[64,15361]{1,0:T(8,128)(2,1)S(1)} %slice.27), channel_id=1, source_target_pairs={{0,1},{1,2},{2,3},{3,4},{4,5},{5,6},{6,7},{7,8},{8,9},{9,10},{10,1... | collective-permute-start | bytes 5898632 | tf_op jit(solution)/shard_map/ppermute | solution.py:16
  6.2 8.6 %copy-start.1 = (f32[4,16,64]{2,1,0:T(8,128)S(1)}, f32[4,16,64]{2,1,0:T(8,128)}, u32[]{:S(2)}) copy-start(f32[4,16,64]{2,1,0:T(8,128)} %param.5) | copy-start | bytes 49156
  122.4 22.0 %collective-permute-start.1 = (f32[130,256]{0,1:T(8,128)S(1)}, f32[130,256]{0,1:T(8,128)S(1)}, u32[]{:S(2)}, u32[]{:S(2)}) collective-permute-start(f32[130,256]{0,1:T(8,128)S(1)} %pad_maximum_fusion.1), channel_id=1, source_target_pairs={{0,1},{1,0},{2,3},{3,2},{4,5},{5,4},{6,7},{7,6},{8,9},{9,8},{10,11... | collective-permute-start | bytes 399368 | tf_op jit(solution)/shard_map/ppermute | solution.py:179
  144.4 9.4 %collective-permute-start.2 = (f32[130,256]{0,1:T(8,128)S(1)}, f32[130,256]{0,1:T(8,128)S(1)}, u32[]{:S(2)}, u32[]{:S(2)}) collective-permute-start(f32[130,256]{0,1:T(8,128)S(1)} %fusion.6), channel_id=1, source_target_pairs={{0,2},{1,3},{2,0},{3,1},{4,6},{5,7},{6,4},{7,5},{8,10},{9,11},{10,... | collective-permute-start | bytes 399368 | tf_op jit(solution)/shard_map/ppermute | solution.py:179
  153.9 8.4 %collective-permute-start.3 = (f32[130,256]{0,1:T(8,128)S(1)}, f32[130,256]{0,1:T(8,128)S(1)}, u32[]{:S(2)}, u32[]{:S(2)}) collective-permute-start(f32[130,256]{0,1:T(8,128)S(1)} %add.34), channel_id=1, source_target_pairs={{0,4},{1,5},{2,6},{3,7},{4,0},{5,1},{6,2},{7,3},{8,12},{9,13},{10,... | collective-permute-start | bytes 399368 | tf_op jit(solution)/shard_map/ppermute | solution.py:179
  162.4 7.7 %collective-permute-start.4 = (f32[130,256]{0,1:T(8,128)S(1)}, f32[130,256]{0,1:T(8,128)S(1)}, u32[]{:S(2)}, u32[]{:S(2)}) collective-permute-start(f32[130,256]{0,1:T(8,128)S(1)} %add.35), channel_id=1, source_target_pairs={{0,8},{1,9},{2,10},{3,11},{4,12},{5,13},{6,14},{7,15},{8,0},{9,1},... | collective-permute-start | bytes 399368 | tf_op jit(solution)/shard_map/ppermute | solution.py:179
  170.1 12.6 %collective-permute-start.5 = (f32[130,256]{0,1:T(8,128)S(1)}, f32[130,256]{0,1:T(8,128)S(1)}, u32[]{:S(2)}, u32[]{:S(2)}) collective-permute-start(f32[130,256]{0,1:T(8,128)S(1)} %add.36), channel_id=1, source_target_pairs={{0,16},{1,17},{2,18},{3,19},{4,20},{5,21},{6,22},{7,23},{8,24},{9,... | collective-permute-start | bytes 399368 | tf_op jit(solution)/shard_map/ppermute | solution.py:179
  299.6 8.1 %copy-start = (bf16[32768]{0:T(1024)(128)(2,1)S(1)}, bf16[32768]{0:T(1024)(128)(2,1)}, u32[]{:S(2)}) copy-start(bf16[32768]{0:T(1024)(128)(2,1)} %param.4) | copy-start | bytes 196612

commit v2 on v1

--- a/solution.py
+++ b/solution.py
@@ -38,7 +38,7 @@
 CHUNK = 256
 
 
-def feature_kernel(dilations, span, taps_per_filter, chunk, w_ref, taps_ref, tgt_ref, f_ref, g_ref, c_ref):
+def feature_kernel(dilations, span, taps_per_filter, chunk, w_ref, taps_ref, tgt_ref, f_ref, g_ref, c_ref, wf_ref):
     block = pl.program_id(0)
     block_len = f_ref.shape[1]
     channels = w_ref.shape[0]
@@ -47,6 +47,13 @@
     def _():
         g_ref[...] = jnp.zeros_like(g_ref)
         c_ref[...] = jnp.zeros_like(c_ref)
+
+        def widen(i, carry):
+            lanes = pl.ds(pl.multiple_of(i * 128, 128), 128)
+            wf_ref[:, lanes] = w_ref[:, lanes].astype(jnp.float32)
+            return carry
+
+        lax.fori_loop(0, w_ref.shape[1] // 128, widen, 0)
 
     for j, d in enumerate(dilations):
         def chunk_body(i, carry, j=j, d=d):
@@ -58,10 +65,10 @@
                 r = offset % 128
                 a = offset - r
                 if r == 0:
-                    x = w_ref[:, pl.ds(pl.multiple_of(start + a, 128), chunk)].astype(jnp.float32)
+                    x = wf_ref[:, pl.ds(pl.multiple_of(start + a, 128), chunk)]
                 else:
                     if a not in slabs:
-                        slabs[a] = w_ref[:, pl.ds(pl.multiple_of(start + a, 128), chunk + 128)].astype(jnp.float32)
+                        slabs[a] = wf_ref[:, pl.ds(pl.multiple_of(start + a, 128), chunk + 128)]
                     x = slabs[a][:, r:r + chunk]
                 w = jnp.tile(taps_ref[j * taps_per_filter + k], (1, chunk // 128))
                 acc = w * x if acc is None else acc + w * x
@@ -105,6 +112,7 @@
             jax.ShapeDtypeStruct((rows, rows), jnp.float32),
             jax.ShapeDtypeStruct((1, rows), jnp.float32),
         ],
+        scratch_shapes=[pltpu.VMEM(window.shape, jnp.float32)],
         compiler_params=pltpu.CompilerParams(
             dimension_semantics=("arbitrary",), vmem_limit_bytes=48 * 1024 * 1024
         ),
@@ -214,7 +222,7 @@
     gram_sum, cross_sum = reduce_system(gram_sum, cross_sum, ("wide", "narrow"))
     total_rows = length * lax.axis_size("wide") * lax.axis_size("narrow")
     system = gram_sum + ridge_share * total_rows * jnp.eye(gram_sum.shape[0], dtype=jnp.float32)
-    coefficients = ridge_solve_kernel(system, cross_sum)
+    coefficients = ridge_solve(system, cross_sum)
     rounded = coefficients.astype(jnp.bfloat16)
     fitted = jnp.dot(rounded, features, preferred_element_type=jnp.float32)
     return (coefficients, target.astype(jnp.float32) - fitted)

time: 309 us -> 286 us (0.926)
  Pallas kernels: 219 us -> 149 us
  other arithmetic: 7.9 us -> 61.1 us
  waiting for transfers between devices: 30.7 us -> 18.2 us
    pallas_call x1 -> x0, Pallas kernels: 114 us -> none  [ridge_solve_kernel(): pl.pallas_call(solve_kernel, in_specs=[pl.BlockSpec(memory_space=pltpu.VM...]
    another operation x0 -> x10, other arithmetic: none -> 54.1 us  [the longest x6 34.2 us: ridge_solve(): factor = jnp.linalg.cholesky(system)]
    pallas_call x1, Pallas kernels: 105 us -> 149 us  [features_and_sums(): pl.pallas_call(kernel, grid=(length // block_len,), in_specs=[pl.BlockSpe...]
    ppermute x5, waiting for transfers between devices: 28.1 us -> 15.7 us  [butterfly_sum(): x = x + lax.ppermute(x, axes, [(i, i ^ step) for i in range(size)])]
    another operation x1 -> x18, local copies, waits for them, and re-layouts: 0.13 us -> 4.72 us  [reduce_system(): jnp.stack([cross_sum, jnp.concatenate([jnp.diagonal(trail), jnp.zeros((n...]
where the time goes in v2:
time: 286 us
  Pallas kernels  149 us (52%)
  other arithmetic  61.1 us (21%)
  starting transfers between devices  35.3 us (12%)
  waiting for transfers between devices  18.2 us (6%)
  local copies, waits for them, and re-layouts  10.3 us (4%)
  matrix products  9.69 us (3%)
    pallas_call x1, Pallas kernels, features_and_sums(): pl.pallas_call(kernel, grid=(length // block_len,), in_specs=[pl.BlockSpe...  149 us
    another operation x6, other arithmetic, ridge_solve(): factor = jnp.linalg.cholesky(system)  34.2 us
    ppermute x5, starting transfers between devices, butterfly_sum(): x = x + lax.ppermute(x, axes, [(i, i ^ step) for i in range(size)])  32.8 us
    another operation x4, other arithmetic, ridge_solve(): lax.linalg.triangular_solve(factor, middle, left_side=True, lower=True, t...  19.9 us
    ppermute x5, waiting for transfers between devices, butterfly_sum(): x = x + lax.ppermute(x, axes, [(i, i ^ step) for i in range(size)])  15.7 us
    dot_general x1, matrix products, local(): fitted = jnp.dot(rounded, features, preferred_element_type=jnp.float32)  8.07 us
    concatenate x1, other arithmetic, local(): jnp.concatenate([previous, stream], 1)[:, :history_len - 1 + length]  6.06 us
  transfers between devices with their start and end apart: 6, of which 6 were waited for; matrix products, arithmetic and copies ran while one was open for 0% of the time, Pallas kernels for 0%

profile of v2, /device:TPU:0, one launch (start us, length us, event | category | flops | bytes accessed | tf_op | source)
XLA Modules:
  0.0 285.7 jit_solution(15970625451885213379)
XLA Ops:
  0.6 2.1 slice.81
  2.8 2.5 collective-permute-start
  5.3 0.9 reshape.57.tgt_ref
  6.2 2.5 collective-permute-done
  8.8 6.1 %pad_maximum_fusion.w_ref = bf16[64,48128]{1,0:T(8,128)(2,1)} fusion(bf16[64,32768]{1,0:T(8,128)(2,1)} %param.3, bf16[64,15361]{1,0:T(8,128)(2,1)S(1)} %collective-permute-done), kind=kLoop, calls=%fused_computation.3 | loop fusion | flops 12320768 | bytes 12320896 | tf_op jit(solution)/shard_map/concatenate | solution.py:219
  14.8 0.6 broadcast_in_dim.39.taps_ref
  15.4 148.7 %shard_map.50 = (bf16[256,32768]{1,0:T(8,128)(2,1)}, f32[256,256]{1,0:T(8,128)S(1)}, f32[1,256]{1,0:T(1,128)S(1)}) custom-call(bf16[64,48128]{1,0:T(8,128)(2,1)} %pad_maximum_fusion.w_ref, f32[64,64,128]{2,1,0:T(8,128)S(1)} %broadcast_in_dim.39.taps_ref, bf16[1,32768]{1,0:T(2,128)(2,1)S(1)} %reshape.57.tgt_ref), custom_call_target="tpu_custom_call" | custom-call | tf_op jit(solution)/shard_map/pallas_call | solution.py:97
  164.2 1.4 gather_fusion
  165.7 20.8 %collective-permute-start.1 = (f32[130,256]{1,0:T(8,128)S(1)}, f32[130,256]{1,0:T(8,128)S(1)}, u32[]{:S(2)}, u32[]{:S(2)}) collective-permute-start(f32[130,256]{1,0:T(8,128)S(1)} %pad_maximum_fusion.1), channel_id=1, source_target_pairs={{0,1},{1,0},{2,3},{3,2},{4,5},{5,4},{6,7},{7,6},{8,9},{9,8},{10,11... | collective-permute-start | bytes 399368 | tf_op jit(solution)/shard_map/ppermute | solution.py:187
  186.5 1.0 collective-permute-done.1
  187.5 2.8 collective-permute-start.2
  190.3 4.0 %collective-permute-done.2 = f32[130,256]{1,0:T(8,128)S(1)} collective-permute-done((f32[130,256]{1,0:T(8,128)S(1)}, f32[130,256]{1,0:T(8,128)S(1)}, u32[]{:S(2)}, u32[]{:S(2)}) %collective-permute-start.2) | collective-permute-done | bytes 133152 | tf_op jit(solution)/shard_map/ppermute | solution.py:187
  194.3 2.7 collective-permute-start.3
  197.0 3.1 %collective-permute-done.3 = f32[130,256]{1,0:T(8,128)S(1)} collective-permute-done((f32[130,256]{1,0:T(8,128)S(1)}, f32[130,256]{1,0:T(8,128)S(1)}, u32[]{:S(2)}, u32[]{:S(2)}) %collective-permute-start.3) | collective-permute-done | bytes 133152 | tf_op jit(solution)/shard_map/ppermute | solution.py:187
  200.1 3.0 %collective-permute-start.4 = (f32[130,256]{1,0:T(8,128)S(1)}, f32[130,256]{1,0:T(8,128)S(1)}, u32[]{:S(2)}, u32[]{:S(2)}) collective-permute-start(f32[130,256]{1,0:T(8,128)S(1)} %add.59), channel_id=1, source_target_pairs={{0,8},{1,9},{2,10},{3,11},{4,12},{5,13},{6,14},{7,15},{8,0},{9,1},... | collective-permute-start | bytes 399368 | tf_op jit(solution)/shard_map/ppermute | solution.py:187
  203.1 3.0 %collective-permute-done.4 = f32[130,256]{1,0:T(8,128)S(1)} collective-permute-done((f32[130,256]{1,0:T(8,128)S(1)}, f32[130,256]{1,0:T(8,128)S(1)}, u32[]{:S(2)}, u32[]{:S(2)}) %collective-permute-start.4) | collective-permute-done | bytes 133152 | tf_op jit(solution)/shard_map/ppermute | solution.py:187
  206.2 3.5 %collective-permute-start.5 = (f32[130,256]{1,0:T(8,128)S(1)}, f32[130,256]{1,0:T(8,128)S(1)}, u32[]{:S(2)}, u32[]{:S(2)}) collective-permute-start(f32[130,256]{1,0:T(8,128)S(1)} %add.60), channel_id=1, source_target_pairs={{0,16},{1,17},{2,18},{3,19},{4,20},{5,21},{6,22},{7,23},{8,24},{9,... | collective-permute-start | bytes 399368 | tf_op jit(solution)/shard_map/ppermute | solution.py:187
  209.7 4.5 %collective-permute-done.5 = f32[130,256]{1,0:T(8,128)S(1)} collective-permute-done((f32[130,256]{1,0:T(8,128)S(1)}, f32[130,256]{1,0:T(8,128)S(1)}, u32[]{:S(2)}, u32[]{:S(2)}) %collective-permute-start.5) | collective-permute-done | bytes 133152 | tf_op jit(solution)/shard_map/ppermute | solution.py:187
  214.9 11.7 %cholesky.58 = f32[128,128]{1,0:T(8,128)S(1)} custom-call(f32[128,128]{1,0:T(8,128)S(1)} %cholesky.129), custom_call_target="Cholesky" | custom-call | tf_op jit(solution)/shard_map/jit(cholesky)/cholesky | solution.py:171
  226.9 9.8 %custom-call.16 = f32[1,128,128]{1,2,0:T(8,128)S(1)} custom-call(f32[1,128,128]{2,1,0:T(8,128)S(1)} %copy.27), custom_call_target="InvertDiagBlocksLowerTriangular" | custom-call | tf_op jit(solution)/shard_map/jit(cholesky)/cholesky | solution.py:171
  237.1 0.3 convolution_subtract_fusion
  237.3 11.7 %cholesky.117 = f32[128,128]{1,0:T(8,128)S(1)} custom-call(f32[128,128]{1,0:T(8,128)S(1)} %convolution_subtract_fusion), custom_call_target="Cholesky" | custom-call | tf_op jit(solution)/shard_map/jit(cholesky)/cholesky | solution.py:171
  249.3 0.7 compare_reduce_fusion
  251.5 4.3 %while.1 = (s32[]{:T(128)}, f32[256,256]{0,1:T(8,128)S(1)}, s32[2,2]{1,0:T(2,128)S(1)}, f32[2,128,128]{2,1,0:T(8,128)S(1)}, s32[]{:T(128)}) while((s32[]{:T(128)}, f32[256,256]{0,1:T(8,128)S(1)}, s32[2,2]{1,0:T(2,128)S(1)}, f32[2,128,128]{2,1,0:T(8,128)S(1)}, s32[]{:T(128)}) %tuple.32), condition=%wide.while_cond, body=%wide.while_body.sunk | while | flops 2 | bytes 393321 | solution.py:173
  251.5 0.6 fusion.24
  252.1 1.4 dynamic-slice.7
  253.6 0.6 fusion.24
  254.2 1.4 dynamic-slice.7
  255.8 19.9 %custom-call.17 = f32[2,128,128]{1,2,0:T(8,128)S(1)} custom-call(f32[2,128,128]{2,1,0:T(8,128)S(1)} %get-tuple-element.15), custom_call_target="InvertDiagBlocksLowerTriangular" | custom-call | tf_op jit(solution)/shard_map/triangular_solve | solution.py:173
  276.4 0.2 convolution_bitcast_fusion.1
  276.9 8.1 %fusion.16 = f32[1,32768]{1,0:T(1,128)S(1)} fusion(bf16[256,1]{0,1:T(2,128)(2,1)S(1)} %reshape.96, bf16[256,32768]{1,0:T(8,128)(2,1)} %get-tuple-element.7), kind=kOutput, calls=%fused_computation.58 | convolution fusion | flops 16777216 | bytes 16908800 | tf_op jit(solution)/shard_map/dot_general | solution.py:227
  285.0 0.7 convert_subtract_fusion
  (55 shorter events, 2.8 us)
Async XLA Ops:
  2.8 6.0 %collective-permute-start = (bf16[64,15361]{1,0:T(8,128)(2,1)S(1)}, bf16[64,15361]{1,0:T(8,128)(2,1)S(1)}, u32[]{:S(2)}, u32[]{:S(2)}) collective-permute-start(bf16[64,15361]{1,0:T(8,128)(2,1)S(1)} %slice.81), channel_id=1, source_target_pairs={{0,1},{1,2},{2,3},{3,4},{4,5},{5,6},{6,7},{7,8},{8,9},{9,10},{10,1... | collective-permute-start | bytes 5898632 | tf_op jit(solution)/shard_map/ppermute | solution.py:16
  6.2 8.6 %copy-start.1 = (f32[4,16,64]{2,1,0:T(8,128)S(1)}, f32[4,16,64]{2,1,0:T(8,128)}, u32[]{:S(2)}) copy-start(f32[4,16,64]{2,1,0:T(8,128)} %param.5) | copy-start | bytes 49156
  165.7 21.8 %collective-permute-start.1 = (f32[130,256]{1,0:T(8,128)S(1)}, f32[130,256]{1,0:T(8,128)S(1)}, u32[]{:S(2)}, u32[]{:S(2)}) collective-permute-start(f32[130,256]{1,0:T(8,128)S(1)} %pad_maximum_fusion.1), channel_id=1, source_target_pairs={{0,1},{1,0},{2,3},{3,2},{4,5},{5,4},{6,7},{7,6},{8,9},{9,8},{10,11... | collective-permute-start | bytes 399368 | tf_op jit(solution)/shard_map/ppermute | solution.py:187
  187.5 6.8 %collective-permute-start.2 = (f32[130,256]{1,0:T(8,128)S(1)}, f32[130,256]{1,0:T(8,128)S(1)}, u32[]{:S(2)}, u32[]{:S(2)}) collective-permute-start(f32[130,256]{1,0:T(8,128)S(1)} %fusion.14), channel_id=1, source_target_pairs={{0,2},{1,3},{2,0},{3,1},{4,6},{5,7},{6,4},{7,5},{8,10},{9,11},{10,... | collective-permute-start | bytes 399368 | tf_op jit(solution)/shard_map/ppermute | solution.py:187
  194.3 5.8 %collective-permute-start.3 = (f32[130,256]{1,0:T(8,128)S(1)}, f32[130,256]{1,0:T(8,128)S(1)}, u32[]{:S(2)}, u32[]{:S(2)}) collective-permute-start(f32[130,256]{1,0:T(8,128)S(1)} %add.58), channel_id=1, source_target_pairs={{0,4},{1,5},{2,6},{3,7},{4,0},{5,1},{6,2},{7,3},{8,12},{9,13},{10,... | collective-permute-start | bytes 399368 | tf_op jit(solution)/shard_map/ppermute | solution.py:187
  200.1 6.0 %collective-permute-start.4 = (f32[130,256]{1,0:T(8,128)S(1)}, f32[130,256]{1,0:T(8,128)S(1)}, u32[]{:S(2)}, u32[]{:S(2)}) collective-permute-start(f32[130,256]{1,0:T(8,128)S(1)} %add.59), channel_id=1, source_target_pairs={{0,8},{1,9},{2,10},{3,11},{4,12},{5,13},{6,14},{7,15},{8,0},{9,1},... | collective-permute-start | bytes 399368 | tf_op jit(solution)/shard_map/ppermute | solution.py:187
  206.2 8.1 %collective-permute-start.5 = (f32[130,256]{1,0:T(8,128)S(1)}, f32[130,256]{1,0:T(8,128)S(1)}, u32[]{:S(2)}, u32[]{:S(2)}) collective-permute-start(f32[130,256]{1,0:T(8,128)S(1)} %add.60), channel_id=1, source_target_pairs={{0,16},{1,17},{2,18},{3,19},{4,20},{5,21},{6,22},{7,23},{8,24},{9,... | collective-permute-start | bytes 399368 | tf_op jit(solution)/shard_map/ppermute | solution.py:187
  276.8 8.2 %copy-start.2 = (f32[256,1]{0,1:T(1,128)}, f32[256,1]{0,1:T(1,128)S(1)}, u32[]{:S(2)}) copy-start(f32[256,1]{0,1:T(1,128)S(1)} %pad_maximum_fusion.3) | copy-start | bytes 3076
  276.9 8.1 %copy-start = (bf16[32768]{0:T(1024)(128)(2,1)S(1)}, bf16[32768]{0:T(1024)(128)(2,1)}, u32[]{:S(2)}) copy-start(bf16[32768]{0:T(1024)(128)(2,1)} %param.4) | copy-start | bytes 196612

commit v3 on v1

--- a/solution.py
+++ b/solution.py
@@ -35,13 +35,16 @@
 
 
 TIME_BLOCK = 2048
-CHUNK = 256
-
-
-def feature_kernel(dilations, span, taps_per_filter, chunk, w_ref, taps_ref, tgt_ref, f_ref, g_ref, c_ref):
+ROW_GROUP = 16
+NARROW_CHUNK = 1024
+WIDE_CHUNK = 1024
+
+
+def feature_kernel(dilations, span, taps_per_filter, w_ref, taps_ref, tgt_ref, f_ref, g_ref, c_ref):
     block = pl.program_id(0)
     block_len = f_ref.shape[1]
     channels = w_ref.shape[0]
+    group = ROW_GROUP
 
     @pl.when(block == 0)
     def _():
@@ -49,26 +52,31 @@
         c_ref[...] = jnp.zeros_like(c_ref)
 
     for j, d in enumerate(dilations):
-        def chunk_body(i, carry, j=j, d=d):
-            start = pl.multiple_of(block * block_len + i * chunk, 128)
-            slabs = {}
-            acc = None
-            for k in range(taps_per_filter):
-                offset = span - k * d
-                r = offset % 128
-                a = offset - r
-                if r == 0:
-                    x = w_ref[:, pl.ds(pl.multiple_of(start + a, 128), chunk)].astype(jnp.float32)
-                else:
-                    if a not in slabs:
-                        slabs[a] = w_ref[:, pl.ds(pl.multiple_of(start + a, 128), chunk + 128)].astype(jnp.float32)
-                    x = slabs[a][:, r:r + chunk]
-                w = jnp.tile(taps_ref[j * taps_per_filter + k], (1, chunk // 128))
-                acc = w * x if acc is None else acc + w * x
-            f_ref[j * channels:(j + 1) * channels, pl.ds(pl.multiple_of(i * chunk, 128), chunk)] = acc.astype(f_ref.dtype)
-            return carry
-
-        lax.fori_loop(0, block_len // chunk, chunk_body, 0)
+        chunk = min(block_len, NARROW_CHUNK if d % 64 else WIDE_CHUNK)
+        for g in range(channels // group):
+            rows = pl.ds(g * group, group)
+
+            def chunk_body(i, carry, j=j, d=d, rows=rows, g=g, chunk=chunk):
+                start = pl.multiple_of(block * block_len + i * chunk, 128)
+                slabs = {}
+                acc = None
+                for k in range(taps_per_filter):
+                    offset = span - k * d
+                    r = offset % 128
+                    a = offset - r
+                    if r == 0:
+                        x = w_ref[rows, pl.ds(pl.multiple_of(start + a, 128), chunk)].astype(jnp.float32)
+                    else:
+                        if a not in slabs:
+                            slabs[a] = w_ref[rows, pl.ds(pl.multiple_of(start + a, 128), chunk + 128)].astype(jnp.float32)
+                        x = slabs[a][:, r:r + chunk]
+                    w = jnp.tile(taps_ref[j * taps_per_filter + k, rows, :], (1, chunk // 128))
+                    acc = w * x if acc is None else acc + w * x
+                out_rows = pl.ds(j * channels + g * group, group)
+                f_ref[out_rows, pl.ds(pl.multiple_of(i * chunk, 128), chunk)] = acc.astype(f_ref.dtype)
+                return carry
+
+            lax.fori_loop(0, block_len // chunk, chunk_body, 0)
 
     feats = f_ref[...]
     g_ref[...] += lax.dot_general(feats, feats, (((1,), (1,)), ((), ())), preferred_element_type=jnp.float32)
@@ -86,7 +94,7 @@
         depthwise_taps.reshape(n_filters * taps_per_filter, channels, 1),
         (n_filters * taps_per_filter, channels, 128),
     )
-    kernel = functools.partial(feature_kernel, dilations, span, taps_per_filter, min(CHUNK, block_len))
+    kernel = functools.partial(feature_kernel, dilations, span, taps_per_filter)
     return pl.pallas_call(
         kernel,
         grid=(length // block_len,),
@@ -116,6 +124,7 @@
     n = a_ref.shape[0]
     a_ref[...] = system_ref[...]
     lanes = lax.broadcasted_iota(jnp.int32, (1, n), 1)
+    sublanes = lax.broadcasted_iota(jnp.int32, (n, 1), 0)
 
     def pick(vec, at):
         return jnp.sum(jnp.where(at, vec, 0.0), axis=1, keepdims=True)
@@ -131,7 +140,8 @@
         rhs = rhs - yj * col_j
         forward = jnp.where(at, yj, forward)
         diag = jnp.where(at, root, diag)
-        column = jnp.transpose(jnp.broadcast_to(col_j, (8, n)))[:, 0:1]
+        column = jnp.sum(jnp.where(lanes == j, a_ref[...], 0.0), axis=1, keepdims=True) / root
+        column = jnp.where(sublanes >= j, column, 0.0)
         a_ref[...] = a_ref[...] - column * col_j
         return rhs, forward, diag
 

time: 309 us -> 242 us (0.78)
  Pallas kernels: 219 us -> 153 us
    pallas_call x1, Pallas kernels: 114 us -> 58.8 us  [ridge_solve_kernel(): pl.pallas_call(solve_kernel, in_specs=[pl.BlockSpec(memory_space=pltpu.VM...]
    pallas_call x1, Pallas kernels: 105 us -> 94.1 us  [features_and_sums(): pl.pallas_call(kernel, grid=(length // block_len,), in_specs=[pl.BlockSpe...]
where the time goes in v3:
time: 242 us
  Pallas kernels  153 us (63%)
  starting transfers between devices  34.4 us (14%)
  waiting for transfers between devices  30.7 us (13%)
  matrix products  8.07 us (3%)
  other arithmetic  7.9 us (3%)
  local copies, waits for them, and re-layouts  7.32 us (3%)
    pallas_call x1, Pallas kernels, features_and_sums(): pl.pallas_call(kernel, grid=(length // block_len,), in_specs=[pl.BlockSpe...  94.1 us
    pallas_call x1, Pallas kernels, ridge_solve_kernel(): pl.pallas_call(solve_kernel, in_specs=[pl.BlockSpec(memory_space=pltpu.VM...  58.8 us
    ppermute x5, starting transfers between devices, butterfly_sum(): x = x + lax.ppermute(x, axes, [(i, i ^ step) for i in range(size)])  31.9 us
    ppermute x5, waiting for transfers between devices, butterfly_sum(): x = x + lax.ppermute(x, axes, [(i, i ^ step) for i in range(size)])  28.1 us
    dot_general x1, matrix products, local(): fitted = jnp.dot(rounded, features, preferred_element_type=jnp.float32)  8.07 us
    concatenate x1, other arithmetic, local(): jnp.concatenate([previous, stream], 1)[:, :history_len - 1 + length]  6.05 us
  transfers between devices with their start and end apart: 6, of which 6 were waited for; matrix products, arithmetic and copies ran while one was open for 0% of the time, Pallas kernels for 0%

profile of v3, /device:TPU:0, one launch (start us, length us, event | category | flops | bytes accessed | tf_op | source)
XLA Modules:
  0.0 242.1 jit_solution(13472045954644474635)
XLA Ops:
  0.6 2.1 slice.27
  2.8 2.5 %collective-permute-start = (bf16[64,15361]{1,0:T(8,128)(2,1)S(1)}, bf16[64,15361]{1,0:T(8,128)(2,1)S(1)}, u32[]{:S(2)}, u32[]{:S(2)}) collective-permute-start(bf16[64,15361]{1,0:T(8,128)(2,1)S(1)} %slice.27), channel_id=1, source_target_pairs={{0,1},{1,2},{2,3},{3,4},{4,5},{5,6},{6,7},{7,8},{8,9},{9,10},{10,1... | collective-permute-start | bytes 5898632 | tf_op jit(solution)/shard_map/ppermute | solution.py:16
  5.3 0.9 reshape.11.tgt_ref
  6.2 2.5 %collective-permute-done = bf16[64,15361]{1,0:T(8,128)(2,1)S(1)} collective-permute-done((bf16[64,15361]{1,0:T(8,128)(2,1)S(1)}, bf16[64,15361]{1,0:T(8,128)(2,1)S(1)}, u32[]{:S(2)}, u32[]{:S(2)}) %collective-permute-start) | collective-permute-done | bytes 1966240 | tf_op jit(solution)/shard_map/ppermute | solution.py:16
  8.8 6.0 %pad_maximum_fusion.w_ref = bf16[64,48128]{1,0:T(8,128)(2,1)} fusion(bf16[64,32768]{1,0:T(8,128)(2,1)} %param.3, bf16[64,15361]{1,0:T(8,128)(2,1)S(1)} %collective-permute-done), kind=kLoop, calls=%fused_computation.1 | loop fusion | flops 12320768 | bytes 12320896 | tf_op jit(solution)/shard_map/concatenate | solution.py:221
  14.8 0.6 broadcast_in_dim.37.taps_ref
  15.4 94.1 %shard_map.50 = (bf16[256,32768]{1,0:T(8,128)(2,1)}, f32[256,256]{1,0:T(8,128)S(1)}, f32[1,256]{1,0:T(1,128)S(1)}) custom-call(bf16[64,48128]{1,0:T(8,128)(2,1)} %pad_maximum_fusion.w_ref, f32[64,64,128]{2,1,0:T(8,128)S(1)} %broadcast_in_dim.37.taps_ref, bf16[1,32768]{1,0:T(2,128)(2,1)S(1)} %reshape.11.tgt_ref), custom_call_target="tpu_custom_call" | custom-call | tf_op jit(solution)/shard_map/pallas_call | solution.py:98
  109.5 0.1 copy.19
  109.6 1.3 gather_fusion
  110.9 0.1 copy.23
  111.1 0.1 copy.22
  111.2 0.1 pad_maximum_fusion.1
  111.3 20.8 %collective-permute-start.1 = (f32[130,256]{0,1:T(8,128)S(1)}, f32[130,256]{0,1:T(8,128)S(1)}, u32[]{:S(2)}, u32[]{:S(2)}) collective-permute-start(f32[130,256]{0,1:T(8,128)S(1)} %pad_maximum_fusion.1), channel_id=1, source_target_pairs={{0,1},{1,0},{2,3},{3,2},{4,5},{5,4},{6,7},{7,6},{8,9},{9,8},{10,11... | collective-permute-start | bytes 399368 | tf_op jit(solution)/shard_map/ppermute | solution.py:189
  132.2 1.2 collective-permute-done.1
  133.3 0.1 fusion.6
  133.4 2.8 %collective-permute-start.2 = (f32[130,256]{0,1:T(8,128)S(1)}, f32[130,256]{0,1:T(8,128)S(1)}, u32[]{:S(2)}, u32[]{:S(2)}) collective-permute-start(f32[130,256]{0,1:T(8,128)S(1)} %fusion.6), channel_id=1, source_target_pairs={{0,2},{1,3},{2,0},{3,1},{4,6},{5,7},{6,4},{7,5},{8,10},{9,11},{10,... | collective-permute-start | bytes 399368 | tf_op jit(solution)/shard_map/ppermute | solution.py:189
  136.2 6.6 %collective-permute-done.2 = f32[130,256]{0,1:T(8,128)S(1)} collective-permute-done((f32[130,256]{0,1:T(8,128)S(1)}, f32[130,256]{0,1:T(8,128)S(1)}, u32[]{:S(2)}, u32[]{:S(2)}) %collective-permute-start.2) | collective-permute-done | bytes 133152 | tf_op jit(solution)/shard_map/ppermute | solution.py:189
  142.9 2.7 %collective-permute-start.3 = (f32[130,256]{0,1:T(8,128)S(1)}, f32[130,256]{0,1:T(8,128)S(1)}, u32[]{:S(2)}, u32[]{:S(2)}) collective-permute-start(f32[130,256]{0,1:T(8,128)S(1)} %add.34), channel_id=1, source_target_pairs={{0,4},{1,5},{2,6},{3,7},{4,0},{5,1},{6,2},{7,3},{8,12},{9,13},{10,... | collective-permute-start | bytes 399368 | tf_op jit(solution)/shard_map/ppermute | solution.py:189
  145.5 5.8 %collective-permute-done.3 = f32[130,256]{0,1:T(8,128)S(1)} collective-permute-done((f32[130,256]{0,1:T(8,128)S(1)}, f32[130,256]{0,1:T(8,128)S(1)}, u32[]{:S(2)}, u32[]{:S(2)}) %collective-permute-start.3) | collective-permute-done | bytes 133152 | tf_op jit(solution)/shard_map/ppermute | solution.py:189
  151.3 2.8 %collective-permute-start.4 = (f32[130,256]{0,1:T(8,128)S(1)}, f32[130,256]{0,1:T(8,128)S(1)}, u32[]{:S(2)}, u32[]{:S(2)}) collective-permute-start(f32[130,256]{0,1:T(8,128)S(1)} %add.35), channel_id=1, source_target_pairs={{0,8},{1,9},{2,10},{3,11},{4,12},{5,13},{6,14},{7,15},{8,0},{9,1},... | collective-permute-start | bytes 399368 | tf_op jit(solution)/shard_map/ppermute | solution.py:189
  154.1 4.9 %collective-permute-done.4 = f32[130,256]{0,1:T(8,128)S(1)} collective-permute-done((f32[130,256]{0,1:T(8,128)S(1)}, f32[130,256]{0,1:T(8,128)S(1)}, u32[]{:S(2)}, u32[]{:S(2)}) %collective-permute-start.4) | collective-permute-done | bytes 133152 | tf_op jit(solution)/shard_map/ppermute | solution.py:189
  159.1 2.8 %collective-permute-start.5 = (f32[130,256]{0,1:T(8,128)S(1)}, f32[130,256]{0,1:T(8,128)S(1)}, u32[]{:S(2)}, u32[]{:S(2)}) collective-permute-start(f32[130,256]{0,1:T(8,128)S(1)} %add.36), channel_id=1, source_target_pairs={{0,16},{1,17},{2,18},{3,19},{4,20},{5,21},{6,22},{7,23},{8,24},{9,... | collective-permute-start | bytes 399368 | tf_op jit(solution)/shard_map/ppermute | solution.py:189
  161.9 0.1 copy.24
  162.0 9.7 %collective-permute-done.5 = f32[130,256]{0,1:T(8,128)S(1)} collective-permute-done((f32[130,256]{0,1:T(8,128)S(1)}, f32[130,256]{0,1:T(8,128)S(1)}, u32[]{:S(2)}, u32[]{:S(2)}) %collective-permute-start.5) | collective-permute-done | bytes 133152 | tf_op jit(solution)/shard_map/ppermute | solution.py:189
  171.7 0.1 copy.25
  171.9 0.6 slice.44.c_ref
  172.8 0.1 copy.29
  173.0 0.8 copy.33.system_ref
  173.8 58.8 %shard_map.51 = f32[1,256]{1,0:T(1,128)} custom-call(f32[256,256]{1,0:T(8,128)} %copy.33.system_ref, f32[1,256]{1,0:T(1,128)} %slice.44.c_ref), custom_call_target="tpu_custom_call" | custom-call | tf_op jit(solution)/shard_map/pallas_call | solution.py:162
  232.7 0.7 convert_element_type.8
  233.3 8.1 %fusion.3 = f32[1,32768]{1,0:T(1,128)S(1)} fusion(bf16[256,1]{0,1:T(2,128)(2,1)S(1)} %reshape.18, bf16[256,32768]{1,0:T(8,128)(2,1)} %get-tuple-element.7), kind=kOutput, calls=%fused_computation.19 | convolution fusion | flops 16777216 | bytes 16908800 | tf_op jit(solution)/shard_map/dot_general | solution.py:229
  241.4 0.7 convert_subtract_fusion
  (20 shorter events, 0.6 us)
Async XLA Ops:
  2.8 6.0 %collective-permute-start = (bf16[64,15361]{1,0:T(8,128)(2,1)S(1)}, bf16[64,15361]{1,0:T(8,128)(2,1)S(1)}, u32[]{:S(2)}, u32[]{:S(2)}) collective-permute-start(bf16[64,15361]{1,0:T(8,128)(2,1)S(1)} %slice.27), channel_id=1, source_target_pairs={{0,1},{1,2},{2,3},{3,4},{4,5},{5,6},{6,7},{7,8},{8,9},{9,10},{10,1... | collective-permute-start | bytes 5898632 | tf_op jit(solution)/shard_map/ppermute | solution.py:16
  6.2 8.6 %copy-start.1 = (f32[4,16,64]{2,1,0:T(8,128)S(1)}, f32[4,16,64]{2,1,0:T(8,128)}, u32[]{:S(2)}) copy-start(f32[4,16,64]{2,1,0:T(8,128)} %param.5) | copy-start | bytes 49156
  111.3 22.0 %collective-permute-start.1 = (f32[130,256]{0,1:T(8,128)S(1)}, f32[130,256]{0,1:T(8,128)S(1)}, u32[]{:S(2)}, u32[]{:S(2)}) collective-permute-start(f32[130,256]{0,1:T(8,128)S(1)} %pad_maximum_fusion.1), channel_id=1, source_target_pairs={{0,1},{1,0},{2,3},{3,2},{4,5},{5,4},{6,7},{7,6},{8,9},{9,8},{10,11... | collective-permute-start | bytes 399368 | tf_op jit(solution)/shard_map/ppermute | solution.py:189
  133.4 9.4 %collective-permute-start.2 = (f32[130,256]{0,1:T(8,128)S(1)}, f32[130,256]{0,1:T(8,128)S(1)}, u32[]{:S(2)}, u32[]{:S(2)}) collective-permute-start(f32[130,256]{0,1:T(8,128)S(1)} %fusion.6), channel_id=1, source_target_pairs={{0,2},{1,3},{2,0},{3,1},{4,6},{5,7},{6,4},{7,5},{8,10},{9,11},{10,... | collective-permute-start | bytes 399368 | tf_op jit(solution)/shard_map/ppermute | solution.py:189
  142.9 8.4 %collective-permute-start.3 = (f32[130,256]{0,1:T(8,128)S(1)}, f32[130,256]{0,1:T(8,128)S(1)}, u32[]{:S(2)}, u32[]{:S(2)}) collective-permute-start(f32[130,256]{0,1:T(8,128)S(1)} %add.34), channel_id=1, source_target_pairs={{0,4},{1,5},{2,6},{3,7},{4,0},{5,1},{6,2},{7,3},{8,12},{9,13},{10,... | collective-permute-start | bytes 399368 | tf_op jit(solution)/shard_map/ppermute | solution.py:189
  151.3 7.7 %collective-permute-start.4 = (f32[130,256]{0,1:T(8,128)S(1)}, f32[130,256]{0,1:T(8,128)S(1)}, u32[]{:S(2)}, u32[]{:S(2)}) collective-permute-start(f32[130,256]{0,1:T(8,128)S(1)} %add.35), channel_id=1, source_target_pairs={{0,8},{1,9},{2,10},{3,11},{4,12},{5,13},{6,14},{7,15},{8,0},{9,1},... | collective-permute-start | bytes 399368 | tf_op jit(solution)/shard_map/ppermute | solution.py:189
  159.1 12.6 %collective-permute-start.5 = (f32[130,256]{0,1:T(8,128)S(1)}, f32[130,256]{0,1:T(8,128)S(1)}, u32[]{:S(2)}, u32[]{:S(2)}) collective-permute-start(f32[130,256]{0,1:T(8,128)S(1)} %add.36), channel_id=1, source_target_pairs={{0,16},{1,17},{2,18},{3,19},{4,20},{5,21},{6,22},{7,23},{8,24},{9,... | collective-permute-start | bytes 399368 | tf_op jit(solution)/shard_map/ppermute | solution.py:189
  233.3 8.1 %copy-start = (bf16[32768]{0:T(1024)(128)(2,1)S(1)}, bf16[32768]{0:T(1024)(128)(2,1)}, u32[]{:S(2)}) copy-start(bf16[32768]{0:T(1024)(128)(2,1)} %param.4) | copy-start | bytes 196612

commit v4 on v3

--- a/solution.py
+++ b/solution.py
@@ -40,7 +40,7 @@
 WIDE_CHUNK = 1024
 
 
-def feature_kernel(dilations, span, taps_per_filter, w_ref, taps_ref, tgt_ref, f_ref, g_ref, c_ref):
+def feature_kernel(dilations, span, base, first_block, taps_per_filter, w_ref, taps_ref, tgt_ref, f_ref, g_ref, c_ref):
     block = pl.program_id(0)
     block_len = f_ref.shape[1]
     channels = w_ref.shape[0]
@@ -57,11 +57,11 @@
             rows = pl.ds(g * group, group)
 
             def chunk_body(i, carry, j=j, d=d, rows=rows, g=g, chunk=chunk):
-                start = pl.multiple_of(block * block_len + i * chunk, 128)
+                start = pl.multiple_of((first_block + block) * block_len + i * chunk, 128)
                 slabs = {}
                 acc = None
                 for k in range(taps_per_filter):
-                    offset = span - k * d
+                    offset = span - k * d - base
                     r = offset % 128
                     a = offset - r
                     if r == 0:
@@ -83,7 +83,7 @@
     c_ref[...] += lax.dot_general(tgt_ref[...], feats, (((1,), (1,)), ((), ())), preferred_element_type=jnp.float32)
 
 
-def features_and_sums(window, depthwise_taps, target, top_dilation, length, interpret=False):
+def features_and_sums(window, base, first_block, n_blocks, depthwise_taps, target, top_dilation, length, interpret=False):
     channels = window.shape[0]
     dilations = dilation_list(top_dilation)
     n_filters, taps_per_filter = len(dilations), depthwise_taps.shape[1]
@@ -94,14 +94,14 @@
         depthwise_taps.reshape(n_filters * taps_per_filter, channels, 1),
         (n_filters * taps_per_filter, channels, 128),
     )
-    kernel = functools.partial(feature_kernel, dilations, span, taps_per_filter)
+    kernel = functools.partial(feature_kernel, dilations, span, base, first_block, taps_per_filter)
     return pl.pallas_call(
         kernel,
-        grid=(length // block_len,),
+        grid=(n_blocks,),
         in_specs=[
             pl.BlockSpec(memory_space=pltpu.VMEM),
             pl.BlockSpec(memory_space=pltpu.VMEM),
-            pl.BlockSpec((1, block_len), lambda b: (0, b)),
+            pl.BlockSpec((1, block_len), lambda b: (0, b + first_block)),
         ],
         out_specs=[
             pl.BlockSpec((rows, block_len), lambda b: (0, b)),
@@ -109,7 +109,7 @@
             pl.BlockSpec((1, rows), lambda b: (0, 0)),
         ],
         out_shape=[
-            jax.ShapeDtypeStruct((rows, length), jnp.bfloat16),
+            jax.ShapeDtypeStruct((rows, n_blocks * block_len), jnp.bfloat16),
             jax.ShapeDtypeStruct((rows, rows), jnp.float32),
             jax.ShapeDtypeStruct((1, rows), jnp.float32),
         ],
@@ -218,15 +218,30 @@
     history_len = 15 * top_dilation + 1
     tail_end = stream[:, length - history_len :]
     previous = shifted(tail_end, ("wide", "narrow"), 1)
-    window = jnp.concatenate([previous, stream], 1)[:, : history_len - 1 + length]
-    features, gram_sum, cross_sum = features_and_sums(window, depthwise_taps, target, top_dilation, length)
+    span = history_len - 1
+    block_len = min(TIME_BLOCK, length)
+    n_blocks = length // block_len
+    split = min(n_blocks, -(-span // block_len))
+    window = jnp.concatenate([previous, stream], 1)[:, : split * block_len + span]
+    features, gram_sum, cross_sum = features_and_sums(
+        window, 0, 0, split, depthwise_taps, target, top_dilation, length
+    )
+    if split < n_blocks:
+        delayed = jnp.concatenate([jnp.zeros_like(stream[:, :1]), stream[:, : length - 1]], 1)
+        late_features, late_gram, late_cross = features_and_sums(
+            delayed, span, split, n_blocks - split, depthwise_taps, target, top_dilation, length
+        )
+        features = (features, late_features)
+        gram_sum, cross_sum = gram_sum + late_gram, cross_sum + late_cross
+    else:
+        features = (features,)
     cross_sum = cross_sum[0]
     gram_sum, cross_sum = reduce_system(gram_sum, cross_sum, ("wide", "narrow"))
     total_rows = length * lax.axis_size("wide") * lax.axis_size("narrow")
     system = gram_sum + ridge_share * total_rows * jnp.eye(gram_sum.shape[0], dtype=jnp.float32)
     coefficients = ridge_solve_kernel(system, cross_sum)
     rounded = coefficients.astype(jnp.bfloat16)
-    fitted = jnp.dot(rounded, features, preferred_element_type=jnp.float32)
+    fitted = jnp.concatenate([jnp.dot(rounded, f, preferred_element_type=jnp.float32) for f in features])
     return (coefficients, target.astype(jnp.float32) - fitted)
 
 

time: 242 us -> 229 us (0.946)
  starting transfers between devices: 34.4 us -> 12.4 us
  local copies, waits for them, and re-layouts: 7.32 us -> 14.1 us
    ppermute x5, starting transfers between devices: 31.9 us -> 8.74 us  [butterfly_sum(): x = x + lax.ppermute(x, axes, [(i, i ^ step) for i in range(size)])]
    concatenate x0 -> x1, local copies, waits for them, and re-layouts: none -> 5.31 us  [local(): jnp.concatenate([jnp.zeros_like(stream[:, :1]), stream[:, :length - 1]], 1)]
    ppermute x1, waiting for transfers between devices: 2.54 us -> 0.01 us  [shifted(): return lax.ppermute(array, axis, pairs)]
    pallas_call x1 -> x2, Pallas kernels: 94.1 us -> 96.6 us  [features_and_sums(): pl.pallas_call(kernel, grid=(n_blocks,), in_specs=[pl.BlockSpec(memory_sp...]
    dot_general x1 -> x2, matrix products: 8.07 us -> 9.18 us  [local(): jnp.dot(rounded, f, preferred_element_type=jnp.float32)]
  transfers between devices with their start and end apart: 6 -> 6, of which waited for: 6 -> 5; matrix products, arithmetic and copies ran while one was open for 0% -> 3% of each run, Pallas kernels for 0% -> 21%
where the time goes in v4:
time: 229 us; the launch traced here: 228 us
  Pallas kernels  155 us (68%)
  waiting for transfers between devices  29.7 us (13%)
  local copies, waits for them, and re-layouts  14.1 us (6%)
  starting transfers between devices  12.4 us (5%)
  matrix products  9.18 us (4%)
  other arithmetic  6.7 us (3%)
    pallas_call x2, Pallas kernels, features_and_sums(): pl.pallas_call(kernel, grid=(n_blocks,), in_specs=[pl.BlockSpec(memory_sp...  96.6 us
    pallas_call x1, Pallas kernels, ridge_solve_kernel(): pl.pallas_call(solve_kernel, in_specs=[pl.BlockSpec(memory_space=pltpu.VM...  58.8 us
    ppermute x5, waiting for transfers between devices, butterfly_sum(): x = x + lax.ppermute(x, axes, [(i, i ^ step) for i in range(size)])  29.7 us
    dot_general x2, matrix products, local(): jnp.dot(rounded, f, preferred_element_type=jnp.float32)  9.18 us
    ppermute x5, starting transfers between devices, butterfly_sum(): x = x + lax.ppermute(x, axes, [(i, i ^ step) for i in range(size)])  8.74 us
    concatenate x1, local copies, waits for them, and re-layouts, local(): jnp.concatenate([jnp.zeros_like(stream[:, :1]), stream[:, :length - 1]], 1)  5.31 us
    concatenate x1, other arithmetic, local(): jnp.concatenate([previous, stream], 1)[:, :split * block_len + span]  4.8 us
  transfers between devices with their start and end apart: 6, of which 5 were waited for; matrix products, arithmetic and copies ran while one was open for 3% of the time, Pallas kernels for 21%

profile of v4, /device:TPU:0, one launch (start us, length us, event | category | flops | bytes accessed | tf_op | source)
XLA Modules:
  0.0 228.3 jit_solution(7738192314660361813)
XLA Ops:
  0.6 3.4 %slice.30 = bf16[64,15361]{1,0:T(8,128)(2,1)} slice(bf16[64,32768]{1,0:T(8,128)(2,1)} %param.3), slice={[0:64], [17407:32768]} | slice | bytes 3932416 | tf_op jit(solution)/shard_map/slice | solution.py:219
  4.1 3.7 %collective-permute-start = (bf16[64,15361]{1,0:T(8,128)(2,1)}, bf16[64,15361]{1,0:T(8,128)(2,1)}, u32[]{:S(2)}, u32[]{:S(2)}) collective-permute-start(bf16[64,15361]{1,0:T(8,128)(2,1)} %slice.30), channel_id=1, source_target_pairs={{0,1},{1,2},{2,3},{3,4},{4,5},{5,6},{6,7},{7,8},{8,9},{9,10},{10,1... | collective-permute-start | bytes 5898632 | tf_op jit(solution)/shard_map/ppermute | solution.py:16
  7.8 0.9 reshape.13.tgt_ref
  8.7 5.3 %concatenate.32.w_ref = bf16[64,32768]{1,0:T(8,128)(2,1)} pad(bf16[64,32767]{1,0:T(8,128)(2,1)} %bitcast.22, bf16[]{:T(256)} %constant.5.clone.1), padding=0_0x1_0 | pad | bytes 8388482 | tf_op jit(solution)/shard_map/concatenate | solution.py:230
  14.0 0.6 broadcast_in_dim.41.taps_ref
  14.6 48.4 %shard_map.51 = (bf16[256,16384]{1,0:T(8,128)(2,1)}, f32[256,256]{1,0:T(8,128)S(1)}, f32[1,256]{1,0:T(1,128)S(1)}) custom-call(bf16[64,32768]{1,0:T(8,128)(2,1)} %concatenate.32.w_ref, f32[64,64,128]{2,1,0:T(8,128)S(1)} %broadcast_in_dim.41.taps_ref, bf16[1,32768]{1,0:T(2,128)(2,1)S(1)} %reshape.13.tgt_ref), custom_call_target="tpu_custom_call" | custom-call | tf_op jit(solution)/shard_map/pallas_call | solution.py:98
  63.0 0.1 copy.35
  63.2 4.8 %pad_maximum_fusion.w_ref = bf16[64,31744]{1,0:T(8,128)(2,1)} fusion(bf16[64,32768]{1,0:T(8,128)(2,1)} %param.3, bf16[64,15361]{1,0:T(8,128)(2,1)} %collective-permute-done), kind=kLoop, calls=%fused_computation.1 | loop fusion | flops 8126464 | bytes 10223744 | tf_op jit(solution)/shard_map/concatenate | solution.py:225
  68.0 48.2 %shard_map.50 = (bf16[256,16384]{1,0:T(8,128)(2,1)}, f32[256,256]{1,0:T(8,128)S(1)}, f32[1,256]{1,0:T(1,128)S(1)}) custom-call(bf16[64,31744]{1,0:T(8,128)(2,1)} %pad_maximum_fusion.w_ref, f32[64,64,128]{2,1,0:T(8,128)S(1)} %broadcast_in_dim.41.taps_ref, bf16[1,32768]{1,0:T(2,128)(2,1)S(1)} %reshape.13.tgt_ref), custom_call_target="tpu_custom_call" | custom-call | tf_op jit(solution)/shard_map/pallas_call | solution.py:98
  116.1 0.1 copy.34
  116.3 1.3 gather_fusion
  117.6 0.1 copy.37
  117.8 0.1 copy.36
  117.9 0.1 pad_maximum_fusion.1
  118.0 1.4 collective-permute-start.1
  119.4 1.2 collective-permute-done.1
  120.6 0.1 fusion.9
  120.7 1.5 collective-permute-start.2
  122.2 7.2 %collective-permute-done.2 = f32[130,256]{0,1:T(8,128)S(1)} collective-permute-done((f32[130,256]{0,1:T(8,128)S(1)}, f32[130,256]{0,1:T(8,128)S(1)}, u32[]{:S(2)}, u32[]{:S(2)}) %collective-permute-start.2) | collective-permute-done | bytes 133152 | tf_op jit(solution)/shard_map/ppermute | solution.py:189
  129.4 1.6 collective-permute-start.3
  131.0 6.2 %collective-permute-done.3 = f32[130,256]{0,1:T(8,128)S(1)} collective-permute-done((f32[130,256]{0,1:T(8,128)S(1)}, f32[130,256]{0,1:T(8,128)S(1)}, u32[]{:S(2)}, u32[]{:S(2)}) %collective-permute-start.3) | collective-permute-done | bytes 133152 | tf_op jit(solution)/shard_map/ppermute | solution.py:189
  137.2 1.6 collective-permute-start.4
  138.9 5.3 %collective-permute-done.4 = f32[130,256]{0,1:T(8,128)S(1)} collective-permute-done((f32[130,256]{0,1:T(8,128)S(1)}, f32[130,256]{0,1:T(8,128)S(1)}, u32[]{:S(2)}, u32[]{:S(2)}) %collective-permute-start.4) | collective-permute-done | bytes 133152 | tf_op jit(solution)/shard_map/ppermute | solution.py:189
  144.2 2.7 %collective-permute-start.5 = (f32[130,256]{0,1:T(8,128)S(1)}, f32[130,256]{0,1:T(8,128)S(1)}, u32[]{:S(2)}, u32[]{:S(2)}) collective-permute-start(f32[130,256]{0,1:T(8,128)S(1)} %add.46), channel_id=1, source_target_pairs={{0,16},{1,17},{2,18},{3,19},{4,20},{5,21},{6,22},{7,23},{8,24},{9,... | collective-permute-start | bytes 399368 | tf_op jit(solution)/shard_map/ppermute | solution.py:189
  147.0 9.8 %collective-permute-done.5 = f32[130,256]{0,1:T(8,128)S(1)} collective-permute-done((f32[130,256]{0,1:T(8,128)S(1)}, f32[130,256]{0,1:T(8,128)S(1)}, u32[]{:S(2)}, u32[]{:S(2)}) %collective-permute-start.5) | collective-permute-done | bytes 133152 | tf_op jit(solution)/shard_map/ppermute | solution.py:189
  156.9 0.6 slice.48.c_ref
  158.1 0.8 copy.47.system_ref
  158.9 58.8 %shard_map.52 = f32[1,256]{1,0:T(1,128)} custom-call(f32[256,256]{1,0:T(8,128)} %copy.47.system_ref, f32[1,256]{1,0:T(1,128)} %slice.48.c_ref), custom_call_target="tpu_custom_call" | custom-call | tf_op jit(solution)/shard_map/pallas_call | solution.py:162
  217.8 0.7 convert_element_type.8
  218.4 4.6 %fusion.4 = f32[1,16384]{1,0:T(1,128)S(1)} fusion(bf16[256,1]{0,1:T(2,128)(2,1)S(1)} %reshape.20, bf16[256,16384]{1,0:T(8,128)(2,1)} %get-tuple-element.13), kind=kOutput, calls=%fused_computation.20 | convolution fusion | flops 8388608 | bytes 8454656 | tf_op jit(solution)/shard_map/dot_general | solution.py:244
  223.1 4.6 %fusion.3 = f32[1,16384]{1,0:T(1,128)S(1)} fusion(bf16[256,1]{0,1:T(2,128)(2,1)S(1)} %reshape.20, bf16[256,16384]{1,0:T(8,128)(2,1)} %get-tuple-element.12), kind=kOutput, calls=%fused_computation.19 | convolution fusion | flops 8388608 | bytes 8454656 | tf_op jit(solution)/shard_map/dot_general | solution.py:244
  227.6 0.7 maximum_subtract_fusion
  (26 shorter events, 0.9 us)
Async XLA Ops:
  0.6 13.4 %copy-start.1 = (f32[4,16,64]{2,1,0:T(8,128)S(1)}, f32[4,16,64]{2,1,0:T(8,128)}, u32[]{:S(2)}) copy-start(f32[4,16,64]{2,1,0:T(8,128)} %param.5) | copy-start | bytes 49156
  4.1 59.1 %collective-permute-start = (bf16[64,15361]{1,0:T(8,128)(2,1)}, bf16[64,15361]{1,0:T(8,128)(2,1)}, u32[]{:S(2)}, u32[]{:S(2)}) collective-permute-start(bf16[64,15361]{1,0:T(8,128)(2,1)} %slice.30), channel_id=1, source_target_pairs={{0,1},{1,2},{2,3},{3,4},{4,5},{5,6},{6,7},{7,8},{8,9},{9,10},{10,1... | collective-permute-start | bytes 5898632 | tf_op jit(solution)/shard_map/ppermute | solution.py:16
  118.0 2.6 %collective-permute-start.1 = (f32[130,256]{0,1:T(8,128)S(1)}, f32[130,256]{0,1:T(8,128)S(1)}, u32[]{:S(2)}, u32[]{:S(2)}) collective-permute-start(f32[130,256]{0,1:T(8,128)S(1)} %pad_maximum_fusion.1), channel_id=1, source_target_pairs={{0,1},{1,0},{2,3},{3,2},{4,5},{5,4},{6,7},{7,6},{8,9},{9,8},{10,11... | collective-permute-start | bytes 399368 | tf_op jit(solution)/shard_map/ppermute | solution.py:189
  120.7 8.7 %collective-permute-start.2 = (f32[130,256]{0,1:T(8,128)S(1)}, f32[130,256]{0,1:T(8,128)S(1)}, u32[]{:S(2)}, u32[]{:S(2)}) collective-permute-start(f32[130,256]{0,1:T(8,128)S(1)} %fusion.9), channel_id=1, source_target_pairs={{0,2},{1,3},{2,0},{3,1},{4,6},{5,7},{6,4},{7,5},{8,10},{9,11},{10,... | collective-permute-start | bytes 399368 | tf_op jit(solution)/shard_map/ppermute | solution.py:189
  129.4 7.8 %collective-permute-start.3 = (f32[130,256]{0,1:T(8,128)S(1)}, f32[130,256]{0,1:T(8,128)S(1)}, u32[]{:S(2)}, u32[]{:S(2)}) collective-permute-start(f32[130,256]{0,1:T(8,128)S(1)} %add.44), channel_id=1, source_target_pairs={{0,4},{1,5},{2,6},{3,7},{4,0},{5,1},{6,2},{7,3},{8,12},{9,13},{10,... | collective-permute-start | bytes 399368 | tf_op jit(solution)/shard_map/ppermute | solution.py:189
  137.2 6.9 %collective-permute-start.4 = (f32[130,256]{0,1:T(8,128)S(1)}, f32[130,256]{0,1:T(8,128)S(1)}, u32[]{:S(2)}, u32[]{:S(2)}) collective-permute-start(f32[130,256]{0,1:T(8,128)S(1)} %add.45), channel_id=1, source_target_pairs={{0,8},{1,9},{2,10},{3,11},{4,12},{5,13},{6,14},{7,15},{8,0},{9,1},... | collective-permute-start | bytes 399368 | tf_op jit(solution)/shard_map/ppermute | solution.py:189
  144.2 12.6 %collective-permute-start.5 = (f32[130,256]{0,1:T(8,128)S(1)}, f32[130,256]{0,1:T(8,128)S(1)}, u32[]{:S(2)}, u32[]{:S(2)}) collective-permute-start(f32[130,256]{0,1:T(8,128)S(1)} %add.46), channel_id=1, source_target_pairs={{0,16},{1,17},{2,18},{3,19},{4,20},{5,21},{6,22},{7,23},{8,24},{9,... | collective-permute-start | bytes 399368 | tf_op jit(solution)/shard_map/ppermute | solution.py:189
  218.4 9.2 %copy-start = (bf16[32768]{0:T(1024)(128)(2,1)S(1)}, bf16[32768]{0:T(1024)(128)(2,1)}, u32[]{:S(2)}) copy-start(bf16[32768]{0:T(1024)(128)(2,1)} %param.4) | copy-start | bytes 196612

commit v5 on v4

--- a/solution.py
+++ b/solution.py
@@ -169,6 +169,41 @@
     )(system, cross_sum.reshape(1, n))[0]
 
 
+def jordan_kernel(system_ref, c_ref, x_ref, a_ref):
+    n = a_ref.shape[0]
+    a_ref[...] = system_ref[...]
+    x_ref[...] = c_ref[...]
+    lanes = lax.broadcasted_iota(jnp.int32, (1, n), 1)
+    sublanes = lax.broadcasted_iota(jnp.int32, (n, 1), 0)
+
+    def step(j, carry):
+        at = lanes == j
+        here = sublanes == j
+        row = a_ref[pl.ds(j, 1), :]
+        pivot = jnp.sum(jnp.where(at, row, 0.0), axis=1, keepdims=True)
+        column = jnp.sum(jnp.where(at, a_ref[...], 0.0), axis=1, keepdims=True)
+        scaled_row = row / pivot
+        scaled_rhs = x_ref[pl.ds(j, 1), :] / pivot
+        a_ref[...] = jnp.where(here, scaled_row, a_ref[...] - column * scaled_row)
+        x_ref[...] = jnp.where(here, scaled_rhs, x_ref[...] - column * scaled_rhs)
+        return carry
+
+    lax.fori_loop(0, n, step, 0)
+
+
+def ridge_solve_jordan(system, cross_sum, interpret=False):
+    n = system.shape[0]
+    rhs = jnp.broadcast_to(cross_sum[:, None], (n, 128))
+    return pl.pallas_call(
+        jordan_kernel,
+        in_specs=[pl.BlockSpec(memory_space=pltpu.VMEM), pl.BlockSpec(memory_space=pltpu.VMEM)],
+        out_specs=pl.BlockSpec(memory_space=pltpu.VMEM),
+        out_shape=jax.ShapeDtypeStruct((n, 128), jnp.float32),
+        scratch_shapes=[pltpu.VMEM((n, n), jnp.float32)],
+        interpret=interpret,
+    )(system, rhs)[:, 0]
+
+
 def ridge_solve(system, cross_sum):
     factor = jnp.linalg.cholesky(system)
     middle = lax.linalg.triangular_solve(factor, cross_sum[:, None], left_side=True, lower=True)
@@ -239,7 +274,7 @@
     gram_sum, cross_sum = reduce_system(gram_sum, cross_sum, ("wide", "narrow"))
     total_rows = length * lax.axis_size("wide") * lax.axis_size("narrow")
     system = gram_sum + ridge_share * total_rows * jnp.eye(gram_sum.shape[0], dtype=jnp.float32)
-    coefficients = ridge_solve_kernel(system, cross_sum)
+    coefficients = ridge_solve_jordan(system, cross_sum)
     rounded = coefficients.astype(jnp.bfloat16)
     fitted = jnp.concatenate([jnp.dot(rounded, f, preferred_element_type=jnp.float32) for f in features])
     return (coefficients, target.astype(jnp.float32) - fitted)

time: 229 us -> 208 us (0.908)
  Pallas kernels: 155 us -> 134 us
    pallas_call x1, Pallas kernels: 58.8 us -> 37.7 us  [ridge_solve_jordan(): pl.pallas_call(jordan_kernel, in_specs=[pl.BlockSpec(memory_space=pltpu.V...]
  transfers between devices with their start and end apart: 6 -> 6, of which waited for: 5 -> 5; matrix products, arithmetic and copies ran while one was open for 3% -> 3% of each run, Pallas kernels for 21% -> 23%
where the time goes in v5:
time: 208 us
  Pallas kernels  134 us (64%)
  waiting for transfers between devices  29.8 us (14%)
  local copies, waits for them, and re-layouts  14.4 us (7%)
  starting transfers between devices  12.4 us (6%)
  matrix products  9.18 us (4%)
  other arithmetic  6.74 us (3%)
    pallas_call x2, Pallas kernels, features_and_sums(): pl.pallas_call(kernel, grid=(n_blocks,), in_specs=[pl.BlockSpec(memory_sp...  96.8 us
    pallas_call x1, Pallas kernels, ridge_solve_jordan(): pl.pallas_call(jordan_kernel, in_specs=[pl.BlockSpec(memory_space=pltpu.V...  37.7 us
    ppermute x5, waiting for transfers between devices, butterfly_sum(): x = x + lax.ppermute(x, axes, [(i, i ^ step) for i in range(size)])  29.8 us
    dot_general x2, matrix products, local(): jnp.dot(rounded, f, preferred_element_type=jnp.float32)  9.18 us
    ppermute x5, starting transfers between devices, butterfly_sum(): x = x + lax.ppermute(x, axes, [(i, i ^ step) for i in range(size)])  8.73 us
    concatenate x1, local copies, waits for them, and re-layouts, local(): jnp.concatenate([jnp.zeros_like(stream[:, :1]), stream[:, :length - 1]], 1)  5.29 us
    concatenate x1, other arithmetic, local(): jnp.concatenate([previous, stream], 1)[:, :split * block_len + span]  4.81 us
  transfers between devices with their start and end apart: 6, of which 5 were waited for; matrix products, arithmetic and copies ran while one was open for 3% of the time, Pallas kernels for 23%

profile of v5, /device:TPU:0, one launch (start us, length us, event | category | flops | bytes accessed | tf_op | source)
XLA Modules:
  0.0 207.8 jit_solution(2078963458141679631)
XLA Ops:
  0.6 3.4 %slice.33 = bf16[64,15361]{1,0:T(8,128)(2,1)} slice(bf16[64,32768]{1,0:T(8,128)(2,1)} %param.3), slice={[0:64], [17407:32768]} | slice | bytes 3932416 | tf_op jit(solution)/shard_map/slice | solution.py:254
  4.0 3.7 %collective-permute-start = (bf16[64,15361]{1,0:T(8,128)(2,1)}, bf16[64,15361]{1,0:T(8,128)(2,1)}, u32[]{:S(2)}, u32[]{:S(2)}) collective-permute-start(bf16[64,15361]{1,0:T(8,128)(2,1)} %slice.33), channel_id=1, source_target_pairs={{0,1},{1,2},{2,3},{3,4},{4,5},{5,6},{6,7},{7,8},{8,9},{9,10},{10,1... | collective-permute-start | bytes 5898632 | tf_op jit(solution)/shard_map/ppermute | solution.py:16
  7.7 0.9 reshape.14.tgt_ref
  8.7 5.3 %concatenate.32.w_ref = bf16[64,32768]{1,0:T(8,128)(2,1)} pad(bf16[64,32767]{1,0:T(8,128)(2,1)} %bitcast.19, bf16[]{:T(256)} %constant.5.clone.1), padding=0_0x1_0 | pad | bytes 8388482 | tf_op jit(solution)/shard_map/concatenate | solution.py:265
  14.0 0.6 broadcast_in_dim.48.taps_ref
  14.6 48.5 %shard_map.51 = (bf16[256,16384]{1,0:T(8,128)(2,1)}, f32[256,256]{1,0:T(8,128)S(1)}, f32[1,256]{1,0:T(1,128)S(1)}) custom-call(bf16[64,32768]{1,0:T(8,128)(2,1)} %concatenate.32.w_ref, f32[64,64,128]{2,1,0:T(8,128)S(1)} %broadcast_in_dim.48.taps_ref, bf16[1,32768]{1,0:T(2,128)(2,1)S(1)} %reshape.14.tgt_ref), custom_call_target="tpu_custom_call" | custom-call | tf_op jit(solution)/shard_map/pallas_call | solution.py:98
  63.1 0.1 copy.25
  63.2 4.8 %pad_maximum_fusion.w_ref = bf16[64,31744]{1,0:T(8,128)(2,1)} fusion(bf16[64,32768]{1,0:T(8,128)(2,1)} %param.3, bf16[64,15361]{1,0:T(8,128)(2,1)} %collective-permute-done), kind=kLoop, calls=%fused_computation.1 | loop fusion | flops 8126464 | bytes 10223744 | tf_op jit(solution)/shard_map/concatenate | solution.py:260
  68.0 48.3 %shard_map.50 = (bf16[256,16384]{1,0:T(8,128)(2,1)}, f32[256,256]{1,0:T(8,128)S(1)}, f32[1,256]{1,0:T(1,128)S(1)}) custom-call(bf16[64,31744]{1,0:T(8,128)(2,1)} %pad_maximum_fusion.w_ref, f32[64,64,128]{2,1,0:T(8,128)S(1)} %broadcast_in_dim.48.taps_ref, bf16[1,32768]{1,0:T(2,128)(2,1)S(1)} %reshape.14.tgt_ref), custom_call_target="tpu_custom_call" | custom-call | tf_op jit(solution)/shard_map/pallas_call | solution.py:98
  116.3 0.1 copy.24
  116.5 1.3 gather_fusion
  117.8 0.1 copy.27
  118.0 0.1 copy.26
  118.2 1.4 collective-permute-start.1
  119.6 1.2 collective-permute-done.1
  120.9 1.5 collective-permute-start.2
  122.4 7.2 %collective-permute-done.2 = f32[130,256]{0,1:T(8,128)S(1)} collective-permute-done((f32[130,256]{0,1:T(8,128)S(1)}, f32[130,256]{0,1:T(8,128)S(1)}, u32[]{:S(2)}, u32[]{:S(2)}) %collective-permute-start.2) | collective-permute-done | bytes 133152 | tf_op jit(solution)/shard_map/ppermute | solution.py:224
  129.6 1.6 collective-permute-start.3
  131.1 6.2 %collective-permute-done.3 = f32[130,256]{0,1:T(8,128)S(1)} collective-permute-done((f32[130,256]{0,1:T(8,128)S(1)}, f32[130,256]{0,1:T(8,128)S(1)}, u32[]{:S(2)}, u32[]{:S(2)}) %collective-permute-start.3) | collective-permute-done | bytes 133152 | tf_op jit(solution)/shard_map/ppermute | solution.py:224
  137.4 1.6 collective-permute-start.4
  139.0 5.3 %collective-permute-done.4 = f32[130,256]{0,1:T(8,128)S(1)} collective-permute-done((f32[130,256]{0,1:T(8,128)S(1)}, f32[130,256]{0,1:T(8,128)S(1)}, u32[]{:S(2)}, u32[]{:S(2)}) %collective-permute-start.4) | collective-permute-done | bytes 133152 | tf_op jit(solution)/shard_map/ppermute | solution.py:224
  144.4 2.7 %collective-permute-start.5 = (f32[130,256]{0,1:T(8,128)S(1)}, f32[130,256]{0,1:T(8,128)S(1)}, u32[]{:S(2)}, u32[]{:S(2)}) collective-permute-start(f32[130,256]{0,1:T(8,128)S(1)} %add.46), channel_id=1, source_target_pairs={{0,16},{1,17},{2,18},{3,19},{4,20},{5,21},{6,22},{7,23},{8,24},{9,... | collective-permute-start | bytes 399368 | tf_op jit(solution)/shard_map/ppermute | solution.py:224
  147.0 9.9 %collective-permute-done.5 = f32[130,256]{0,1:T(8,128)S(1)} collective-permute-done((f32[130,256]{0,1:T(8,128)S(1)}, f32[130,256]{0,1:T(8,128)S(1)}, u32[]{:S(2)}, u32[]{:S(2)}) %collective-permute-start.5) | collective-permute-done | bytes 133152 | tf_op jit(solution)/shard_map/ppermute | solution.py:224
  157.0 0.2 slice_reduce_fusion.2
  157.2 0.1 slice_reduce_fusion.1
  157.8 0.7 maximum_add_fusion.system_ref
  158.5 0.8 broadcast_in_dim.53.c_ref
  159.2 37.7 %shard_map.52 = f32[256,128]{1,0:T(8,128)} custom-call(f32[256,256]{1,0:T(8,128)} %maximum_add_fusion.system_ref, f32[256,128]{1,0:T(8,128)} %broadcast_in_dim.53.c_ref), custom_call_target="tpu_custom_call" | custom-call | tf_op jit(solution)/shard_map/pallas_call | solution.py:197
  196.9 1.0 slice_reduce_fusion
  198.0 4.6 %fusion.3 = f32[1,16384]{1,0:T(1,128)S(1)} fusion(bf16[256,1]{0,1:T(2,128)(2,1)S(1)} %reshape.21, bf16[256,16384]{1,0:T(8,128)(2,1)} %get-tuple-element.13), kind=kOutput, calls=%fused_computation.22 | convolution fusion | flops 8388608 | bytes 8454656 | tf_op jit(solution)/shard_map/dot_general | solution.py:279
  202.6 4.6 %fusion.2 = f32[1,16384]{1,0:T(1,128)S(1)} fusion(bf16[256,1]{0,1:T(2,128)(2,1)S(1)} %reshape.21, bf16[256,16384]{1,0:T(8,128)(2,1)} %get-tuple-element.12), kind=kOutput, calls=%fused_computation.21 | convolution fusion | flops 8388608 | bytes 8454656 | tf_op jit(solution)/shard_map/dot_general | solution.py:279
  207.1 0.7 maximum_subtract_fusion
  (28 shorter events, 0.8 us)
Async XLA Ops:
  0.6 13.3 %copy-start.1 = (f32[4,16,64]{2,1,0:T(8,128)S(1)}, f32[4,16,64]{2,1,0:T(8,128)}, u32[]{:S(2)}) copy-start(f32[4,16,64]{2,1,0:T(8,128)} %param.5) | copy-start | bytes 49156
  4.0 59.2 %collective-permute-start = (bf16[64,15361]{1,0:T(8,128)(2,1)}, bf16[64,15361]{1,0:T(8,128)(2,1)}, u32[]{:S(2)}, u32[]{:S(2)}) collective-permute-start(bf16[64,15361]{1,0:T(8,128)(2,1)} %slice.33), channel_id=1, source_target_pairs={{0,1},{1,2},{2,3},{3,4},{4,5},{5,6},{6,7},{7,8},{8,9},{9,10},{10,1... | collective-permute-start | bytes 5898632 | tf_op jit(solution)/shard_map/ppermute | solution.py:16
  118.2 2.5 %collective-permute-start.1 = (f32[130,256]{0,1:T(8,128)S(1)}, f32[130,256]{0,1:T(8,128)S(1)}, u32[]{:S(2)}, u32[]{:S(2)}) collective-permute-start(f32[130,256]{0,1:T(8,128)S(1)} %pad_maximum_fusion.1), channel_id=1, source_target_pairs={{0,1},{1,0},{2,3},{3,2},{4,5},{5,4},{6,7},{7,6},{8,9},{9,8},{10,11... | collective-permute-start | bytes 399368 | tf_op jit(solution)/shard_map/ppermute | solution.py:224
  120.9 8.7 %collective-permute-start.2 = (f32[130,256]{0,1:T(8,128)S(1)}, f32[130,256]{0,1:T(8,128)S(1)}, u32[]{:S(2)}, u32[]{:S(2)}) collective-permute-start(f32[130,256]{0,1:T(8,128)S(1)} %fusion.8), channel_id=1, source_target_pairs={{0,2},{1,3},{2,0},{3,1},{4,6},{5,7},{6,4},{7,5},{8,10},{9,11},{10,... | collective-permute-start | bytes 399368 | tf_op jit(solution)/shard_map/ppermute | solution.py:224
  129.6 7.8 %collective-permute-start.3 = (f32[130,256]{0,1:T(8,128)S(1)}, f32[130,256]{0,1:T(8,128)S(1)}, u32[]{:S(2)}, u32[]{:S(2)}) collective-permute-start(f32[130,256]{0,1:T(8,128)S(1)} %add.44), channel_id=1, source_target_pairs={{0,4},{1,5},{2,6},{3,7},{4,0},{5,1},{6,2},{7,3},{8,12},{9,13},{10,... | collective-permute-start | bytes 399368 | tf_op jit(solution)/shard_map/ppermute | solution.py:224
  137.4 6.9 %collective-permute-start.4 = (f32[130,256]{0,1:T(8,128)S(1)}, f32[130,256]{0,1:T(8,128)S(1)}, u32[]{:S(2)}, u32[]{:S(2)}) collective-permute-start(f32[130,256]{0,1:T(8,128)S(1)} %add.45), channel_id=1, source_target_pairs={{0,8},{1,9},{2,10},{3,11},{4,12},{5,13},{6,14},{7,15},{8,0},{9,1},... | collective-permute-start | bytes 399368 | tf_op jit(solution)/shard_map/ppermute | solution.py:224
  144.4 12.6 %collective-permute-start.5 = (f32[130,256]{0,1:T(8,128)S(1)}, f32[130,256]{0,1:T(8,128)S(1)}, u32[]{:S(2)}, u32[]{:S(2)}) collective-permute-start(f32[130,256]{0,1:T(8,128)S(1)} %add.46), channel_id=1, source_target_pairs={{0,16},{1,17},{2,18},{3,19},{4,20},{5,21},{6,22},{7,23},{8,24},{9,... | collective-permute-start | bytes 399368 | tf_op jit(solution)/shard_map/ppermute | solution.py:224
  197.9 9.2 %copy-start.2 = (f32[256]{0:T(256)}, f32[256]{0:T(256)S(1)}, u32[]{:S(2)}) copy-start(f32[256]{0:T(256)S(1)} %slice_reduce_fusion) | copy-start | bytes 3076
  197.9 9.2 %copy-start = (bf16[32768]{0:T(1024)(128)(2,1)S(1)}, bf16[32768]{0:T(1024)(128)(2,1)}, u32[]{:S(2)}) copy-start(bf16[32768]{0:T(1024)(128)(2,1)} %param.4) | copy-start | bytes 196612

commit v6 on v5

--- a/solution.py
+++ b/solution.py
@@ -40,7 +40,7 @@
 WIDE_CHUNK = 1024
 
 
-def feature_kernel(dilations, span, base, first_block, taps_per_filter, w_ref, taps_ref, tgt_ref, f_ref, g_ref, c_ref):
+def feature_kernel(dilations, span, base, first_block, length, taps_per_filter, w_ref, taps_ref, tgt_ref, f_ref, g_ref, c_ref):
     block = pl.program_id(0)
     block_len = f_ref.shape[1]
     channels = w_ref.shape[0]
@@ -78,7 +78,8 @@
 
             lax.fori_loop(0, block_len // chunk, chunk_body, 0)
 
-    feats = f_ref[...]
+    cols = (first_block + block) * block_len + lax.broadcasted_iota(jnp.int32, (1, block_len), 1)
+    feats = jnp.where(cols < length - 1, f_ref[...], jnp.zeros_like(f_ref[...]))
     g_ref[...] += lax.dot_general(feats, feats, (((1,), (1,)), ((), ())), preferred_element_type=jnp.float32)
     c_ref[...] += lax.dot_general(tgt_ref[...], feats, (((1,), (1,)), ((), ())), preferred_element_type=jnp.float32)
 
@@ -94,7 +95,7 @@
         depthwise_taps.reshape(n_filters * taps_per_filter, channels, 1),
         (n_filters * taps_per_filter, channels, 128),
     )
-    kernel = functools.partial(feature_kernel, dilations, span, base, first_block, taps_per_filter)
+    kernel = functools.partial(feature_kernel, dilations, span, base, first_block, length, taps_per_filter)
     return pl.pallas_call(
         kernel,
         grid=(n_blocks,),
@@ -173,22 +174,24 @@
     n = a_ref.shape[0]
     a_ref[...] = system_ref[...]
     x_ref[...] = c_ref[...]
-    lanes = lax.broadcasted_iota(jnp.int32, (1, n), 1)
     sublanes = lax.broadcasted_iota(jnp.int32, (n, 1), 0)
 
-    def step(j, carry):
-        at = lanes == j
-        here = sublanes == j
-        row = a_ref[pl.ds(j, 1), :]
-        pivot = jnp.sum(jnp.where(at, row, 0.0), axis=1, keepdims=True)
-        column = jnp.sum(jnp.where(at, a_ref[...], 0.0), axis=1, keepdims=True)
-        scaled_row = row / pivot
-        scaled_rhs = x_ref[pl.ds(j, 1), :] / pivot
-        a_ref[...] = jnp.where(here, scaled_row, a_ref[...] - column * scaled_row)
-        x_ref[...] = jnp.where(here, scaled_rhs, x_ref[...] - column * scaled_rhs)
-        return carry
-
-    lax.fori_loop(0, n, step, 0)
+    for lo in range(0, n, 128):
+        lanes = lo + lax.broadcasted_iota(jnp.int32, (1, n - lo), 1)
+
+        def step(j, carry, lo=lo, lanes=lanes):
+            at = lanes == j
+            here = sublanes == j
+            row = a_ref[pl.ds(j, 1), :][:, lo:]
+            pivot = jnp.sum(jnp.where(at, row, 0.0), axis=1, keepdims=True)
+            column = jnp.sum(jnp.where(at, a_ref[:, lo:], 0.0), axis=1, keepdims=True)
+            scaled_row = row / pivot
+            scaled_rhs = x_ref[pl.ds(j, 1), :] / pivot
+            a_ref[:, lo:] = jnp.where(here, scaled_row, a_ref[:, lo:] - column * scaled_row)
+            x_ref[...] = jnp.where(here, scaled_rhs, x_ref[...] - column * scaled_rhs)
+            return carry
+
+        lax.fori_loop(lo, min(n, lo + 128), step, 0)
 
 
 def ridge_solve_jordan(system, cross_sum, interpret=False):
@@ -247,36 +250,52 @@
     return gram_sum, packed[h]
 
 
+def first_features(history, depthwise_taps, top_dilation):
+    last = history.shape[1] - 1
+    picks = jnp.asarray(
+        [[last - k * d for k in range(depthwise_taps.shape[1])] for d in dilation_list(top_dilation)],
+        jnp.int32,
+    )
+    samples = jnp.transpose(history[:, picks], (1, 2, 0)).astype(jnp.float32)
+    total = jnp.zeros(samples.shape[::2], jnp.float32)
+    for k in range(depthwise_taps.shape[1]):
+        total = total + depthwise_taps[:, k] * samples[:, k]
+    return total.astype(jnp.bfloat16).reshape(-1)
+
+
 def local(stream, target, depthwise_taps):
     length = stream.shape[1]
     top_dilation = min(1024, length // 16)
     history_len = 15 * top_dilation + 1
-    tail_end = stream[:, length - history_len :]
-    previous = shifted(tail_end, ("wide", "narrow"), 1)
     span = history_len - 1
+    sent = min(length, -(-history_len // 128) * 128)
+    previous = shifted(stream[:, length - sent :], ("wide", "narrow"), 1)
     block_len = min(TIME_BLOCK, length)
     n_blocks = length // block_len
     split = min(n_blocks, -(-span // block_len))
-    window = jnp.concatenate([previous, stream], 1)[:, : split * block_len + span]
-    features, gram_sum, cross_sum = features_and_sums(
-        window, 0, 0, split, depthwise_taps, target, top_dilation, length
-    )
+    ahead = jnp.concatenate([target[1:], jnp.zeros_like(target[:1])])
+    window = jnp.concatenate([previous[:, sent - span :], stream[:, : split * block_len]], 1)
+    early, gram_sum, cross_sum = features_and_sums(
+        window, 0, 0, split, depthwise_taps, ahead, top_dilation, length
+    )
+    parts = [early]
     if split < n_blocks:
-        delayed = jnp.concatenate([jnp.zeros_like(stream[:, :1]), stream[:, : length - 1]], 1)
-        late_features, late_gram, late_cross = features_and_sums(
-            delayed, span, split, n_blocks - split, depthwise_taps, target, top_dilation, length
+        late, late_gram, late_cross = features_and_sums(
+            stream, span, split, n_blocks - split, depthwise_taps, ahead, top_dilation, length
         )
-        features = (features, late_features)
+        parts.append(late)
         gram_sum, cross_sum = gram_sum + late_gram, cross_sum + late_cross
-    else:
-        features = (features,)
-    cross_sum = cross_sum[0]
+    first = first_features(previous, depthwise_taps, top_dilation).astype(jnp.float32)
+    gram_sum = gram_sum + first[:, None] * first[None, :]
+    cross_sum = cross_sum[0] + first * target[0].astype(jnp.float32)
     gram_sum, cross_sum = reduce_system(gram_sum, cross_sum, ("wide", "narrow"))
     total_rows = length * lax.axis_size("wide") * lax.axis_size("narrow")
     system = gram_sum + ridge_share * total_rows * jnp.eye(gram_sum.shape[0], dtype=jnp.float32)
     coefficients = ridge_solve_jordan(system, cross_sum)
     rounded = coefficients.astype(jnp.bfloat16)
-    fitted = jnp.concatenate([jnp.dot(rounded, f, preferred_element_type=jnp.float32) for f in features])
+    fitted = [jnp.dot(rounded, first.astype(jnp.bfloat16), preferred_element_type=jnp.float32)[None]]
+    fitted += [jnp.dot(rounded, f, preferred_element_type=jnp.float32) for f in parts]
+    fitted = jnp.concatenate(fitted)[:length]
     return (coefficients, target.astype(jnp.float32) - fitted)
 
 

time: 208 us -> 213 us (1.024)
  local copies, waits for them, and re-layouts: 14.4 us -> 22.9 us
  Pallas kernels: 134 us -> 131 us
    ppermute x0 -> x1, local copies, waits for them, and re-layouts: none -> 4.77 us  [shifted(): return lax.ppermute(array, axis, pairs)]
    concatenate x1, local copies, waits for them, and re-layouts: 5.29 us -> 0.76 us  [local(): fitted = jnp.concatenate(fitted)[:length]]
    slice x1 -> x6, local copies, waits for them, and re-layouts: 3.41 us -> 7.35 us  [the longest x1 3.03 us: local(): previous = shifted(stream[:, length - sent:], ('wide', 'narrow'), 1)]
    gather x0 -> x1, local copies, waits for them, and re-layouts: none -> 3.23 us  [first_features(): samples = jnp.transpose(history[:, picks], (1, 2, 0)).astype(jnp.float32)]
    concatenate x1 -> x2, other arithmetic: 4.81 us -> 2.25 us  [the longest x1 2.18 us: local(): jnp.concatenate([previous[:, sent - span:], stream[:, :split * block_len]...]
    pallas_call x1, Pallas kernels: 37.7 us -> 35.4 us  [ridge_solve_jordan(): pl.pallas_call(jordan_kernel, in_specs=[pl.BlockSpec(memory_space=pltpu.V...]
  transfers between devices with their start and end apart: 6 -> 6, of which waited for: 5 -> 5; matrix products, arithmetic and copies ran while one was open for 3% -> 1% of each run, Pallas kernels for 23% -> 23%
where the time goes in v6:
time: 213 us
  Pallas kernels  131 us (62%)
  waiting for transfers between devices  29.7 us (14%)
  local copies, waits for them, and re-layouts  22.9 us (11%)
  starting transfers between devices  12.4 us (6%)
  matrix products  9.18 us (4%)
  other arithmetic  5.62 us (3%)
    pallas_call x2, Pallas kernels, features_and_sums(): pl.pallas_call(kernel, grid=(n_blocks,), in_specs=[pl.BlockSpec(memory_sp...  95.9 us
    pallas_call x1, Pallas kernels, ridge_solve_jordan(): pl.pallas_call(jordan_kernel, in_specs=[pl.BlockSpec(memory_space=pltpu.V...  35.4 us
    ppermute x5, waiting for transfers between devices, butterfly_sum(): x = x + lax.ppermute(x, axes, [(i, i ^ step) for i in range(size)])  29.7 us
    dot_general x2, matrix products, local(): jnp.dot(rounded, f, preferred_element_type=jnp.float32)  9.18 us
    ppermute x5, starting transfers between devices, butterfly_sum(): x = x + lax.ppermute(x, axes, [(i, i ^ step) for i in range(size)])  8.72 us
    ppermute x1, local copies, waits for them, and re-layouts, shifted(): return lax.ppermute(array, axis, pairs)  4.77 us
  transfers between devices with their start and end apart: 6, of which 5 were waited for; matrix products, arithmetic and copies ran while one was open for 1% of the time, Pallas kernels for 23%

profile of v6, /device:TPU:0, one launch (start us, length us, event | category | flops | bytes accessed | tf_op | source)
XLA Modules:
  0.0 212.7 jit_solution(11257369606307796226)
XLA Ops:
  0.6 3.0 %slice.138 = bf16[64,15488]{1,0:T(8,128)(2,1)} slice(bf16[64,32768]{1,0:T(8,128)(2,1)} %w_ref.1), slice={[0:64], [17280:32768]} | slice | bytes 3964928 | tf_op jit(solution)/shard_map/slice | solution.py:272
  3.7 3.7 %collective-permute-start = (bf16[64,15488]{1,0:T(8,128)(2,1)}, bf16[64,15488]{1,0:T(8,128)(2,1)}, u32[]{:S(2)}, u32[]{:S(2)}) collective-permute-start(bf16[64,15488]{1,0:T(8,128)(2,1)} %slice.138), channel_id=1, source_target_pairs={{0,1},{1,2},{2,3},{3,4},{4,5},{5,6},{6,7},{7,8},{8,9},{9,10},{10,1... | collective-permute-start | bytes 5947400 | tf_op jit(solution)/shard_map/ppermute | solution.py:16
  7.4 1.2 slice.177
  8.6 0.9 slice.141
  10.9 48.0 %shard_map.60 = (bf16[256,16384]{1,0:T(8,128)(2,1)}, f32[256,256]{1,0:T(8,128)S(1)}, f32[1,256]{1,0:T(1,128)S(1)}) custom-call(bf16[64,32768]{1,0:T(8,128)(2,1)} %w_ref.1, f32[64,64,128]{2,1,0:T(8,128)S(1)} %broadcast_in_dim.55.taps_ref, bf16[1,32768]{1,0:T(2,128)(2,1)S(1)} %reshape.672.tgt_ref), custom_call_target="tpu_custom_call" | custom-call | tf_op jit(solution)/shard_map/pallas_call | solution.py:99
  59.1 4.8 %copy.30 = bf16[64,15488]{0,1:T(8,128)(2,1)} copy(bf16[64,15488]{1,0:T(8,128)(2,1)} %collective-permute-done) | data formatting | bytes 3964928 | tf_op jit(solution)/shard_map/ppermute | solution.py:16
  63.9 3.2 %gather_fusion = bf16[64,64]{1,0:T(8,128)(2,1)S(1)} fusion(bf16[64,15488]{0,1:T(8,128)(2,1)} %copy.30, s32[1024]{0:T(1024)S(1)} %pad_clamp_fusion), kind=kCustom, calls=%fused_computation | custom fusion | bytes 16640 | tf_op jit(solution)/shard_map/gather | solution.py:259
  67.7 0.7 reduce.17
  68.7 1.8 slice.188
  70.9 2.2 %pad_maximum_fusion.w_ref = bf16[64,31744]{1,0:T(8,128)(2,1)} fusion(bf16[64,16384]{1,0:T(8,128)(2,1)S(1)} %slice-done, bf16[64,15360]{1,0:T(8,128)(2,1)S(1)} %slice.188), kind=kLoop, calls=%fused_computation.2 | loop fusion | flops 8126464 | bytes 8126464 | tf_op jit(solution)/shard_map/concatenate | solution.py:277
  73.1 47.9 %shard_map.59 = (bf16[256,16384]{1,0:T(8,128)(2,1)}, f32[256,256]{1,0:T(8,128)S(1)}, f32[1,256]{1,0:T(1,128)S(1)}) custom-call(bf16[64,31744]{1,0:T(8,128)(2,1)} %pad_maximum_fusion.w_ref, f32[64,64,128]{2,1,0:T(8,128)S(1)} %broadcast_in_dim.55.taps_ref, bf16[1,32768]{1,0:T(2,128)(2,1)S(1)} %reshape.672.tgt_ref), custom_call_target="tpu_custom_call" | custom-call | tf_op jit(solution)/shard_map/pallas_call | solution.py:99
  121.3 1.3 gather_fusion.1
  123.0 1.4 collective-permute-start.1
  124.4 1.2 collective-permute-done.1
  125.6 1.5 collective-permute-start.2
  127.1 7.2 %collective-permute-done.2 = f32[130,256]{0,1:T(8,128)S(1)} collective-permute-done((f32[130,256]{0,1:T(8,128)S(1)}, f32[130,256]{0,1:T(8,128)S(1)}, u32[]{:S(2)}, u32[]{:S(2)}) %collective-permute-start.2) | collective-permute-done | bytes 133152 | tf_op jit(solution)/shard_map/ppermute | solution.py:227
  134.3 1.6 collective-permute-start.3
  135.9 6.2 %collective-permute-done.3 = f32[130,256]{0,1:T(8,128)S(1)} collective-permute-done((f32[130,256]{0,1:T(8,128)S(1)}, f32[130,256]{0,1:T(8,128)S(1)}, u32[]{:S(2)}, u32[]{:S(2)}) %collective-permute-start.3) | collective-permute-done | bytes 133152 | tf_op jit(solution)/shard_map/ppermute | solution.py:227
  142.2 1.6 collective-permute-start.4
  143.8 5.3 %collective-permute-done.4 = f32[130,256]{0,1:T(8,128)S(1)} collective-permute-done((f32[130,256]{0,1:T(8,128)S(1)}, f32[130,256]{0,1:T(8,128)S(1)}, u32[]{:S(2)}, u32[]{:S(2)}) %collective-permute-start.4) | collective-permute-done | bytes 133152 | tf_op jit(solution)/shard_map/ppermute | solution.py:227
  149.1 2.7 %collective-permute-start.5 = (f32[130,256]{0,1:T(8,128)S(1)}, f32[130,256]{0,1:T(8,128)S(1)}, u32[]{:S(2)}, u32[]{:S(2)}) collective-permute-start(f32[130,256]{0,1:T(8,128)S(1)} %add.433), channel_id=1, source_target_pairs={{0,16},{1,17},{2,18},{3,19},{4,20},{5,21},{6,22},{7,23},{8,24},{9,... | collective-permute-start | bytes 399368 | tf_op jit(solution)/shard_map/ppermute | solution.py:227
  151.9 9.9 %collective-permute-done.5 = f32[130,256]{0,1:T(8,128)S(1)} collective-permute-done((f32[130,256]{0,1:T(8,128)S(1)}, f32[130,256]{0,1:T(8,128)S(1)}, u32[]{:S(2)}, u32[]{:S(2)}) %collective-permute-start.5) | collective-permute-done | bytes 133152 | tf_op jit(solution)/shard_map/ppermute | solution.py:227
  162.5 0.7 maximum_add_fusion.system_ref
  163.3 0.8 broadcast_in_dim.61.c_ref
  164.0 35.4 %shard_map.61 = f32[256,128]{1,0:T(8,128)} custom-call(f32[256,256]{1,0:T(8,128)} %maximum_add_fusion.system_ref, f32[256,128]{1,0:T(8,128)} %broadcast_in_dim.61.c_ref), custom_call_target="tpu_custom_call" | custom-call | tf_op jit(solution)/shard_map/pallas_call | solution.py:200
  199.4 1.0 fusion
  200.4 1.0 slice_reduce_fusion.1
  201.5 4.6 %fusion.21 = f32[1,16384]{1,0:T(1,128)S(1)} fusion(bf16[256,1]{0,1:T(2,128)(2,1)S(1)} %reshape.717, bf16[256,16384]{1,0:T(8,128)(2,1)} %get-tuple-element.13), kind=kOutput, calls=%fused_computation.66 | convolution fusion | flops 8388608 | bytes 8454656 | tf_op jit(solution)/shard_map/dot_general | solution.py:297
  206.0 4.6 %fusion.20 = f32[1,16384]{1,0:T(1,128)S(1)} fusion(bf16[256,1]{0,1:T(2,128)(2,1)S(1)} %reshape.717, bf16[256,16384]{1,0:T(8,128)(2,1)} %get-tuple-element.12), kind=kOutput, calls=%fused_computation.65 | convolution fusion | flops 8388608 | bytes 8454656 | tf_op jit(solution)/shard_map/dot_general | solution.py:297
  210.7 0.6 fusion.18
  211.3 0.8 concatenate.40
  212.0 0.7 slice_subtract_fusion
  (50 shorter events, 3.9 us)
Async XLA Ops:
  0.6 9.7 %copy-start.1 = (f32[4,16,64]{2,1,0:T(8,128)S(1)}, f32[4,16,64]{2,1,0:T(8,128)}, u32[]{:S(2)}) copy-start(f32[4,16,64]{2,1,0:T(8,128)} %param.6) | copy-start | bytes 49156
  3.7 55.4 %collective-permute-start = (bf16[64,15488]{1,0:T(8,128)(2,1)}, bf16[64,15488]{1,0:T(8,128)(2,1)}, u32[]{:S(2)}, u32[]{:S(2)}) collective-permute-start(bf16[64,15488]{1,0:T(8,128)(2,1)} %slice.138), channel_id=1, source_target_pairs={{0,1},{1,2},{2,3},{3,4},{4,5},{5,6},{6,7},{7,8},{8,9},{9,10},{10,1... | collective-permute-start | bytes 5947400 | tf_op jit(solution)/shard_map/ppermute | solution.py:16
  10.3 48.7 %copy-start.3 = (s32[64]{0:T(128)S(1)}, s32[64]{0:T(128)}, u32[]{:S(2)}) copy-start(s32[64]{0:T(128)} %constant.41) | copy-start | bytes 772
  68.7 2.2 %slice-start = ((bf16[64,32768]{1,0:T(8,128)(2,1)}), bf16[64,16384]{1,0:T(8,128)(2,1)S(1)}, s32[]{:S(2)}) async-start(bf16[64,32768]{1,0:T(8,128)(2,1)} %w_ref.1), calls=%async_computation | async-start | bytes 4194304 | tf_op jit(solution)/shard_map/slice | solution.py:277
  123.0 2.5 %collective-permute-start.1 = (f32[130,256]{0,1:T(8,128)S(1)}, f32[130,256]{0,1:T(8,128)S(1)}, u32[]{:S(2)}, u32[]{:S(2)}) collective-permute-start(f32[130,256]{0,1:T(8,128)S(1)} %pad_maximum_fusion.1), channel_id=1, source_target_pairs={{0,1},{1,0},{2,3},{3,2},{4,5},{5,4},{6,7},{7,6},{8,9},{9,8},{10,11... | collective-permute-start | bytes 399368 | tf_op jit(solution)/shard_map/ppermute | solution.py:227
  125.6 8.7 %collective-permute-start.2 = (f32[130,256]{0,1:T(8,128)S(1)}, f32[130,256]{0,1:T(8,128)S(1)}, u32[]{:S(2)}, u32[]{:S(2)}) collective-permute-start(f32[130,256]{0,1:T(8,128)S(1)} %fusion.26), channel_id=1, source_target_pairs={{0,2},{1,3},{2,0},{3,1},{4,6},{5,7},{6,4},{7,5},{8,10},{9,11},{10,... | collective-permute-start | bytes 399368 | tf_op jit(solution)/shard_map/ppermute | solution.py:227
  134.3 7.8 %collective-permute-start.3 = (f32[130,256]{0,1:T(8,128)S(1)}, f32[130,256]{0,1:T(8,128)S(1)}, u32[]{:S(2)}, u32[]{:S(2)}) collective-permute-start(f32[130,256]{0,1:T(8,128)S(1)} %add.431), channel_id=1, source_target_pairs={{0,4},{1,5},{2,6},{3,7},{4,0},{5,1},{6,2},{7,3},{8,12},{9,13},{10,... | collective-permute-start | bytes 399368 | tf_op jit(solution)/shard_map/ppermute | solution.py:227
  142.2 6.9 %collective-permute-start.4 = (f32[130,256]{0,1:T(8,128)S(1)}, f32[130,256]{0,1:T(8,128)S(1)}, u32[]{:S(2)}, u32[]{:S(2)}) collective-permute-start(f32[130,256]{0,1:T(8,128)S(1)} %add.432), channel_id=1, source_target_pairs={{0,8},{1,9},{2,10},{3,11},{4,12},{5,13},{6,14},{7,15},{8,0},{9,1},... | collective-permute-start | bytes 399368 | tf_op jit(solution)/shard_map/ppermute | solution.py:227
  149.1 12.6 %collective-permute-start.5 = (f32[130,256]{0,1:T(8,128)S(1)}, f32[130,256]{0,1:T(8,128)S(1)}, u32[]{:S(2)}, u32[]{:S(2)}) collective-permute-start(f32[130,256]{0,1:T(8,128)S(1)} %add.433), channel_id=1, source_target_pairs={{0,16},{1,17},{2,18},{3,19},{4,20},{5,21},{6,22},{7,23},{8,24},{9,... | collective-permute-start | bytes 399368 | tf_op jit(solution)/shard_map/ppermute | solution.py:227
  201.4 4.6 %copy-start.2 = (f32[256]{0:T(256)}, f32[256]{0:T(256)S(1)}, u32[]{:S(2)}) copy-start(f32[256]{0:T(256)S(1)} %slice_reduce_fusion.1) | copy-start | bytes 3076
  206.0 6.0 %copy-start = (bf16[32768]{0:T(1024)(128)(2,1)S(1)}, bf16[32768]{0:T(1024)(128)(2,1)}, u32[]{:S(2)}) copy-start(bf16[32768]{0:T(1024)(128)(2,1)} %param.5) | copy-start | bytes 196612

commit v7 on v6

--- a/solution.py
+++ b/solution.py
@@ -251,14 +251,17 @@
 
 
 def first_features(history, depthwise_taps, top_dilation):
+    taps_per_filter = depthwise_taps.shape[1]
     last = history.shape[1] - 1
-    picks = jnp.asarray(
-        [[last - k * d for k in range(depthwise_taps.shape[1])] for d in dilation_list(top_dilation)],
-        jnp.int32,
-    )
-    samples = jnp.transpose(history[:, picks], (1, 2, 0)).astype(jnp.float32)
+    samples = jnp.stack(
+        [
+            history[:, last - (taps_per_filter - 1) * d : last + 1 : d][:, ::-1]
+            for d in dilation_list(top_dilation)
+        ]
+    )
+    samples = jnp.transpose(samples, (0, 2, 1)).astype(jnp.float32)
     total = jnp.zeros(samples.shape[::2], jnp.float32)
-    for k in range(depthwise_taps.shape[1]):
+    for k in range(taps_per_filter):
         total = total + depthwise_taps[:, k] * samples[:, k]
     return total.astype(jnp.bfloat16).reshape(-1)
 

time: 213 us -> 211 us (level)
  local copies, waits for them, and re-layouts: 22.9 us -> 20.3 us
    slice x0 -> x4, local copies, waits for them, and re-layouts: none -> 4.77 us  [first_features(): history[:, last - (taps_per_filter - 1) * d:last + 1:d][:, ::-1]]
    ppermute x1 -> x0, local copies, waits for them, and re-layouts: 4.77 us -> none  [shifted(): return lax.ppermute(array, axis, pairs)]
    gather x1 -> x0, local copies, waits for them, and re-layouts: 3.23 us -> none  [first_features(): samples = jnp.transpose(history[:, picks], (1, 2, 0)).astype(jnp.float32)]
where the time goes in v7:
time: 211 us; the launch traced here: 210 us
  Pallas kernels  131 us (62%)
  waiting for transfers between devices  29.7 us (14%)
  local copies, waits for them, and re-layouts  20.3 us (10%)
  starting transfers between devices  12.4 us (6%)
  matrix products  9.18 us (4%)
  other arithmetic  5.64 us (3%)
    pallas_call x2, Pallas kernels, features_and_sums(): pl.pallas_call(kernel, grid=(n_blocks,), in_specs=[pl.BlockSpec(memory_sp...  95.9 us
    pallas_call x1, Pallas kernels, ridge_solve_jordan(): pl.pallas_call(jordan_kernel, in_specs=[pl.BlockSpec(memory_space=pltpu.V...  35.4 us
    ppermute x5, waiting for transfers between devices, butterfly_sum(): x = x + lax.ppermute(x, axes, [(i, i ^ step) for i in range(size)])  29.7 us
    dot_general x2, matrix products, local(): jnp.dot(rounded, f, preferred_element_type=jnp.float32)  9.18 us
    ppermute x5, starting transfers between devices, butterfly_sum(): x = x + lax.ppermute(x, axes, [(i, i ^ step) for i in range(size)])  8.77 us
    slice x4, local copies, waits for them, and re-layouts, first_features(): history[:, last - (taps_per_filter - 1) * d:last + 1:d][:, ::-1]  4.77 us
  transfers between devices with their start and end apart: 6, of which 5 were waited for; matrix products, arithmetic and copies ran while one was open for 1% of the time, Pallas kernels for 23%

profile of v7, /device:TPU:0, one launch (start us, length us, event | category | flops | bytes accessed | tf_op | source)
XLA Modules:
  0.0 210.2 jit_solution(9431332975354207262)
XLA Ops:
  0.6 3.0 %slice.150 = bf16[64,15488]{1,0:T(8,128)(2,1)} slice(bf16[64,32768]{1,0:T(8,128)(2,1)} %w_ref.1), slice={[0:64], [17280:32768]} | slice | bytes 3964928 | tf_op jit(solution)/shard_map/slice | solution.py:275
  3.7 3.7 %collective-permute-start = (bf16[64,15488]{1,0:T(8,128)(2,1)}, bf16[64,15488]{1,0:T(8,128)(2,1)}, u32[]{:S(2)}, u32[]{:S(2)}) collective-permute-start(bf16[64,15488]{1,0:T(8,128)(2,1)} %slice.150), channel_id=1, source_target_pairs={{0,1},{1,2},{2,3},{3,4},{4,5},{5,6},{6,7},{7,8},{8,9},{9,10},{10,1... | collective-permute-start | bytes 5947400 | tf_op jit(solution)/shard_map/ppermute | solution.py:16
  7.3 1.2 slice.193
  8.5 0.9 slice.153
  10.9 48.0 %shard_map.51 = (bf16[256,16384]{1,0:T(8,128)(2,1)}, f32[256,256]{1,0:T(8,128)S(1)}, f32[1,256]{1,0:T(1,128)S(1)}) custom-call(bf16[64,32768]{1,0:T(8,128)(2,1)} %w_ref.1, f32[64,64,128]{2,1,0:T(8,128)S(1)} %broadcast_in_dim.52.taps_ref, bf16[1,32768]{1,0:T(2,128)(2,1)S(1)} %reshape.672.tgt_ref), custom_call_target="tpu_custom_call" | custom-call | tf_op jit(solution)/shard_map/pallas_call | solution.py:99
  59.0 1.7 slice.158
  60.9 1.2 slice.157
  62.2 1.1 slice.156
  63.5 0.8 slice.203
  66.1 1.8 slice.202
  68.3 2.2 %pad_maximum_fusion.w_ref = bf16[64,31744]{1,0:T(8,128)(2,1)} fusion(bf16[64,16384]{1,0:T(8,128)(2,1)S(1)} %slice-done, bf16[64,15360]{1,0:T(8,128)(2,1)S(1)} %slice.202), kind=kLoop, calls=%fused_computation.1 | loop fusion | flops 8126464 | bytes 8126464 | tf_op jit(solution)/shard_map/concatenate | solution.py:280
  70.5 47.9 %shard_map.50 = (bf16[256,16384]{1,0:T(8,128)(2,1)}, f32[256,256]{1,0:T(8,128)S(1)}, f32[1,256]{1,0:T(1,128)S(1)}) custom-call(bf16[64,31744]{1,0:T(8,128)(2,1)} %pad_maximum_fusion.w_ref, f32[64,64,128]{2,1,0:T(8,128)S(1)} %broadcast_in_dim.52.taps_ref, bf16[1,32768]{1,0:T(2,128)(2,1)S(1)} %reshape.672.tgt_ref), custom_call_target="tpu_custom_call" | custom-call | tf_op jit(solution)/shard_map/pallas_call | solution.py:99
  118.7 1.3 gather_fusion
  120.4 1.4 collective-permute-start.1
  121.8 1.2 collective-permute-done.1
  123.1 1.5 collective-permute-start.2
  124.6 7.2 %collective-permute-done.2 = f32[130,256]{0,1:T(8,128)S(1)} collective-permute-done((f32[130,256]{0,1:T(8,128)S(1)}, f32[130,256]{0,1:T(8,128)S(1)}, u32[]{:S(2)}, u32[]{:S(2)}) %collective-permute-start.2) | collective-permute-done | bytes 133152 | tf_op jit(solution)/shard_map/ppermute | solution.py:227
  131.8 1.6 collective-permute-start.3
  133.3 6.2 %collective-permute-done.3 = f32[130,256]{0,1:T(8,128)S(1)} collective-permute-done((f32[130,256]{0,1:T(8,128)S(1)}, f32[130,256]{0,1:T(8,128)S(1)}, u32[]{:S(2)}, u32[]{:S(2)}) %collective-permute-start.3) | collective-permute-done | bytes 133152 | tf_op jit(solution)/shard_map/ppermute | solution.py:227
  139.6 1.6 collective-permute-start.4
  141.2 5.3 %collective-permute-done.4 = f32[130,256]{0,1:T(8,128)S(1)} collective-permute-done((f32[130,256]{0,1:T(8,128)S(1)}, f32[130,256]{0,1:T(8,128)S(1)}, u32[]{:S(2)}, u32[]{:S(2)}) %collective-permute-start.4) | collective-permute-done | bytes 133152 | tf_op jit(solution)/shard_map/ppermute | solution.py:227
  146.6 2.7 %collective-permute-start.5 = (f32[130,256]{0,1:T(8,128)S(1)}, f32[130,256]{0,1:T(8,128)S(1)}, u32[]{:S(2)}, u32[]{:S(2)}) collective-permute-start(f32[130,256]{0,1:T(8,128)S(1)} %add.425), channel_id=1, source_target_pairs={{0,16},{1,17},{2,18},{3,19},{4,20},{5,21},{6,22},{7,23},{8,24},{9,... | collective-permute-start | bytes 399368 | tf_op jit(solution)/shard_map/ppermute | solution.py:227
  149.3 9.9 %collective-permute-done.5 = f32[130,256]{0,1:T(8,128)S(1)} collective-permute-done((f32[130,256]{0,1:T(8,128)S(1)}, f32[130,256]{0,1:T(8,128)S(1)}, u32[]{:S(2)}, u32[]{:S(2)}) %collective-permute-start.5) | collective-permute-done | bytes 133152 | tf_op jit(solution)/shard_map/ppermute | solution.py:227
  160.0 0.7 maximum_add_fusion.system_ref
  160.7 0.8 broadcast_in_dim.57.c_ref
  161.4 35.4 %shard_map.52 = f32[256,128]{1,0:T(8,128)} custom-call(f32[256,256]{1,0:T(8,128)} %maximum_add_fusion.system_ref, f32[256,128]{1,0:T(8,128)} %broadcast_in_dim.57.c_ref), custom_call_target="tpu_custom_call" | custom-call | tf_op jit(solution)/shard_map/pallas_call | solution.py:200
  196.8 1.0 fusion
  197.8 1.0 slice_reduce_fusion.1
  198.9 4.6 %fusion.21 = f32[1,16384]{1,0:T(1,128)S(1)} fusion(bf16[256,1]{0,1:T(2,128)(2,1)S(1)} %reshape.707, bf16[256,16384]{1,0:T(8,128)(2,1)} %get-tuple-element.13), kind=kOutput, calls=%fused_computation.64 | convolution fusion | flops 8388608 | bytes 8454656 | tf_op jit(solution)/shard_map/dot_general | solution.py:300
  203.5 4.6 %fusion.20 = f32[1,16384]{1,0:T(1,128)S(1)} fusion(bf16[256,1]{0,1:T(2,128)(2,1)S(1)} %reshape.707, bf16[256,16384]{1,0:T(8,128)(2,1)} %get-tuple-element.12), kind=kOutput, calls=%fused_computation.63 | convolution fusion | flops 8388608 | bytes 8454656 | tf_op jit(solution)/shard_map/dot_general | solution.py:300
  208.7 0.8 concatenate.40
  209.5 0.7 slice_subtract_fusion
  (57 shorter events, 5.8 us)
Async XLA Ops:
  0.6 9.6 %copy-start.1 = (f32[4,16,64]{2,1,0:T(8,128)S(1)}, f32[4,16,64]{2,1,0:T(8,128)}, u32[]{:S(2)}) copy-start(f32[4,16,64]{2,1,0:T(8,128)} %param.5) | copy-start | bytes 49156
  3.7 55.3 %collective-permute-start = (bf16[64,15488]{1,0:T(8,128)(2,1)}, bf16[64,15488]{1,0:T(8,128)(2,1)}, u32[]{:S(2)}, u32[]{:S(2)}) collective-permute-start(bf16[64,15488]{1,0:T(8,128)(2,1)} %slice.150), channel_id=1, source_target_pairs={{0,1},{1,2},{2,3},{3,4},{4,5},{5,6},{6,7},{7,8},{8,9},{9,10},{10,1... | collective-permute-start | bytes 5947400 | tf_op jit(solution)/shard_map/ppermute | solution.py:16
  66.1 2.2 %slice-start = ((bf16[64,32768]{1,0:T(8,128)(2,1)}), bf16[64,16384]{1,0:T(8,128)(2,1)S(1)}, s32[]{:S(2)}) async-start(bf16[64,32768]{1,0:T(8,128)(2,1)} %w_ref.1), calls=%async_computation | async-start | bytes 4194304 | tf_op jit(solution)/shard_map/slice | solution.py:280
  120.4 2.6 %collective-permute-start.1 = (f32[130,256]{0,1:T(8,128)S(1)}, f32[130,256]{0,1:T(8,128)S(1)}, u32[]{:S(2)}, u32[]{:S(2)}) collective-permute-start(f32[130,256]{0,1:T(8,128)S(1)} %pad_maximum_fusion.1), channel_id=1, source_target_pairs={{0,1},{1,0},{2,3},{3,2},{4,5},{5,4},{6,7},{7,6},{8,9},{9,8},{10,11... | collective-permute-start | bytes 399368 | tf_op jit(solution)/shard_map/ppermute | solution.py:227
  123.1 8.7 %collective-permute-start.2 = (f32[130,256]{0,1:T(8,128)S(1)}, f32[130,256]{0,1:T(8,128)S(1)}, u32[]{:S(2)}, u32[]{:S(2)}) collective-permute-start(f32[130,256]{0,1:T(8,128)S(1)} %fusion.26), channel_id=1, source_target_pairs={{0,2},{1,3},{2,0},{3,1},{4,6},{5,7},{6,4},{7,5},{8,10},{9,11},{10,... | collective-permute-start | bytes 399368 | tf_op jit(solution)/shard_map/ppermute | solution.py:227
  131.8 7.8 %collective-permute-start.3 = (f32[130,256]{0,1:T(8,128)S(1)}, f32[130,256]{0,1:T(8,128)S(1)}, u32[]{:S(2)}, u32[]{:S(2)}) collective-permute-start(f32[130,256]{0,1:T(8,128)S(1)} %add.423), channel_id=1, source_target_pairs={{0,4},{1,5},{2,6},{3,7},{4,0},{5,1},{6,2},{7,3},{8,12},{9,13},{10,... | collective-permute-start | bytes 399368 | tf_op jit(solution)/shard_map/ppermute | solution.py:227
  139.6 6.9 %collective-permute-start.4 = (f32[130,256]{0,1:T(8,128)S(1)}, f32[130,256]{0,1:T(8,128)S(1)}, u32[]{:S(2)}, u32[]{:S(2)}) collective-permute-start(f32[130,256]{0,1:T(8,128)S(1)} %add.424), channel_id=1, source_target_pairs={{0,8},{1,9},{2,10},{3,11},{4,12},{5,13},{6,14},{7,15},{8,0},{9,1},... | collective-permute-start | bytes 399368 | tf_op jit(solution)/shard_map/ppermute | solution.py:227
  146.6 12.6 %collective-permute-start.5 = (f32[130,256]{0,1:T(8,128)S(1)}, f32[130,256]{0,1:T(8,128)S(1)}, u32[]{:S(2)}, u32[]{:S(2)}) collective-permute-start(f32[130,256]{0,1:T(8,128)S(1)} %add.425), channel_id=1, source_target_pairs={{0,16},{1,17},{2,18},{3,19},{4,20},{5,21},{6,22},{7,23},{8,24},{9,... | collective-permute-start | bytes 399368 | tf_op jit(solution)/shard_map/ppermute | solution.py:227
  198.9 4.6 %copy-start.2 = (f32[256]{0:T(256)}, f32[256]{0:T(256)S(1)}, u32[]{:S(2)}) copy-start(f32[256]{0:T(256)S(1)} %slice_reduce_fusion.1) | copy-start | bytes 3076
  203.5 6.0 %copy-start = (bf16[32768]{0:T(1024)(128)(2,1)S(1)}, bf16[32768]{0:T(1024)(128)(2,1)}, u32[]{:S(2)}) copy-start(bf16[32768]{0:T(1024)(128)(2,1)} %param.4) | copy-start | bytes 196612

commit v8 on v5

--- a/solution.py
+++ b/solution.py
@@ -173,22 +173,24 @@
     n = a_ref.shape[0]
     a_ref[...] = system_ref[...]
     x_ref[...] = c_ref[...]
-    lanes = lax.broadcasted_iota(jnp.int32, (1, n), 1)
     sublanes = lax.broadcasted_iota(jnp.int32, (n, 1), 0)
 
-    def step(j, carry):
-        at = lanes == j
-        here = sublanes == j
-        row = a_ref[pl.ds(j, 1), :]
-        pivot = jnp.sum(jnp.where(at, row, 0.0), axis=1, keepdims=True)
-        column = jnp.sum(jnp.where(at, a_ref[...], 0.0), axis=1, keepdims=True)
-        scaled_row = row / pivot
-        scaled_rhs = x_ref[pl.ds(j, 1), :] / pivot
-        a_ref[...] = jnp.where(here, scaled_row, a_ref[...] - column * scaled_row)
-        x_ref[...] = jnp.where(here, scaled_rhs, x_ref[...] - column * scaled_rhs)
-        return carry
-
-    lax.fori_loop(0, n, step, 0)
+    for lo in range(0, n, 128):
+        lanes = lo + lax.broadcasted_iota(jnp.int32, (1, n - lo), 1)
+
+        def step(j, carry, lo=lo, lanes=lanes):
+            at = lanes == j
+            here = sublanes == j
+            row = a_ref[pl.ds(j, 1), :][:, lo:]
+            pivot = jnp.sum(jnp.where(at, row, 0.0), axis=1, keepdims=True)
+            column = jnp.sum(jnp.where(at, a_ref[:, lo:], 0.0), axis=1, keepdims=True)
+            scaled_row = row / pivot
+            scaled_rhs = x_ref[pl.ds(j, 1), :] / pivot
+            a_ref[:, lo:] = jnp.where(here, scaled_row, a_ref[:, lo:] - column * scaled_row)
+            x_ref[...] = jnp.where(here, scaled_rhs, x_ref[...] - column * scaled_rhs)
+            return carry
+
+        lax.fori_loop(lo, min(n, lo + 128), step, 0)
 
 
 def ridge_solve_jordan(system, cross_sum, interpret=False):

time: 208 us -> 206 us (level)
    pallas_call x1, Pallas kernels: 37.7 us -> 35.4 us  [ridge_solve_jordan(): pl.pallas_call(jordan_kernel, in_specs=[pl.BlockSpec(memory_space=pltpu.V...]
  transfers between devices with their start and end apart: 6 -> 6, of which waited for: 5 -> 5; matrix products, arithmetic and copies ran while one was open for 3% -> 3% of each run, Pallas kernels for 23% -> 24%
where the time goes in v8:
time: 206 us
  Pallas kernels  132 us (64%)
  waiting for transfers between devices  29.8 us (14%)
  local copies, waits for them, and re-layouts  14.4 us (7%)
  starting transfers between devices  12.4 us (6%)
  matrix products  9.18 us (4%)
  other arithmetic  6.74 us (3%)
    pallas_call x2, Pallas kernels, features_and_sums(): pl.pallas_call(kernel, grid=(n_blocks,), in_specs=[pl.BlockSpec(memory_sp...  96.8 us
    pallas_call x1, Pallas kernels, ridge_solve_jordan(): pl.pallas_call(jordan_kernel, in_specs=[pl.BlockSpec(memory_space=pltpu.V...  35.4 us
    ppermute x5, waiting for transfers between devices, butterfly_sum(): x = x + lax.ppermute(x, axes, [(i, i ^ step) for i in range(size)])  29.8 us
    dot_general x2, matrix products, local(): jnp.dot(rounded, f, preferred_element_type=jnp.float32)  9.18 us
    ppermute x5, starting transfers between devices, butterfly_sum(): x = x + lax.ppermute(x, axes, [(i, i ^ step) for i in range(size)])  8.73 us
    concatenate x1, local copies, waits for them, and re-layouts, local(): jnp.concatenate([jnp.zeros_like(stream[:, :1]), stream[:, :length - 1]], 1)  5.29 us
    concatenate x1, other arithmetic, local(): jnp.concatenate([previous, stream], 1)[:, :split * block_len + span]  4.81 us
  transfers between devices with their start and end apart: 6, of which 5 were waited for; matrix products, arithmetic and copies ran while one was open for 3% of the time, Pallas kernels for 24%

profile of v8, /device:TPU:0, one launch (start us, length us, event | category | flops | bytes accessed | tf_op | source)
XLA Modules:
  0.0 205.5 jit_solution(3945757089054585637)
XLA Ops:
  0.6 3.4 %slice.33 = bf16[64,15361]{1,0:T(8,128)(2,1)} slice(bf16[64,32768]{1,0:T(8,128)(2,1)} %param.3), slice={[0:64], [17407:32768]} | slice | bytes 3932416 | tf_op jit(solution)/shard_map/slice | solution.py:256
  4.0 3.7 %collective-permute-start = (bf16[64,15361]{1,0:T(8,128)(2,1)}, bf16[64,15361]{1,0:T(8,128)(2,1)}, u32[]{:S(2)}, u32[]{:S(2)}) collective-permute-start(bf16[64,15361]{1,0:T(8,128)(2,1)} %slice.33), channel_id=1, source_target_pairs={{0,1},{1,2},{2,3},{3,4},{4,5},{5,6},{6,7},{7,8},{8,9},{9,10},{10,1... | collective-permute-start | bytes 5898632 | tf_op jit(solution)/shard_map/ppermute | solution.py:16
  7.7 0.9 reshape.14.tgt_ref
  8.7 5.3 %concatenate.32.w_ref = bf16[64,32768]{1,0:T(8,128)(2,1)} pad(bf16[64,32767]{1,0:T(8,128)(2,1)} %bitcast.19, bf16[]{:T(256)} %constant.5.clone.1), padding=0_0x1_0 | pad | bytes 8388482 | tf_op jit(solution)/shard_map/concatenate | solution.py:267
  14.0 0.6 broadcast_in_dim.48.taps_ref
  14.6 48.5 %shard_map.51 = (bf16[256,16384]{1,0:T(8,128)(2,1)}, f32[256,256]{1,0:T(8,128)S(1)}, f32[1,256]{1,0:T(1,128)S(1)}) custom-call(bf16[64,32768]{1,0:T(8,128)(2,1)} %concatenate.32.w_ref, f32[64,64,128]{2,1,0:T(8,128)S(1)} %broadcast_in_dim.48.taps_ref, bf16[1,32768]{1,0:T(2,128)(2,1)S(1)} %reshape.14.tgt_ref), custom_call_target="tpu_custom_call" | custom-call | tf_op jit(solution)/shard_map/pallas_call | solution.py:98
  63.1 0.1 copy.25
  63.2 4.8 %pad_maximum_fusion.w_ref = bf16[64,31744]{1,0:T(8,128)(2,1)} fusion(bf16[64,32768]{1,0:T(8,128)(2,1)} %param.3, bf16[64,15361]{1,0:T(8,128)(2,1)} %collective-permute-done), kind=kLoop, calls=%fused_computation.1 | loop fusion | flops 8126464 | bytes 10223744 | tf_op jit(solution)/shard_map/concatenate | solution.py:262
  68.0 48.3 %shard_map.50 = (bf16[256,16384]{1,0:T(8,128)(2,1)}, f32[256,256]{1,0:T(8,128)S(1)}, f32[1,256]{1,0:T(1,128)S(1)}) custom-call(bf16[64,31744]{1,0:T(8,128)(2,1)} %pad_maximum_fusion.w_ref, f32[64,64,128]{2,1,0:T(8,128)S(1)} %broadcast_in_dim.48.taps_ref, bf16[1,32768]{1,0:T(2,128)(2,1)S(1)} %reshape.14.tgt_ref), custom_call_target="tpu_custom_call" | custom-call | tf_op jit(solution)/shard_map/pallas_call | solution.py:98
  116.3 0.1 copy.24
  116.5 1.3 gather_fusion
  117.8 0.1 copy.27
  118.0 0.1 copy.26
  118.2 1.4 collective-permute-start.1
  119.6 1.2 collective-permute-done.1
  120.9 1.5 collective-permute-start.2
  122.4 7.2 %collective-permute-done.2 = f32[130,256]{0,1:T(8,128)S(1)} collective-permute-done((f32[130,256]{0,1:T(8,128)S(1)}, f32[130,256]{0,1:T(8,128)S(1)}, u32[]{:S(2)}, u32[]{:S(2)}) %collective-permute-start.2) | collective-permute-done | bytes 133152 | tf_op jit(solution)/shard_map/ppermute | solution.py:226
  129.6 1.6 collective-permute-start.3
  131.1 6.2 %collective-permute-done.3 = f32[130,256]{0,1:T(8,128)S(1)} collective-permute-done((f32[130,256]{0,1:T(8,128)S(1)}, f32[130,256]{0,1:T(8,128)S(1)}, u32[]{:S(2)}, u32[]{:S(2)}) %collective-permute-start.3) | collective-permute-done | bytes 133152 | tf_op jit(solution)/shard_map/ppermute | solution.py:226
  137.4 1.6 collective-permute-start.4
  139.0 5.3 %collective-permute-done.4 = f32[130,256]{0,1:T(8,128)S(1)} collective-permute-done((f32[130,256]{0,1:T(8,128)S(1)}, f32[130,256]{0,1:T(8,128)S(1)}, u32[]{:S(2)}, u32[]{:S(2)}) %collective-permute-start.4) | collective-permute-done | bytes 133152 | tf_op jit(solution)/shard_map/ppermute | solution.py:226
  144.4 2.7 %collective-permute-start.5 = (f32[130,256]{0,1:T(8,128)S(1)}, f32[130,256]{0,1:T(8,128)S(1)}, u32[]{:S(2)}, u32[]{:S(2)}) collective-permute-start(f32[130,256]{0,1:T(8,128)S(1)} %add.46), channel_id=1, source_target_pairs={{0,16},{1,17},{2,18},{3,19},{4,20},{5,21},{6,22},{7,23},{8,24},{9,... | collective-permute-start | bytes 399368 | tf_op jit(solution)/shard_map/ppermute | solution.py:226
  147.0 9.9 %collective-permute-done.5 = f32[130,256]{0,1:T(8,128)S(1)} collective-permute-done((f32[130,256]{0,1:T(8,128)S(1)}, f32[130,256]{0,1:T(8,128)S(1)}, u32[]{:S(2)}, u32[]{:S(2)}) %collective-permute-start.5) | collective-permute-done | bytes 133152 | tf_op jit(solution)/shard_map/ppermute | solution.py:226
  157.0 0.2 slice_reduce_fusion.2
  157.2 0.1 slice_reduce_fusion.1
  157.8 0.7 maximum_add_fusion.system_ref
  158.5 0.8 broadcast_in_dim.53.c_ref
  159.2 35.4 %shard_map.52 = f32[256,128]{1,0:T(8,128)} custom-call(f32[256,256]{1,0:T(8,128)} %maximum_add_fusion.system_ref, f32[256,128]{1,0:T(8,128)} %broadcast_in_dim.53.c_ref), custom_call_target="tpu_custom_call" | custom-call | tf_op jit(solution)/shard_map/pallas_call | solution.py:199
  194.6 1.0 slice_reduce_fusion
  195.7 4.6 %fusion.3 = f32[1,16384]{1,0:T(1,128)S(1)} fusion(bf16[256,1]{0,1:T(2,128)(2,1)S(1)} %reshape.21, bf16[256,16384]{1,0:T(8,128)(2,1)} %get-tuple-element.13), kind=kOutput, calls=%fused_computation.22 | convolution fusion | flops 8388608 | bytes 8454656 | tf_op jit(solution)/shard_map/dot_general | solution.py:281
  200.3 4.6 %fusion.2 = f32[1,16384]{1,0:T(1,128)S(1)} fusion(bf16[256,1]{0,1:T(2,128)(2,1)S(1)} %reshape.21, bf16[256,16384]{1,0:T(8,128)(2,1)} %get-tuple-element.12), kind=kOutput, calls=%fused_computation.21 | convolution fusion | flops 8388608 | bytes 8454656 | tf_op jit(solution)/shard_map/dot_general | solution.py:281
  204.9 0.7 maximum_subtract_fusion
  (28 shorter events, 0.8 us)
Async XLA Ops:
  0.6 13.3 %copy-start.1 = (f32[4,16,64]{2,1,0:T(8,128)S(1)}, f32[4,16,64]{2,1,0:T(8,128)}, u32[]{:S(2)}) copy-start(f32[4,16,64]{2,1,0:T(8,128)} %param.5) | copy-start | bytes 49156
  4.0 59.2 %collective-permute-start = (bf16[64,15361]{1,0:T(8,128)(2,1)}, bf16[64,15361]{1,0:T(8,128)(2,1)}, u32[]{:S(2)}, u32[]{:S(2)}) collective-permute-start(bf16[64,15361]{1,0:T(8,128)(2,1)} %slice.33), channel_id=1, source_target_pairs={{0,1},{1,2},{2,3},{3,4},{4,5},{5,6},{6,7},{7,8},{8,9},{9,10},{10,1... | collective-permute-start | bytes 5898632 | tf_op jit(solution)/shard_map/ppermute | solution.py:16
  118.2 2.5 %collective-permute-start.1 = (f32[130,256]{0,1:T(8,128)S(1)}, f32[130,256]{0,1:T(8,128)S(1)}, u32[]{:S(2)}, u32[]{:S(2)}) collective-permute-start(f32[130,256]{0,1:T(8,128)S(1)} %pad_maximum_fusion.1), channel_id=1, source_target_pairs={{0,1},{1,0},{2,3},{3,2},{4,5},{5,4},{6,7},{7,6},{8,9},{9,8},{10,11... | collective-permute-start | bytes 399368 | tf_op jit(solution)/shard_map/ppermute | solution.py:226
  120.9 8.7 %collective-permute-start.2 = (f32[130,256]{0,1:T(8,128)S(1)}, f32[130,256]{0,1:T(8,128)S(1)}, u32[]{:S(2)}, u32[]{:S(2)}) collective-permute-start(f32[130,256]{0,1:T(8,128)S(1)} %fusion.8), channel_id=1, source_target_pairs={{0,2},{1,3},{2,0},{3,1},{4,6},{5,7},{6,4},{7,5},{8,10},{9,11},{10,... | collective-permute-start | bytes 399368 | tf_op jit(solution)/shard_map/ppermute | solution.py:226
  129.6 7.8 %collective-permute-start.3 = (f32[130,256]{0,1:T(8,128)S(1)}, f32[130,256]{0,1:T(8,128)S(1)}, u32[]{:S(2)}, u32[]{:S(2)}) collective-permute-start(f32[130,256]{0,1:T(8,128)S(1)} %add.44), channel_id=1, source_target_pairs={{0,4},{1,5},{2,6},{3,7},{4,0},{5,1},{6,2},{7,3},{8,12},{9,13},{10,... | collective-permute-start | bytes 399368 | tf_op jit(solution)/shard_map/ppermute | solution.py:226
  137.4 6.9 %collective-permute-start.4 = (f32[130,256]{0,1:T(8,128)S(1)}, f32[130,256]{0,1:T(8,128)S(1)}, u32[]{:S(2)}, u32[]{:S(2)}) collective-permute-start(f32[130,256]{0,1:T(8,128)S(1)} %add.45), channel_id=1, source_target_pairs={{0,8},{1,9},{2,10},{3,11},{4,12},{5,13},{6,14},{7,15},{8,0},{9,1},... | collective-permute-start | bytes 399368 | tf_op jit(solution)/shard_map/ppermute | solution.py:226
  144.4 12.6 %collective-permute-start.5 = (f32[130,256]{0,1:T(8,128)S(1)}, f32[130,256]{0,1:T(8,128)S(1)}, u32[]{:S(2)}, u32[]{:S(2)}) collective-permute-start(f32[130,256]{0,1:T(8,128)S(1)} %add.46), channel_id=1, source_target_pairs={{0,16},{1,17},{2,18},{3,19},{4,20},{5,21},{6,22},{7,23},{8,24},{9,... | collective-permute-start | bytes 399368 | tf_op jit(solution)/shard_map/ppermute | solution.py:226
  195.6 9.2 %copy-start.2 = (f32[256]{0:T(256)}, f32[256]{0:T(256)S(1)}, u32[]{:S(2)}) copy-start(f32[256]{0:T(256)S(1)} %slice_reduce_fusion) | copy-start | bytes 3076
  195.7 9.2 %copy-start = (bf16[32768]{0:T(1024)(128)(2,1)S(1)}, bf16[32768]{0:T(1024)(128)(2,1)}, u32[]{:S(2)}) copy-start(bf16[32768]{0:T(1024)(128)(2,1)} %param.4) | copy-start | bytes 196612

commit v9 on v8

--- a/solution.py
+++ b/solution.py
@@ -169,10 +169,20 @@
     )(system, cross_sum.reshape(1, n))[0]
 
 
-def jordan_kernel(system_ref, c_ref, x_ref, a_ref):
+def jordan_kernel(ridge, packed_ref, x_ref, a_ref):
     n = a_ref.shape[0]
-    a_ref[...] = system_ref[...]
-    x_ref[...] = c_ref[...]
+    h = n // 2
+    rows = lax.broadcasted_iota(jnp.int32, (h, h), 0)
+    cols = lax.broadcasted_iota(jnp.int32, (h, h), 1)
+    folded = packed_ref[:h, :h]
+    flipped = jnp.transpose(folded)
+    off = packed_ref[:h, h:]
+    trail_diag = packed_ref[h + 1 : h + 2, :h]
+    a_ref[:h, :h] = jnp.where(rows <= cols, folded, flipped) + jnp.where(rows == cols, ridge, 0.0)
+    a_ref[:h, h:] = off
+    a_ref[h:, :h] = jnp.transpose(off)
+    a_ref[h:, h:] = jnp.where(rows > cols, folded, jnp.where(rows < cols, flipped, trail_diag + ridge))
+    x_ref[...] = jnp.transpose(jnp.broadcast_to(packed_ref[h : h + 1, :], (128, n)))
     sublanes = lax.broadcasted_iota(jnp.int32, (n, 1), 0)
 
     for lo in range(0, n, 128):
@@ -193,17 +203,16 @@
         lax.fori_loop(lo, min(n, lo + 128), step, 0)
 
 
-def ridge_solve_jordan(system, cross_sum, interpret=False):
-    n = system.shape[0]
-    rhs = jnp.broadcast_to(cross_sum[:, None], (n, 128))
+def ridge_solve_packed(packed, ridge, interpret=False):
+    n = packed.shape[1]
     return pl.pallas_call(
-        jordan_kernel,
-        in_specs=[pl.BlockSpec(memory_space=pltpu.VMEM), pl.BlockSpec(memory_space=pltpu.VMEM)],
+        functools.partial(jordan_kernel, ridge),
+        in_specs=[pl.BlockSpec(memory_space=pltpu.VMEM)],
         out_specs=pl.BlockSpec(memory_space=pltpu.VMEM),
         out_shape=jax.ShapeDtypeStruct((n, 128), jnp.float32),
         scratch_shapes=[pltpu.VMEM((n, n), jnp.float32)],
         interpret=interpret,
-    )(system, rhs)[:, 0]
+    )(packed)[:, 0]
 
 
 def ridge_solve(system, cross_sum):
@@ -237,16 +246,7 @@
     folded = jnp.where(rows <= cols, lead, trail)
     extra = jnp.stack([cross_sum, jnp.concatenate([jnp.diagonal(trail), jnp.zeros((n - h,), jnp.float32)])])
     packed = jnp.concatenate([jnp.concatenate([folded, off], 1), extra], 0)
-    packed = butterfly_sum(packed, axes)
-    folded, off = packed[:h, :h], packed[:h, h:]
-    upper = jnp.where(rows <= cols, folded, 0.0)
-    lead = upper + jnp.where(rows < cols, folded, 0.0).T
-    strict = jnp.where(rows > cols, folded, 0.0)
-    trail = strict + strict.T + jnp.diag(packed[h + 1, :h])
-    gram_sum = jnp.concatenate(
-        [jnp.concatenate([lead, off], 1), jnp.concatenate([off.T, trail], 1)], 0
-    )
-    return gram_sum, packed[h]
+    return butterfly_sum(packed, axes)
 
 
 def local(stream, target, depthwise_taps):
@@ -273,10 +273,9 @@
     else:
         features = (features,)
     cross_sum = cross_sum[0]
-    gram_sum, cross_sum = reduce_system(gram_sum, cross_sum, ("wide", "narrow"))
+    packed = reduce_system(gram_sum, cross_sum, ("wide", "narrow"))
     total_rows = length * lax.axis_size("wide") * lax.axis_size("narrow")
-    system = gram_sum + ridge_share * total_rows * jnp.eye(gram_sum.shape[0], dtype=jnp.float32)
-    coefficients = ridge_solve_jordan(system, cross_sum)
+    coefficients = ridge_solve_packed(packed, ridge_share * total_rows)
     rounded = coefficients.astype(jnp.bfloat16)
     fitted = jnp.concatenate([jnp.dot(rounded, f, preferred_element_type=jnp.float32) for f in features])
     return (coefficients, target.astype(jnp.float32) - fitted)

time: 206 us -> 184 us (0.89)
  waiting for transfers between devices: 29.8 us -> 17.4 us
  local copies, waits for them, and re-layouts: 14.4 us -> 11.5 us
  matrix products: 9.18 us -> 6.29 us
  other arithmetic: 6.74 us -> 4.15 us
    ppermute x5, waiting for transfers between devices: 29.8 us -> 17.4 us  [butterfly_sum(): x = x + lax.ppermute(x, axes, [(i, i ^ step) for i in range(size)])]
    dot_general x2, matrix products: 9.18 us -> 6.29 us  [local(): jnp.dot(rounded, f, preferred_element_type=jnp.float32)]
    concatenate x1, other arithmetic: 4.81 us -> 2.63 us  [local(): jnp.concatenate([previous, stream], 1)[:, :split * block_len + span]]
  transfers between devices with their start and end apart: 6 -> 6, of which waited for: 5 -> 5; matrix products, arithmetic and copies ran while one was open for 3% -> 4% of each run, Pallas kernels for 24% -> 26%
where the time goes in v9:
time: 184 us
  Pallas kernels  131 us (71%)
  waiting for transfers between devices  17.4 us (9%)
  starting transfers between devices  12.4 us (7%)
  local copies, waits for them, and re-layouts  11.5 us (6%)
  matrix products  6.29 us (3%)
  other arithmetic  4.15 us (2%)
    pallas_call x2, Pallas kernels, features_and_sums(): pl.pallas_call(kernel, grid=(n_blocks,), in_specs=[pl.BlockSpec(memory_sp...  95.9 us
    pallas_call x1, Pallas kernels, ridge_solve_packed(): pl.pallas_call(functools.partial(jordan_kernel, ridge), in_specs=[pl.Bloc...  35.4 us
    ppermute x5, waiting for transfers between devices, butterfly_sum(): x = x + lax.ppermute(x, axes, [(i, i ^ step) for i in range(size)])  17.4 us
    ppermute x5, starting transfers between devices, butterfly_sum(): x = x + lax.ppermute(x, axes, [(i, i ^ step) for i in range(size)])  9.91 us
    dot_general x2, matrix products, local(): jnp.dot(rounded, f, preferred_element_type=jnp.float32)  6.29 us
    concatenate x1, local copies, waits for them, and re-layouts, local(): jnp.concatenate([jnp.zeros_like(stream[:, :1]), stream[:, :length - 1]], 1)  5.46 us
  transfers between devices with their start and end apart: 6, of which 5 were waited for; matrix products, arithmetic and copies ran while one was open for 4% of the time, Pallas kernels for 26%

profile of v9, /device:TPU:0, one launch (start us, length us, event | category | flops | bytes accessed | tf_op | source)
XLA Modules:
  0.0 183.9 jit_solution(1334457268243619654)
XLA Ops:
  0.6 0.0 copy-start.3
  0.6 2.1 %slice.21 = bf16[64,15361]{1,0:T(8,128)(2,1)S(1)} slice(bf16[64,32768]{1,0:T(8,128)(2,1)} %param.3), slice={[0:64], [17407:32768]} | slice | bytes 3932416 | tf_op jit(solution)/shard_map/slice | solution.py:256
  2.8 2.5 %collective-permute-start = (bf16[64,15361]{1,0:T(8,128)(2,1)S(1)}, bf16[64,15361]{1,0:T(8,128)(2,1)S(1)}, u32[]{:S(2)}, u32[]{:S(2)}) collective-permute-start(bf16[64,15361]{1,0:T(8,128)(2,1)S(1)} %slice.21), channel_id=1, source_target_pairs={{0,1},{1,2},{2,3},{3,4},{4,5},{5,6},{6,7},{7,8},{8,9},{9,10},{10,1... | collective-permute-start | bytes 5898632 | tf_op jit(solution)/shard_map/ppermute | solution.py:16
  5.3 0.9 reshape.9.tgt_ref
  6.2 0.0 copy-start
  6.2 5.5 %concatenate.23.w_ref = bf16[64,32768]{1,0:T(8,128)(2,1)} pad(bf16[64,32767]{1,0:T(8,128)(2,1)} %bitcast.11, bf16[]{:T(256)} %constant.3.clone.1), padding=0_0x1_0 | pad | bytes 8388482 | tf_op jit(solution)/shard_map/concatenate | solution.py:267
  11.7 0.6 broadcast_in_dim.7.taps_ref
  12.3 48.0 %shard_map.51 = (bf16[256,16384]{1,0:T(8,128)(2,1)}, f32[256,256]{1,0:T(8,128)S(1)}, f32[1,256]{1,0:T(1,128)S(1)}) custom-call(bf16[64,32768]{1,0:T(8,128)(2,1)} %concatenate.23.w_ref, f32[64,64,128]{2,1,0:T(8,128)S(1)} %broadcast_in_dim.7.taps_ref, bf16[1,32768]{1,0:T(2,128)(2,1)S(1)} %reshape.9.tgt_ref), custom_call_target="tpu_custom_call" | custom-call | tf_op jit(solution)/shard_map/pallas_call | solution.py:98
  60.3 0.0 collective-permute-done
  60.3 2.6 %pad_maximum_fusion.w_ref = bf16[64,31744]{1,0:T(8,128)(2,1)} fusion(bf16[64,32768]{1,0:T(8,128)(2,1)S(1)} %copy-done, bf16[64,15361]{1,0:T(8,128)(2,1)S(1)} %collective-permute-done), kind=kLoop, calls=%fused_computation.1 | loop fusion | flops 8126464 | bytes 10223744 | tf_op jit(solution)/shard_map/concatenate | solution.py:262
  62.9 47.9 %shard_map.50 = (bf16[256,16384]{1,0:T(8,128)(2,1)}, f32[256,256]{1,0:T(8,128)S(1)}, f32[1,256]{1,0:T(1,128)S(1)}) custom-call(bf16[64,31744]{1,0:T(8,128)(2,1)} %pad_maximum_fusion.w_ref, f32[64,64,128]{2,1,0:T(8,128)S(1)} %broadcast_in_dim.7.taps_ref, bf16[1,32768]{1,0:T(2,128)(2,1)S(1)} %reshape.9.tgt_ref), custom_call_target="tpu_custom_call" | custom-call | tf_op jit(solution)/shard_map/pallas_call | solution.py:98
  110.9 1.2 gather_fusion
  112.2 2.6 %collective-permute-start.1 = (f32[130,256]{1,0:T(8,128)S(1)}, f32[130,256]{1,0:T(8,128)S(1)}, u32[]{:S(2)}, u32[]{:S(2)}) collective-permute-start(f32[130,256]{1,0:T(8,128)S(1)} %pad_maximum_fusion.1), channel_id=1, source_target_pairs={{0,1},{1,0},{2,3},{3,2},{4,5},{5,4},{6,7},{7,6},{8,9},{9,8},{10,11... | collective-permute-start | bytes 399368 | tf_op jit(solution)/shard_map/ppermute | solution.py:235
  114.7 1.0 collective-permute-done.1
  115.8 1.5 collective-permute-start.2
  117.3 4.5 %collective-permute-done.2 = f32[130,256]{1,0:T(8,128)S(1)} collective-permute-done((f32[130,256]{1,0:T(8,128)S(1)}, f32[130,256]{1,0:T(8,128)S(1)}, u32[]{:S(2)}, u32[]{:S(2)}) %collective-permute-start.2) | collective-permute-done | bytes 133152 | tf_op jit(solution)/shard_map/ppermute | solution.py:235
  121.8 1.6 collective-permute-start.3
  123.4 3.6 %collective-permute-done.3 = f32[130,256]{1,0:T(8,128)S(1)} collective-permute-done((f32[130,256]{1,0:T(8,128)S(1)}, f32[130,256]{1,0:T(8,128)S(1)}, u32[]{:S(2)}, u32[]{:S(2)}) %collective-permute-start.3) | collective-permute-done | bytes 133152 | tf_op jit(solution)/shard_map/ppermute | solution.py:235
  127.0 1.6 collective-permute-start.4
  128.6 3.5 %collective-permute-done.4 = f32[130,256]{1,0:T(8,128)S(1)} collective-permute-done((f32[130,256]{1,0:T(8,128)S(1)}, f32[130,256]{1,0:T(8,128)S(1)}, u32[]{:S(2)}, u32[]{:S(2)}) %collective-permute-start.4) | collective-permute-done | bytes 133152 | tf_op jit(solution)/shard_map/ppermute | solution.py:235
  132.1 2.7 %collective-permute-start.5 = (f32[130,256]{1,0:T(8,128)S(1)}, f32[130,256]{1,0:T(8,128)S(1)}, u32[]{:S(2)}, u32[]{:S(2)}) collective-permute-start(f32[130,256]{1,0:T(8,128)S(1)} %add.34), channel_id=1, source_target_pairs={{0,16},{1,17},{2,18},{3,19},{4,20},{5,21},{6,22},{7,23},{8,24},{9,... | collective-permute-start | bytes 399368 | tf_op jit(solution)/shard_map/ppermute | solution.py:235
  134.8 4.9 %collective-permute-done.5 = f32[130,256]{1,0:T(8,128)S(1)} collective-permute-done((f32[130,256]{1,0:T(8,128)S(1)}, f32[130,256]{1,0:T(8,128)S(1)}, u32[]{:S(2)}, u32[]{:S(2)}) %collective-permute-start.5) | collective-permute-done | bytes 133152 | tf_op jit(solution)/shard_map/ppermute | solution.py:235
  139.6 0.7 add.35.packed_ref
  140.3 35.4 %shard_map.52 = f32[256,128]{1,0:T(8,128)} custom-call(f32[130,256]{1,0:T(8,128)} %add.35.packed_ref), custom_call_target="tpu_custom_call" | custom-call | tf_op jit(solution)/shard_map/pallas_call | solution.py:208
  175.7 1.2 slice_reduce_fusion
  176.9 0.0 copy-start.4
  176.9 0.0 copy-start.2
  176.9 5.1 %fusion.2 = f32[1,16384]{1,0:T(1,128)S(1)} fusion(bf16[256,1]{0,1:T(2,128)(2,1)S(1)} %reshape.18, bf16[256,16384]{1,0:T(8,128)(2,1)} %get-tuple-element.13), kind=kOutput, calls=%fused_computation.10 | convolution fusion | flops 8388608 | bytes 8454656 | tf_op jit(solution)/shard_map/dot_general | solution.py:280
  182.0 0.0 copy-done.1
  182.0 1.2 fusion.1
  183.2 0.0 copy-done.4
  183.2 0.7 maximum_subtract_fusion
  (16 shorter events, 0.2 us)
Async XLA Ops:
  0.6 11.1 %copy-start.3 = (f32[4,16,64]{2,1,0:T(8,128)S(1)}, f32[4,16,64]{2,1,0:T(8,128)}, u32[]{:S(2)}) copy-start(f32[4,16,64]{2,1,0:T(8,128)} %param.5) | copy-start | bytes 49156
  2.8 57.5 %collective-permute-start = (bf16[64,15361]{1,0:T(8,128)(2,1)S(1)}, bf16[64,15361]{1,0:T(8,128)(2,1)S(1)}, u32[]{:S(2)}, u32[]{:S(2)}) collective-permute-start(bf16[64,15361]{1,0:T(8,128)(2,1)S(1)} %slice.21), channel_id=1, source_target_pairs={{0,1},{1,2},{2,3},{3,4},{4,5},{5,6},{6,7},{7,8},{8,9},{9,10},{10,1... | collective-permute-start | bytes 5898632 | tf_op jit(solution)/shard_map/ppermute | solution.py:16
  6.2 54.1 %copy-start = (bf16[64,32768]{1,0:T(8,128)(2,1)S(1)}, bf16[64,32768]{1,0:T(8,128)(2,1)}, u32[]{:S(2)}) copy-start(bf16[64,32768]{1,0:T(8,128)(2,1)} %param.3) | copy-start | bytes 12582916
  112.2 3.6 %collective-permute-start.1 = (f32[130,256]{1,0:T(8,128)S(1)}, f32[130,256]{1,0:T(8,128)S(1)}, u32[]{:S(2)}, u32[]{:S(2)}) collective-permute-start(f32[130,256]{1,0:T(8,128)S(1)} %pad_maximum_fusion.1), channel_id=1, source_target_pairs={{0,1},{1,0},{2,3},{3,2},{4,5},{5,4},{6,7},{7,6},{8,9},{9,8},{10,11... | collective-permute-start | bytes 399368 | tf_op jit(solution)/shard_map/ppermute | solution.py:235
  115.8 6.0 %collective-permute-start.2 = (f32[130,256]{1,0:T(8,128)S(1)}, f32[130,256]{1,0:T(8,128)S(1)}, u32[]{:S(2)}, u32[]{:S(2)}) collective-permute-start(f32[130,256]{1,0:T(8,128)S(1)} %fusion), channel_id=1, source_target_pairs={{0,2},{1,3},{2,0},{3,1},{4,6},{5,7},{6,4},{7,5},{8,10},{9,11},{10,... | collective-permute-start | bytes 399368 | tf_op jit(solution)/shard_map/ppermute | solution.py:235
  121.8 5.1 %collective-permute-start.3 = (f32[130,256]{1,0:T(8,128)S(1)}, f32[130,256]{1,0:T(8,128)S(1)}, u32[]{:S(2)}, u32[]{:S(2)}) collective-permute-start(f32[130,256]{1,0:T(8,128)S(1)} %add.32), channel_id=1, source_target_pairs={{0,4},{1,5},{2,6},{3,7},{4,0},{5,1},{6,2},{7,3},{8,12},{9,13},{10,... | collective-permute-start | bytes 399368 | tf_op jit(solution)/shard_map/ppermute | solution.py:235
  127.0 5.1 %collective-permute-start.4 = (f32[130,256]{1,0:T(8,128)S(1)}, f32[130,256]{1,0:T(8,128)S(1)}, u32[]{:S(2)}, u32[]{:S(2)}) collective-permute-start(f32[130,256]{1,0:T(8,128)S(1)} %add.33), channel_id=1, source_target_pairs={{0,8},{1,9},{2,10},{3,11},{4,12},{5,13},{6,14},{7,15},{8,0},{9,1},... | collective-permute-start | bytes 399368 | tf_op jit(solution)/shard_map/ppermute | solution.py:235
  132.1 7.5 %collective-permute-start.5 = (f32[130,256]{1,0:T(8,128)S(1)}, f32[130,256]{1,0:T(8,128)S(1)}, u32[]{:S(2)}, u32[]{:S(2)}) collective-permute-start(f32[130,256]{1,0:T(8,128)S(1)} %add.34), channel_id=1, source_target_pairs={{0,16},{1,17},{2,18},{3,19},{4,20},{5,21},{6,22},{7,23},{8,24},{9,... | collective-permute-start | bytes 399368 | tf_op jit(solution)/shard_map/ppermute | solution.py:235
  175.7 6.3 %copy-start.1 = (bf16[256,16384]{1,0:T(8,128)(2,1)S(1)}, bf16[256,16384]{1,0:T(8,128)(2,1)}, u32[]{:S(2)}) copy-start(bf16[256,16384]{1,0:T(8,128)(2,1)} %get-tuple-element.12) | copy-start | bytes 25165828
  176.9 6.3 %copy-start.4 = (f32[256]{0:T(256)}, f32[256]{0:T(256)S(1)}, u32[]{:S(2)}) copy-start(f32[256]{0:T(256)S(1)} %slice_reduce_fusion) | copy-start | bytes 3076
  176.9 6.3 %copy-start.2 = (bf16[32768]{0:T(1024)(128)(2,1)S(1)}, bf16[32768]{0:T(1024)(128)(2,1)}, u32[]{:S(2)}) copy-start(bf16[32768]{0:T(1024)(128)(2,1)} %param.4) | copy-start | bytes 196612

commit v10 on v9

--- a/solution.py
+++ b/solution.py
@@ -188,19 +188,40 @@
     for lo in range(0, n, 128):
         lanes = lo + lax.broadcasted_iota(jnp.int32, (1, n - lo), 1)
 
-        def step(j, carry, lo=lo, lanes=lanes):
-            at = lanes == j
-            here = sublanes == j
-            row = a_ref[pl.ds(j, 1), :][:, lo:]
-            pivot = jnp.sum(jnp.where(at, row, 0.0), axis=1, keepdims=True)
-            column = jnp.sum(jnp.where(at, a_ref[:, lo:], 0.0), axis=1, keepdims=True)
-            scaled_row = row / pivot
-            scaled_rhs = x_ref[pl.ds(j, 1), :] / pivot
-            a_ref[:, lo:] = jnp.where(here, scaled_row, a_ref[:, lo:] - column * scaled_row)
-            x_ref[...] = jnp.where(here, scaled_rhs, x_ref[...] - column * scaled_rhs)
+        def pick(vec, at):
+            return jnp.sum(jnp.where(at, vec, 0.0), axis=1, keepdims=True)
+
+        def step(p, carry, lo=lo, lanes=lanes):
+            j = 2 * p
+            at0, at1 = lanes == j, lanes == j + 1
+            here0, here1 = sublanes == j, sublanes == j + 1
+            block = a_ref[:, lo:]
+            row0 = a_ref[pl.ds(j, 1), :][:, lo:]
+            row1 = a_ref[pl.ds(j + 1, 1), :][:, lo:]
+            col0 = jnp.sum(jnp.where(at0, block, 0.0), axis=1, keepdims=True)
+            col1 = jnp.sum(jnp.where(at1, block, 0.0), axis=1, keepdims=True)
+            rhs0 = x_ref[pl.ds(j, 1), :]
+            rhs1 = x_ref[pl.ds(j + 1, 1), :]
+            pivot0 = pick(row0, at0)
+            srow0 = row0 / pivot0
+            srhs0 = rhs0 / pivot0
+            lower = pick(row1, at0)
+            row1 = row1 - lower * srow0
+            rhs1 = rhs1 - lower * srhs0
+            upper = pick(srow0, at1)
+            col1 = jnp.where(here0, upper, col1 - col0 * upper)
+            pivot1 = pick(row1, at1)
+            srow1 = row1 / pivot1
+            srhs1 = rhs1 / pivot1
+            rest = block - col0 * srow0 - col1 * srow1
+            done0 = srow0 - upper * srow1
+            a_ref[:, lo:] = jnp.where(here1, srow1, jnp.where(here0, done0, rest))
+            x = x_ref[...]
+            x_rest = x - col0 * srhs0 - col1 * srhs1
+            x_ref[...] = jnp.where(here1, srhs1, jnp.where(here0, srhs0 - upper * srhs1, x_rest))
             return carry
 
-        lax.fori_loop(lo, min(n, lo + 128), step, 0)
+        lax.fori_loop(lo // 2, min(n, lo + 128) // 2, step, 0)
 
 
 def ridge_solve_packed(packed, ridge, interpret=False):

time: 184 us -> 187 us (1.016)
  Pallas kernels: 131 us -> 134 us
    pallas_call x1, Pallas kernels: 35.4 us -> 38 us  [ridge_solve_packed(): pl.pallas_call(functools.partial(jordan_kernel, ridge), in_specs=[pl.Bloc...]
where the time goes in v10:
time: 187 us
  Pallas kernels  134 us (72%)
  waiting for transfers between devices  17.4 us (9%)
  starting transfers between devices  12.4 us (7%)
  local copies, waits for them, and re-layouts  11.5 us (6%)
  matrix products  6.29 us (3%)
  other arithmetic  4.15 us (2%)
    pallas_call x2, Pallas kernels, features_and_sums(): pl.pallas_call(kernel, grid=(n_blocks,), in_specs=[pl.BlockSpec(memory_sp...  95.9 us
    pallas_call x1, Pallas kernels, ridge_solve_packed(): pl.pallas_call(functools.partial(jordan_kernel, ridge), in_specs=[pl.Bloc...  38 us
    ppermute x5, waiting for transfers between devices, butterfly_sum(): x = x + lax.ppermute(x, axes, [(i, i ^ step) for i in range(size)])  17.4 us
    ppermute x5, starting transfers between devices, butterfly_sum(): x = x + lax.ppermute(x, axes, [(i, i ^ step) for i in range(size)])  9.91 us
    dot_general x2, matrix products, local(): jnp.dot(rounded, f, preferred_element_type=jnp.float32)  6.29 us
    concatenate x1, local copies, waits for them, and re-layouts, local(): jnp.concatenate([jnp.zeros_like(stream[:, :1]), stream[:, :length - 1]], 1)  5.46 us
  transfers between devices with their start and end apart: 6, of which 5 were waited for; matrix products, arithmetic and copies ran while one was open for 4% of the time, Pallas kernels for 26%

profile of v10, /device:TPU:0, one launch (start us, length us, event | category | flops | bytes accessed | tf_op | source)
XLA Modules:
  0.0 186.5 jit_solution(17543364269692220848)
XLA Ops:
  0.6 0.0 copy-start.3
  0.6 2.1 %slice.21 = bf16[64,15361]{1,0:T(8,128)(2,1)S(1)} slice(bf16[64,32768]{1,0:T(8,128)(2,1)} %param.3), slice={[0:64], [17407:32768]} | slice | bytes 3932416 | tf_op jit(solution)/shard_map/slice | solution.py:277
  2.8 2.5 %collective-permute-start = (bf16[64,15361]{1,0:T(8,128)(2,1)S(1)}, bf16[64,15361]{1,0:T(8,128)(2,1)S(1)}, u32[]{:S(2)}, u32[]{:S(2)}) collective-permute-start(bf16[64,15361]{1,0:T(8,128)(2,1)S(1)} %slice.21), channel_id=1, source_target_pairs={{0,1},{1,2},{2,3},{3,4},{4,5},{5,6},{6,7},{7,8},{8,9},{9,10},{10,1... | collective-permute-start | bytes 5898632 | tf_op jit(solution)/shard_map/ppermute | solution.py:16
  5.3 0.9 reshape.9.tgt_ref
  6.2 0.0 copy-start
  6.2 5.5 %concatenate.23.w_ref = bf16[64,32768]{1,0:T(8,128)(2,1)} pad(bf16[64,32767]{1,0:T(8,128)(2,1)} %bitcast.11, bf16[]{:T(256)} %constant.3.clone.1), padding=0_0x1_0 | pad | bytes 8388482 | tf_op jit(solution)/shard_map/concatenate | solution.py:288
  11.7 0.0 copy-done.3
  11.7 0.6 broadcast_in_dim.7.taps_ref
  12.3 48.0 %shard_map.51 = (bf16[256,16384]{1,0:T(8,128)(2,1)}, f32[256,256]{1,0:T(8,128)S(1)}, f32[1,256]{1,0:T(1,128)S(1)}) custom-call(bf16[64,32768]{1,0:T(8,128)(2,1)} %concatenate.23.w_ref, f32[64,64,128]{2,1,0:T(8,128)S(1)} %broadcast_in_dim.7.taps_ref, bf16[1,32768]{1,0:T(2,128)(2,1)S(1)} %reshape.9.tgt_ref), custom_call_target="tpu_custom_call" | custom-call | tf_op jit(solution)/shard_map/pallas_call | solution.py:98
  60.3 0.0 collective-permute-done
  60.3 2.6 %pad_maximum_fusion.w_ref = bf16[64,31744]{1,0:T(8,128)(2,1)} fusion(bf16[64,32768]{1,0:T(8,128)(2,1)S(1)} %copy-done, bf16[64,15361]{1,0:T(8,128)(2,1)S(1)} %collective-permute-done), kind=kLoop, calls=%fused_computation.1 | loop fusion | flops 8126464 | bytes 10223744 | tf_op jit(solution)/shard_map/concatenate | solution.py:283
  62.9 47.9 %shard_map.50 = (bf16[256,16384]{1,0:T(8,128)(2,1)}, f32[256,256]{1,0:T(8,128)S(1)}, f32[1,256]{1,0:T(1,128)S(1)}) custom-call(bf16[64,31744]{1,0:T(8,128)(2,1)} %pad_maximum_fusion.w_ref, f32[64,64,128]{2,1,0:T(8,128)S(1)} %broadcast_in_dim.7.taps_ref, bf16[1,32768]{1,0:T(2,128)(2,1)S(1)} %reshape.9.tgt_ref), custom_call_target="tpu_custom_call" | custom-call | tf_op jit(solution)/shard_map/pallas_call | solution.py:98
  110.9 1.2 gather_fusion
  112.2 2.6 %collective-permute-start.1 = (f32[130,256]{1,0:T(8,128)S(1)}, f32[130,256]{1,0:T(8,128)S(1)}, u32[]{:S(2)}, u32[]{:S(2)}) collective-permute-start(f32[130,256]{1,0:T(8,128)S(1)} %pad_maximum_fusion.1), channel_id=1, source_target_pairs={{0,1},{1,0},{2,3},{3,2},{4,5},{5,4},{6,7},{7,6},{8,9},{9,8},{10,11... | collective-permute-start | bytes 399368 | tf_op jit(solution)/shard_map/ppermute | solution.py:256
  114.7 1.0 collective-permute-done.1
  115.8 1.5 collective-permute-start.2
  117.3 4.5 %collective-permute-done.2 = f32[130,256]{1,0:T(8,128)S(1)} collective-permute-done((f32[130,256]{1,0:T(8,128)S(1)}, f32[130,256]{1,0:T(8,128)S(1)}, u32[]{:S(2)}, u32[]{:S(2)}) %collective-permute-start.2) | collective-permute-done | bytes 133152 | tf_op jit(solution)/shard_map/ppermute | solution.py:256
  121.8 1.6 collective-permute-start.3
  123.4 3.6 %collective-permute-done.3 = f32[130,256]{1,0:T(8,128)S(1)} collective-permute-done((f32[130,256]{1,0:T(8,128)S(1)}, f32[130,256]{1,0:T(8,128)S(1)}, u32[]{:S(2)}, u32[]{:S(2)}) %collective-permute-start.3) | collective-permute-done | bytes 133152 | tf_op jit(solution)/shard_map/ppermute | solution.py:256
  127.0 1.6 collective-permute-start.4
  128.6 3.5 %collective-permute-done.4 = f32[130,256]{1,0:T(8,128)S(1)} collective-permute-done((f32[130,256]{1,0:T(8,128)S(1)}, f32[130,256]{1,0:T(8,128)S(1)}, u32[]{:S(2)}, u32[]{:S(2)}) %collective-permute-start.4) | collective-permute-done | bytes 133152 | tf_op jit(solution)/shard_map/ppermute | solution.py:256
  132.1 2.7 %collective-permute-start.5 = (f32[130,256]{1,0:T(8,128)S(1)}, f32[130,256]{1,0:T(8,128)S(1)}, u32[]{:S(2)}, u32[]{:S(2)}) collective-permute-start(f32[130,256]{1,0:T(8,128)S(1)} %add.34), channel_id=1, source_target_pairs={{0,16},{1,17},{2,18},{3,19},{4,20},{5,21},{6,22},{7,23},{8,24},{9,... | collective-permute-start | bytes 399368 | tf_op jit(solution)/shard_map/ppermute | solution.py:256
  134.8 4.9 %collective-permute-done.5 = f32[130,256]{1,0:T(8,128)S(1)} collective-permute-done((f32[130,256]{1,0:T(8,128)S(1)}, f32[130,256]{1,0:T(8,128)S(1)}, u32[]{:S(2)}, u32[]{:S(2)}) %collective-permute-start.5) | collective-permute-done | bytes 133152 | tf_op jit(solution)/shard_map/ppermute | solution.py:256
  139.6 0.7 add.35.packed_ref
  140.3 38.0 %shard_map.52 = f32[256,128]{1,0:T(8,128)} custom-call(f32[130,256]{1,0:T(8,128)} %add.35.packed_ref), custom_call_target="tpu_custom_call" | custom-call | tf_op jit(solution)/shard_map/pallas_call | solution.py:229
  178.3 1.2 slice_reduce_fusion
  179.5 0.0 copy-start.4
  179.5 0.0 copy-start.2
  179.6 5.1 %fusion.2 = f32[1,16384]{1,0:T(1,128)S(1)} fusion(bf16[256,1]{0,1:T(2,128)(2,1)S(1)} %reshape.18, bf16[256,16384]{1,0:T(8,128)(2,1)} %get-tuple-element.13), kind=kOutput, calls=%fused_computation.10 | convolution fusion | flops 8388608 | bytes 8454656 | tf_op jit(solution)/shard_map/dot_general | solution.py:301
  184.7 1.2 fusion.1
  185.8 0.0 copy-done.4
  185.9 0.7 maximum_subtract_fusion
  (16 shorter events, 0.2 us)
Async XLA Ops:
  0.6 11.1 %copy-start.3 = (f32[4,16,64]{2,1,0:T(8,128)S(1)}, f32[4,16,64]{2,1,0:T(8,128)}, u32[]{:S(2)}) copy-start(f32[4,16,64]{2,1,0:T(8,128)} %param.5) | copy-start | bytes 49156
  2.8 57.5 %collective-permute-start = (bf16[64,15361]{1,0:T(8,128)(2,1)S(1)}, bf16[64,15361]{1,0:T(8,128)(2,1)S(1)}, u32[]{:S(2)}, u32[]{:S(2)}) collective-permute-start(bf16[64,15361]{1,0:T(8,128)(2,1)S(1)} %slice.21), channel_id=1, source_target_pairs={{0,1},{1,2},{2,3},{3,4},{4,5},{5,6},{6,7},{7,8},{8,9},{9,10},{10,1... | collective-permute-start | bytes 5898632 | tf_op jit(solution)/shard_map/ppermute | solution.py:16
  6.2 54.1 %copy-start = (bf16[64,32768]{1,0:T(8,128)(2,1)S(1)}, bf16[64,32768]{1,0:T(8,128)(2,1)}, u32[]{:S(2)}) copy-start(bf16[64,32768]{1,0:T(8,128)(2,1)} %param.3) | copy-start | bytes 12582916
  112.2 3.6 %collective-permute-start.1 = (f32[130,256]{1,0:T(8,128)S(1)}, f32[130,256]{1,0:T(8,128)S(1)}, u32[]{:S(2)}, u32[]{:S(2)}) collective-permute-start(f32[130,256]{1,0:T(8,128)S(1)} %pad_maximum_fusion.1), channel_id=1, source_target_pairs={{0,1},{1,0},{2,3},{3,2},{4,5},{5,4},{6,7},{7,6},{8,9},{9,8},{10,11... | collective-permute-start | bytes 399368 | tf_op jit(solution)/shard_map/ppermute | solution.py:256
  115.8 6.0 %collective-permute-start.2 = (f32[130,256]{1,0:T(8,128)S(1)}, f32[130,256]{1,0:T(8,128)S(1)}, u32[]{:S(2)}, u32[]{:S(2)}) collective-permute-start(f32[130,256]{1,0:T(8,128)S(1)} %fusion), channel_id=1, source_target_pairs={{0,2},{1,3},{2,0},{3,1},{4,6},{5,7},{6,4},{7,5},{8,10},{9,11},{10,... | collective-permute-start | bytes 399368 | tf_op jit(solution)/shard_map/ppermute | solution.py:256
  121.8 5.1 %collective-permute-start.3 = (f32[130,256]{1,0:T(8,128)S(1)}, f32[130,256]{1,0:T(8,128)S(1)}, u32[]{:S(2)}, u32[]{:S(2)}) collective-permute-start(f32[130,256]{1,0:T(8,128)S(1)} %add.32), channel_id=1, source_target_pairs={{0,4},{1,5},{2,6},{3,7},{4,0},{5,1},{6,2},{7,3},{8,12},{9,13},{10,... | collective-permute-start | bytes 399368 | tf_op jit(solution)/shard_map/ppermute | solution.py:256
  127.0 5.1 %collective-permute-start.4 = (f32[130,256]{1,0:T(8,128)S(1)}, f32[130,256]{1,0:T(8,128)S(1)}, u32[]{:S(2)}, u32[]{:S(2)}) collective-permute-start(f32[130,256]{1,0:T(8,128)S(1)} %add.33), channel_id=1, source_target_pairs={{0,8},{1,9},{2,10},{3,11},{4,12},{5,13},{6,14},{7,15},{8,0},{9,1},... | collective-permute-start | bytes 399368 | tf_op jit(solution)/shard_map/ppermute | solution.py:256
  132.1 7.5 %collective-permute-start.5 = (f32[130,256]{1,0:T(8,128)S(1)}, f32[130,256]{1,0:T(8,128)S(1)}, u32[]{:S(2)}, u32[]{:S(2)}) collective-permute-start(f32[130,256]{1,0:T(8,128)S(1)} %add.34), channel_id=1, source_target_pairs={{0,16},{1,17},{2,18},{3,19},{4,20},{5,21},{6,22},{7,23},{8,24},{9,... | collective-permute-start | bytes 399368 | tf_op jit(solution)/shard_map/ppermute | solution.py:256
  178.3 6.3 %copy-start.1 = (bf16[256,16384]{1,0:T(8,128)(2,1)S(1)}, bf16[256,16384]{1,0:T(8,128)(2,1)}, u32[]{:S(2)}) copy-start(bf16[256,16384]{1,0:T(8,128)(2,1)} %get-tuple-element.12) | copy-start | bytes 25165828
  179.5 6.3 %copy-start.4 = (f32[256]{0:T(256)}, f32[256]{0:T(256)S(1)}, u32[]{:S(2)}) copy-start(f32[256]{0:T(256)S(1)} %slice_reduce_fusion) | copy-start | bytes 3076
  179.5 6.3 %copy-start.2 = (bf16[32768]{0:T(1024)(128)(2,1)S(1)}, bf16[32768]{0:T(1024)(128)(2,1)}, u32[]{:S(2)}) copy-start(bf16[32768]{0:T(1024)(128)(2,1)} %param.4) | copy-start | bytes 196612

commit v11 on v9

--- a/solution.py
+++ b/solution.py
@@ -193,7 +193,7 @@
             here = sublanes == j
             row = a_ref[pl.ds(j, 1), :][:, lo:]
             pivot = jnp.sum(jnp.where(at, row, 0.0), axis=1, keepdims=True)
-            column = jnp.sum(jnp.where(at, a_ref[:, lo:], 0.0), axis=1, keepdims=True)
+            column = jnp.sum(jnp.where(at[:, :128], a_ref[:, lo : lo + 128], 0.0), axis=1, keepdims=True)
             scaled_row = row / pivot
             scaled_rhs = x_ref[pl.ds(j, 1), :] / pivot
             a_ref[:, lo:] = jnp.where(here, scaled_row, a_ref[:, lo:] - column * scaled_row)

time: 184 us -> 184 us (level)
  no operation moved by 1% of the time
where the time goes in v11:
time: 184 us
  Pallas kernels  131 us (71%)
  waiting for transfers between devices  17.4 us (9%)
  starting transfers between devices  12.4 us (7%)
  local copies, waits for them, and re-layouts  11.5 us (6%)
  matrix products  6.29 us (3%)
  other arithmetic  4.15 us (2%)
    pallas_call x2, Pallas kernels, features_and_sums(): pl.pallas_call(kernel, grid=(n_blocks,), in_specs=[pl.BlockSpec(memory_sp...  95.9 us
    pallas_call x1, Pallas kernels, ridge_solve_packed(): pl.pallas_call(functools.partial(jordan_kernel, ridge), in_specs=[pl.Bloc...  35.1 us
    ppermute x5, waiting for transfers between devices, butterfly_sum(): x = x + lax.ppermute(x, axes, [(i, i ^ step) for i in range(size)])  17.4 us
    ppermute x5, starting transfers between devices, butterfly_sum(): x = x + lax.ppermute(x, axes, [(i, i ^ step) for i in range(size)])  9.91 us
    dot_general x2, matrix products, local(): jnp.dot(rounded, f, preferred_element_type=jnp.float32)  6.29 us
    concatenate x1, local copies, waits for them, and re-layouts, local(): jnp.concatenate([jnp.zeros_like(stream[:, :1]), stream[:, :length - 1]], 1)  5.46 us
  transfers between devices with their start and end apart: 6, of which 5 were waited for; matrix products, arithmetic and copies ran while one was open for 4% of the time, Pallas kernels for 26%

profile of v11, /device:TPU:0, one launch (start us, length us, event | category | flops | bytes accessed | tf_op | source)
XLA Modules:
  0.0 183.6 jit_solution(17687404216796244892)
XLA Ops:
  0.6 0.0 copy-start.3
  0.6 2.1 %slice.21 = bf16[64,15361]{1,0:T(8,128)(2,1)S(1)} slice(bf16[64,32768]{1,0:T(8,128)(2,1)} %param.3), slice={[0:64], [17407:32768]} | slice | bytes 3932416 | tf_op jit(solution)/shard_map/slice | solution.py:256
  2.8 2.5 %collective-permute-start = (bf16[64,15361]{1,0:T(8,128)(2,1)S(1)}, bf16[64,15361]{1,0:T(8,128)(2,1)S(1)}, u32[]{:S(2)}, u32[]{:S(2)}) collective-permute-start(bf16[64,15361]{1,0:T(8,128)(2,1)S(1)} %slice.21), channel_id=1, source_target_pairs={{0,1},{1,2},{2,3},{3,4},{4,5},{5,6},{6,7},{7,8},{8,9},{9,10},{10,1... | collective-permute-start | bytes 5898632 | tf_op jit(solution)/shard_map/ppermute | solution.py:16
  5.3 0.9 reshape.9.tgt_ref
  6.2 0.0 copy-start
  6.2 5.5 %concatenate.23.w_ref = bf16[64,32768]{1,0:T(8,128)(2,1)} pad(bf16[64,32767]{1,0:T(8,128)(2,1)} %bitcast.11, bf16[]{:T(256)} %constant.3.clone.1), padding=0_0x1_0 | pad | bytes 8388482 | tf_op jit(solution)/shard_map/concatenate | solution.py:267
  11.7 0.0 copy-done.3
  11.7 0.6 broadcast_in_dim.7.taps_ref
  12.3 48.0 %shard_map.51 = (bf16[256,16384]{1,0:T(8,128)(2,1)}, f32[256,256]{1,0:T(8,128)S(1)}, f32[1,256]{1,0:T(1,128)S(1)}) custom-call(bf16[64,32768]{1,0:T(8,128)(2,1)} %concatenate.23.w_ref, f32[64,64,128]{2,1,0:T(8,128)S(1)} %broadcast_in_dim.7.taps_ref, bf16[1,32768]{1,0:T(2,128)(2,1)S(1)} %reshape.9.tgt_ref), custom_call_target="tpu_custom_call" | custom-call | tf_op jit(solution)/shard_map/pallas_call | solution.py:98
  60.3 0.0 collective-permute-done
  60.3 0.0 copy-done
  60.3 2.6 %pad_maximum_fusion.w_ref = bf16[64,31744]{1,0:T(8,128)(2,1)} fusion(bf16[64,32768]{1,0:T(8,128)(2,1)S(1)} %copy-done, bf16[64,15361]{1,0:T(8,128)(2,1)S(1)} %collective-permute-done), kind=kLoop, calls=%fused_computation.1 | loop fusion | flops 8126464 | bytes 10223744 | tf_op jit(solution)/shard_map/concatenate | solution.py:262
  62.9 47.9 %shard_map.50 = (bf16[256,16384]{1,0:T(8,128)(2,1)}, f32[256,256]{1,0:T(8,128)S(1)}, f32[1,256]{1,0:T(1,128)S(1)}) custom-call(bf16[64,31744]{1,0:T(8,128)(2,1)} %pad_maximum_fusion.w_ref, f32[64,64,128]{2,1,0:T(8,128)S(1)} %broadcast_in_dim.7.taps_ref, bf16[1,32768]{1,0:T(2,128)(2,1)S(1)} %reshape.9.tgt_ref), custom_call_target="tpu_custom_call" | custom-call | tf_op jit(solution)/shard_map/pallas_call | solution.py:98
  110.9 1.2 gather_fusion
  112.2 2.6 %collective-permute-start.1 = (f32[130,256]{1,0:T(8,128)S(1)}, f32[130,256]{1,0:T(8,128)S(1)}, u32[]{:S(2)}, u32[]{:S(2)}) collective-permute-start(f32[130,256]{1,0:T(8,128)S(1)} %pad_maximum_fusion.1), channel_id=1, source_target_pairs={{0,1},{1,0},{2,3},{3,2},{4,5},{5,4},{6,7},{7,6},{8,9},{9,8},{10,11... | collective-permute-start | bytes 399368 | tf_op jit(solution)/shard_map/ppermute | solution.py:235
  114.7 1.0 collective-permute-done.1
  115.8 1.5 collective-permute-start.2
  117.3 4.5 %collective-permute-done.2 = f32[130,256]{1,0:T(8,128)S(1)} collective-permute-done((f32[130,256]{1,0:T(8,128)S(1)}, f32[130,256]{1,0:T(8,128)S(1)}, u32[]{:S(2)}, u32[]{:S(2)}) %collective-permute-start.2) | collective-permute-done | bytes 133152 | tf_op jit(solution)/shard_map/ppermute | solution.py:235
  121.8 1.6 collective-permute-start.3
  123.4 3.6 %collective-permute-done.3 = f32[130,256]{1,0:T(8,128)S(1)} collective-permute-done((f32[130,256]{1,0:T(8,128)S(1)}, f32[130,256]{1,0:T(8,128)S(1)}, u32[]{:S(2)}, u32[]{:S(2)}) %collective-permute-start.3) | collective-permute-done | bytes 133152 | tf_op jit(solution)/shard_map/ppermute | solution.py:235
  127.0 1.6 collective-permute-start.4
  128.6 3.5 %collective-permute-done.4 = f32[130,256]{1,0:T(8,128)S(1)} collective-permute-done((f32[130,256]{1,0:T(8,128)S(1)}, f32[130,256]{1,0:T(8,128)S(1)}, u32[]{:S(2)}, u32[]{:S(2)}) %collective-permute-start.4) | collective-permute-done | bytes 133152 | tf_op jit(solution)/shard_map/ppermute | solution.py:235
  132.1 2.7 %collective-permute-start.5 = (f32[130,256]{1,0:T(8,128)S(1)}, f32[130,256]{1,0:T(8,128)S(1)}, u32[]{:S(2)}, u32[]{:S(2)}) collective-permute-start(f32[130,256]{1,0:T(8,128)S(1)} %add.34), channel_id=1, source_target_pairs={{0,16},{1,17},{2,18},{3,19},{4,20},{5,21},{6,22},{7,23},{8,24},{9,... | collective-permute-start | bytes 399368 | tf_op jit(solution)/shard_map/ppermute | solution.py:235
  134.8 4.9 %collective-permute-done.5 = f32[130,256]{1,0:T(8,128)S(1)} collective-permute-done((f32[130,256]{1,0:T(8,128)S(1)}, f32[130,256]{1,0:T(8,128)S(1)}, u32[]{:S(2)}, u32[]{:S(2)}) %collective-permute-start.5) | collective-permute-done | bytes 133152 | tf_op jit(solution)/shard_map/ppermute | solution.py:235
  139.6 0.7 add.35.packed_ref
  140.3 35.1 %shard_map.52 = f32[256,128]{1,0:T(8,128)} custom-call(f32[130,256]{1,0:T(8,128)} %add.35.packed_ref), custom_call_target="tpu_custom_call" | custom-call | tf_op jit(solution)/shard_map/pallas_call | solution.py:208
  175.4 1.2 slice_reduce_fusion
  176.6 0.0 copy-start.4
  176.6 0.0 copy-start.2
  176.7 5.1 %fusion.2 = f32[1,16384]{1,0:T(1,128)S(1)} fusion(bf16[256,1]{0,1:T(2,128)(2,1)S(1)} %reshape.18, bf16[256,16384]{1,0:T(8,128)(2,1)} %get-tuple-element.13), kind=kOutput, calls=%fused_computation.10 | convolution fusion | flops 8388608 | bytes 8454656 | tf_op jit(solution)/shard_map/dot_general | solution.py:280
  181.7 1.2 fusion.1
  183.0 0.7 maximum_subtract_fusion
  (16 shorter events, 0.2 us)
Async XLA Ops:
  0.6 11.1 %copy-start.3 = (f32[4,16,64]{2,1,0:T(8,128)S(1)}, f32[4,16,64]{2,1,0:T(8,128)}, u32[]{:S(2)}) copy-start(f32[4,16,64]{2,1,0:T(8,128)} %param.5) | copy-start | bytes 49156
  2.8 57.5 %collective-permute-start = (bf16[64,15361]{1,0:T(8,128)(2,1)S(1)}, bf16[64,15361]{1,0:T(8,128)(2,1)S(1)}, u32[]{:S(2)}, u32[]{:S(2)}) collective-permute-start(bf16[64,15361]{1,0:T(8,128)(2,1)S(1)} %slice.21), channel_id=1, source_target_pairs={{0,1},{1,2},{2,3},{3,4},{4,5},{5,6},{6,7},{7,8},{8,9},{9,10},{10,1... | collective-permute-start | bytes 5898632 | tf_op jit(solution)/shard_map/ppermute | solution.py:16
  6.2 54.1 %copy-start = (bf16[64,32768]{1,0:T(8,128)(2,1)S(1)}, bf16[64,32768]{1,0:T(8,128)(2,1)}, u32[]{:S(2)}) copy-start(bf16[64,32768]{1,0:T(8,128)(2,1)} %param.3) | copy-start | bytes 12582916
  112.2 3.6 %collective-permute-start.1 = (f32[130,256]{1,0:T(8,128)S(1)}, f32[130,256]{1,0:T(8,128)S(1)}, u32[]{:S(2)}, u32[]{:S(2)}) collective-permute-start(f32[130,256]{1,0:T(8,128)S(1)} %pad_maximum_fusion.1), channel_id=1, source_target_pairs={{0,1},{1,0},{2,3},{3,2},{4,5},{5,4},{6,7},{7,6},{8,9},{9,8},{10,11... | collective-permute-start | bytes 399368 | tf_op jit(solution)/shard_map/ppermute | solution.py:235
  115.8 6.0 %collective-permute-start.2 = (f32[130,256]{1,0:T(8,128)S(1)}, f32[130,256]{1,0:T(8,128)S(1)}, u32[]{:S(2)}, u32[]{:S(2)}) collective-permute-start(f32[130,256]{1,0:T(8,128)S(1)} %fusion), channel_id=1, source_target_pairs={{0,2},{1,3},{2,0},{3,1},{4,6},{5,7},{6,4},{7,5},{8,10},{9,11},{10,... | collective-permute-start | bytes 399368 | tf_op jit(solution)/shard_map/ppermute | solution.py:235
  121.8 5.1 %collective-permute-start.3 = (f32[130,256]{1,0:T(8,128)S(1)}, f32[130,256]{1,0:T(8,128)S(1)}, u32[]{:S(2)}, u32[]{:S(2)}) collective-permute-start(f32[130,256]{1,0:T(8,128)S(1)} %add.32), channel_id=1, source_target_pairs={{0,4},{1,5},{2,6},{3,7},{4,0},{5,1},{6,2},{7,3},{8,12},{9,13},{10,... | collective-permute-start | bytes 399368 | tf_op jit(solution)/shard_map/ppermute | solution.py:235
  127.0 5.1 %collective-permute-start.4 = (f32[130,256]{1,0:T(8,128)S(1)}, f32[130,256]{1,0:T(8,128)S(1)}, u32[]{:S(2)}, u32[]{:S(2)}) collective-permute-start(f32[130,256]{1,0:T(8,128)S(1)} %add.33), channel_id=1, source_target_pairs={{0,8},{1,9},{2,10},{3,11},{4,12},{5,13},{6,14},{7,15},{8,0},{9,1},... | collective-permute-start | bytes 399368 | tf_op jit(solution)/shard_map/ppermute | solution.py:235
  132.1 7.5 %collective-permute-start.5 = (f32[130,256]{1,0:T(8,128)S(1)}, f32[130,256]{1,0:T(8,128)S(1)}, u32[]{:S(2)}, u32[]{:S(2)}) collective-permute-start(f32[130,256]{1,0:T(8,128)S(1)} %add.34), channel_id=1, source_target_pairs={{0,16},{1,17},{2,18},{3,19},{4,20},{5,21},{6,22},{7,23},{8,24},{9,... | collective-permute-start | bytes 399368 | tf_op jit(solution)/shard_map/ppermute | solution.py:235
  175.4 6.3 %copy-start.1 = (bf16[256,16384]{1,0:T(8,128)(2,1)S(1)}, bf16[256,16384]{1,0:T(8,128)(2,1)}, u32[]{:S(2)}) copy-start(bf16[256,16384]{1,0:T(8,128)(2,1)} %get-tuple-element.12) | copy-start | bytes 25165828
  176.6 6.3 %copy-start.4 = (f32[256]{0:T(256)}, f32[256]{0:T(256)S(1)}, u32[]{:S(2)}) copy-start(f32[256]{0:T(256)S(1)} %slice_reduce_fusion) | copy-start | bytes 3076
  176.6 6.3 %copy-start.2 = (bf16[32768]{0:T(1024)(128)(2,1)S(1)}, bf16[32768]{0:T(1024)(128)(2,1)}, u32[]{:S(2)}) copy-start(bf16[32768]{0:T(1024)(128)(2,1)} %param.4) | copy-start | bytes 196612

commit v12 on v11

--- a/solution.py
+++ b/solution.py
@@ -34,10 +34,10 @@
     return jnp.concatenate(row_list, 0)
 
 
-TIME_BLOCK = 2048
+TIME_BLOCK = 4096
 ROW_GROUP = 16
-NARROW_CHUNK = 1024
-WIDE_CHUNK = 1024
+NARROW_CHUNK = 2048
+WIDE_CHUNK = 2048
 
 
 def feature_kernel(dilations, span, base, first_block, taps_per_filter, w_ref, taps_ref, tgt_ref, f_ref, g_ref, c_ref):

time: 184 us -> 172 us (0.935)
  Pallas kernels: 131 us -> 119 us
    pallas_call x2, Pallas kernels: 95.9 us -> 84.2 us  [features_and_sums(): pl.pallas_call(kernel, grid=(n_blocks,), in_specs=[pl.BlockSpec(memory_sp...]
  transfers between devices with their start and end apart: 6 -> 6, of which waited for: 5 -> 5; matrix products, arithmetic and copies ran while one was open for 4% -> 4% of each run, Pallas kernels for 26% -> 25%
where the time goes in v12:
time: 172 us
  Pallas kernels  119 us (69%)
  waiting for transfers between devices  17.4 us (10%)
  starting transfers between devices  12.4 us (7%)
  local copies, waits for them, and re-layouts  11.5 us (7%)
  matrix products  6.29 us (4%)
  other arithmetic  4.15 us (2%)
    pallas_call x2, Pallas kernels, features_and_sums(): pl.pallas_call(kernel, grid=(n_blocks,), in_specs=[pl.BlockSpec(memory_sp...  84.2 us
    pallas_call x1, Pallas kernels, ridge_solve_packed(): pl.pallas_call(functools.partial(jordan_kernel, ridge), in_specs=[pl.Bloc...  35.1 us
    ppermute x5, waiting for transfers between devices, butterfly_sum(): x = x + lax.ppermute(x, axes, [(i, i ^ step) for i in range(size)])  17.4 us
    ppermute x5, starting transfers between devices, butterfly_sum(): x = x + lax.ppermute(x, axes, [(i, i ^ step) for i in range(size)])  9.91 us
    dot_general x2, matrix products, local(): jnp.dot(rounded, f, preferred_element_type=jnp.float32)  6.29 us
    concatenate x1, local copies, waits for them, and re-layouts, local(): jnp.concatenate([jnp.zeros_like(stream[:, :1]), stream[:, :length - 1]], 1)  5.46 us
  transfers between devices with their start and end apart: 6, of which 5 were waited for; matrix products, arithmetic and copies ran while one was open for 4% of the time, Pallas kernels for 25%

profile of v12, /device:TPU:0, one launch (start us, length us, event | category | flops | bytes accessed | tf_op | source)
XLA Modules:
  0.0 172.0 jit_solution(5196113050753770730)
XLA Ops:
  0.6 0.0 copy-start.3
  0.6 2.1 %slice.21 = bf16[64,15361]{1,0:T(8,128)(2,1)S(1)} slice(bf16[64,32768]{1,0:T(8,128)(2,1)} %param.3), slice={[0:64], [17407:32768]} | slice | bytes 3932416 | tf_op jit(solution)/shard_map/slice | solution.py:256
  2.8 2.5 %collective-permute-start = (bf16[64,15361]{1,0:T(8,128)(2,1)S(1)}, bf16[64,15361]{1,0:T(8,128)(2,1)S(1)}, u32[]{:S(2)}, u32[]{:S(2)}) collective-permute-start(bf16[64,15361]{1,0:T(8,128)(2,1)S(1)} %slice.21), channel_id=1, source_target_pairs={{0,1},{1,2},{2,3},{3,4},{4,5},{5,6},{6,7},{7,8},{8,9},{9,10},{10,1... | collective-permute-start | bytes 5898632 | tf_op jit(solution)/shard_map/ppermute | solution.py:16
  5.3 0.9 reshape.9.tgt_ref
  6.2 0.0 copy-start
  6.2 5.5 %concatenate.23.w_ref = bf16[64,32768]{1,0:T(8,128)(2,1)} pad(bf16[64,32767]{1,0:T(8,128)(2,1)} %bitcast.11, bf16[]{:T(256)} %constant.3.clone.1), padding=0_0x1_0 | pad | bytes 8388482 | tf_op jit(solution)/shard_map/concatenate | solution.py:267
  11.7 0.0 copy-done.3
  11.7 0.6 broadcast_in_dim.7.taps_ref
  12.3 42.2 %shard_map.51 = (bf16[256,16384]{1,0:T(8,128)(2,1)}, f32[256,256]{1,0:T(8,128)S(1)}, f32[1,256]{1,0:T(1,128)S(1)}) custom-call(bf16[64,32768]{1,0:T(8,128)(2,1)} %concatenate.23.w_ref, f32[64,64,128]{2,1,0:T(8,128)S(1)} %broadcast_in_dim.7.taps_ref, bf16[1,32768]{1,0:T(2,128)(2,1)S(1)} %reshape.9.tgt_ref), custom_call_target="tpu_custom_call" | custom-call | tf_op jit(solution)/shard_map/pallas_call | solution.py:98
  54.6 0.0 collective-permute-done
  54.6 0.0 copy-done
  54.6 2.6 %pad_maximum_fusion.w_ref = bf16[64,31744]{1,0:T(8,128)(2,1)} fusion(bf16[64,32768]{1,0:T(8,128)(2,1)S(1)} %copy-done, bf16[64,15361]{1,0:T(8,128)(2,1)S(1)} %collective-permute-done), kind=kLoop, calls=%fused_computation.1 | loop fusion | flops 8126464 | bytes 10223744 | tf_op jit(solution)/shard_map/concatenate | solution.py:262
  57.2 42.0 %shard_map.50 = (bf16[256,16384]{1,0:T(8,128)(2,1)}, f32[256,256]{1,0:T(8,128)S(1)}, f32[1,256]{1,0:T(1,128)S(1)}) custom-call(bf16[64,31744]{1,0:T(8,128)(2,1)} %pad_maximum_fusion.w_ref, f32[64,64,128]{2,1,0:T(8,128)S(1)} %broadcast_in_dim.7.taps_ref, bf16[1,32768]{1,0:T(2,128)(2,1)S(1)} %reshape.9.tgt_ref), custom_call_target="tpu_custom_call" | custom-call | tf_op jit(solution)/shard_map/pallas_call | solution.py:98
  99.3 1.2 gather_fusion
  100.6 2.6 %collective-permute-start.1 = (f32[130,256]{1,0:T(8,128)S(1)}, f32[130,256]{1,0:T(8,128)S(1)}, u32[]{:S(2)}, u32[]{:S(2)}) collective-permute-start(f32[130,256]{1,0:T(8,128)S(1)} %pad_maximum_fusion.1), channel_id=1, source_target_pairs={{0,1},{1,0},{2,3},{3,2},{4,5},{5,4},{6,7},{7,6},{8,9},{9,8},{10,11... | collective-permute-start | bytes 399368 | tf_op jit(solution)/shard_map/ppermute | solution.py:235
  103.1 1.0 collective-permute-done.1
  104.1 1.5 collective-permute-start.2
  105.6 4.5 %collective-permute-done.2 = f32[130,256]{1,0:T(8,128)S(1)} collective-permute-done((f32[130,256]{1,0:T(8,128)S(1)}, f32[130,256]{1,0:T(8,128)S(1)}, u32[]{:S(2)}, u32[]{:S(2)}) %collective-permute-start.2) | collective-permute-done | bytes 133152 | tf_op jit(solution)/shard_map/ppermute | solution.py:235
  110.2 1.6 collective-permute-start.3
  111.7 3.6 %collective-permute-done.3 = f32[130,256]{1,0:T(8,128)S(1)} collective-permute-done((f32[130,256]{1,0:T(8,128)S(1)}, f32[130,256]{1,0:T(8,128)S(1)}, u32[]{:S(2)}, u32[]{:S(2)}) %collective-permute-start.3) | collective-permute-done | bytes 133152 | tf_op jit(solution)/shard_map/ppermute | solution.py:235
  115.3 1.6 collective-permute-start.4
  117.0 3.5 %collective-permute-done.4 = f32[130,256]{1,0:T(8,128)S(1)} collective-permute-done((f32[130,256]{1,0:T(8,128)S(1)}, f32[130,256]{1,0:T(8,128)S(1)}, u32[]{:S(2)}, u32[]{:S(2)}) %collective-permute-start.4) | collective-permute-done | bytes 133152 | tf_op jit(solution)/shard_map/ppermute | solution.py:235
  120.5 2.7 %collective-permute-start.5 = (f32[130,256]{1,0:T(8,128)S(1)}, f32[130,256]{1,0:T(8,128)S(1)}, u32[]{:S(2)}, u32[]{:S(2)}) collective-permute-start(f32[130,256]{1,0:T(8,128)S(1)} %add.34), channel_id=1, source_target_pairs={{0,16},{1,17},{2,18},{3,19},{4,20},{5,21},{6,22},{7,23},{8,24},{9,... | collective-permute-start | bytes 399368 | tf_op jit(solution)/shard_map/ppermute | solution.py:235
  123.1 4.9 %collective-permute-done.5 = f32[130,256]{1,0:T(8,128)S(1)} collective-permute-done((f32[130,256]{1,0:T(8,128)S(1)}, f32[130,256]{1,0:T(8,128)S(1)}, u32[]{:S(2)}, u32[]{:S(2)}) %collective-permute-start.5) | collective-permute-done | bytes 133152 | tf_op jit(solution)/shard_map/ppermute | solution.py:235
  128.0 0.7 add.35.packed_ref
  128.7 35.1 %shard_map.52 = f32[256,128]{1,0:T(8,128)} custom-call(f32[130,256]{1,0:T(8,128)} %add.35.packed_ref), custom_call_target="tpu_custom_call" | custom-call | tf_op jit(solution)/shard_map/pallas_call | solution.py:208
  163.8 1.2 slice_reduce_fusion
  165.0 0.0 copy-start.4
  165.0 0.0 copy-start.2
  165.0 5.1 %fusion.2 = f32[1,16384]{1,0:T(1,128)S(1)} fusion(bf16[256,1]{0,1:T(2,128)(2,1)S(1)} %reshape.18, bf16[256,16384]{1,0:T(8,128)(2,1)} %get-tuple-element.13), kind=kOutput, calls=%fused_computation.10 | convolution fusion | flops 8388608 | bytes 8454656 | tf_op jit(solution)/shard_map/dot_general | solution.py:280
  170.1 1.2 fusion.1
  171.3 0.7 maximum_subtract_fusion
  (16 shorter events, 0.2 us)
Async XLA Ops:
  0.6 11.1 %copy-start.3 = (f32[4,16,64]{2,1,0:T(8,128)S(1)}, f32[4,16,64]{2,1,0:T(8,128)}, u32[]{:S(2)}) copy-start(f32[4,16,64]{2,1,0:T(8,128)} %param.5) | copy-start | bytes 49156
  2.8 51.8 %collective-permute-start = (bf16[64,15361]{1,0:T(8,128)(2,1)S(1)}, bf16[64,15361]{1,0:T(8,128)(2,1)S(1)}, u32[]{:S(2)}, u32[]{:S(2)}) collective-permute-start(bf16[64,15361]{1,0:T(8,128)(2,1)S(1)} %slice.21), channel_id=1, source_target_pairs={{0,1},{1,2},{2,3},{3,4},{4,5},{5,6},{6,7},{7,8},{8,9},{9,10},{10,1... | collective-permute-start | bytes 5898632 | tf_op jit(solution)/shard_map/ppermute | solution.py:16
  6.2 48.3 %copy-start = (bf16[64,32768]{1,0:T(8,128)(2,1)S(1)}, bf16[64,32768]{1,0:T(8,128)(2,1)}, u32[]{:S(2)}) copy-start(bf16[64,32768]{1,0:T(8,128)(2,1)} %param.3) | copy-start | bytes 12582916
  100.6 3.6 %collective-permute-start.1 = (f32[130,256]{1,0:T(8,128)S(1)}, f32[130,256]{1,0:T(8,128)S(1)}, u32[]{:S(2)}, u32[]{:S(2)}) collective-permute-start(f32[130,256]{1,0:T(8,128)S(1)} %pad_maximum_fusion.1), channel_id=1, source_target_pairs={{0,1},{1,0},{2,3},{3,2},{4,5},{5,4},{6,7},{7,6},{8,9},{9,8},{10,11... | collective-permute-start | bytes 399368 | tf_op jit(solution)/shard_map/ppermute | solution.py:235
  104.1 6.0 %collective-permute-start.2 = (f32[130,256]{1,0:T(8,128)S(1)}, f32[130,256]{1,0:T(8,128)S(1)}, u32[]{:S(2)}, u32[]{:S(2)}) collective-permute-start(f32[130,256]{1,0:T(8,128)S(1)} %fusion), channel_id=1, source_target_pairs={{0,2},{1,3},{2,0},{3,1},{4,6},{5,7},{6,4},{7,5},{8,10},{9,11},{10,... | collective-permute-start | bytes 399368 | tf_op jit(solution)/shard_map/ppermute | solution.py:235
  110.2 5.1 %collective-permute-start.3 = (f32[130,256]{1,0:T(8,128)S(1)}, f32[130,256]{1,0:T(8,128)S(1)}, u32[]{:S(2)}, u32[]{:S(2)}) collective-permute-start(f32[130,256]{1,0:T(8,128)S(1)} %add.32), channel_id=1, source_target_pairs={{0,4},{1,5},{2,6},{3,7},{4,0},{5,1},{6,2},{7,3},{8,12},{9,13},{10,... | collective-permute-start | bytes 399368 | tf_op jit(solution)/shard_map/ppermute | solution.py:235
  115.3 5.1 %collective-permute-start.4 = (f32[130,256]{1,0:T(8,128)S(1)}, f32[130,256]{1,0:T(8,128)S(1)}, u32[]{:S(2)}, u32[]{:S(2)}) collective-permute-start(f32[130,256]{1,0:T(8,128)S(1)} %add.33), channel_id=1, source_target_pairs={{0,8},{1,9},{2,10},{3,11},{4,12},{5,13},{6,14},{7,15},{8,0},{9,1},... | collective-permute-start | bytes 399368 | tf_op jit(solution)/shard_map/ppermute | solution.py:235
  120.5 7.5 %collective-permute-start.5 = (f32[130,256]{1,0:T(8,128)S(1)}, f32[130,256]{1,0:T(8,128)S(1)}, u32[]{:S(2)}, u32[]{:S(2)}) collective-permute-start(f32[130,256]{1,0:T(8,128)S(1)} %add.34), channel_id=1, source_target_pairs={{0,16},{1,17},{2,18},{3,19},{4,20},{5,21},{6,22},{7,23},{8,24},{9,... | collective-permute-start | bytes 399368 | tf_op jit(solution)/shard_map/ppermute | solution.py:235
  163.8 6.3 %copy-start.1 = (bf16[256,16384]{1,0:T(8,128)(2,1)S(1)}, bf16[256,16384]{1,0:T(8,128)(2,1)}, u32[]{:S(2)}) copy-start(bf16[256,16384]{1,0:T(8,128)(2,1)} %get-tuple-element.12) | copy-start | bytes 25165828
  165.0 6.3 %copy-start.4 = (f32[256]{0:T(256)}, f32[256]{0:T(256)S(1)}, u32[]{:S(2)}) copy-start(f32[256]{0:T(256)S(1)} %slice_reduce_fusion) | copy-start | bytes 3076
  165.0 6.3 %copy-start.2 = (bf16[32768]{0:T(1024)(128)(2,1)S(1)}, bf16[32768]{0:T(1024)(128)(2,1)}, u32[]{:S(2)}) copy-start(bf16[32768]{0:T(1024)(128)(2,1)} %param.4) | copy-start | bytes 196612

commit v13 on v12

--- a/solution.py
+++ b/solution.py
@@ -36,8 +36,8 @@
 
 TIME_BLOCK = 4096
 ROW_GROUP = 16
-NARROW_CHUNK = 2048
-WIDE_CHUNK = 2048
+NARROW_CHUNK = 4096
+WIDE_CHUNK = 4096
 
 
 def feature_kernel(dilations, span, base, first_block, taps_per_filter, w_ref, taps_ref, tgt_ref, f_ref, g_ref, c_ref):

time: 172 us -> 162 us (0.942)
  Pallas kernels: 119 us -> 109 us
    pallas_call x2, Pallas kernels: 84.2 us -> 74.3 us  [features_and_sums(): pl.pallas_call(kernel, grid=(n_blocks,), in_specs=[pl.BlockSpec(memory_sp...]
  transfers between devices with their start and end apart: 6 -> 6, of which waited for: 5 -> 5; matrix products, arithmetic and copies ran while one was open for 4% -> 4% of each run, Pallas kernels for 25% -> 23%
where the time goes in v13:
time: 162 us
  Pallas kernels  109 us (67%)
  waiting for transfers between devices  17.4 us (11%)
  starting transfers between devices  12.4 us (8%)
  local copies, waits for them, and re-layouts  11.5 us (7%)
  matrix products  6.29 us (4%)
  other arithmetic  4.15 us (3%)
    pallas_call x2, Pallas kernels, features_and_sums(): pl.pallas_call(kernel, grid=(n_blocks,), in_specs=[pl.BlockSpec(memory_sp...  74.3 us
    pallas_call x1, Pallas kernels, ridge_solve_packed(): pl.pallas_call(functools.partial(jordan_kernel, ridge), in_specs=[pl.Bloc...  35.1 us
    ppermute x5, waiting for transfers between devices, butterfly_sum(): x = x + lax.ppermute(x, axes, [(i, i ^ step) for i in range(size)])  17.4 us
    ppermute x5, starting transfers between devices, butterfly_sum(): x = x + lax.ppermute(x, axes, [(i, i ^ step) for i in range(size)])  9.9 us
    dot_general x2, matrix products, local(): jnp.dot(rounded, f, preferred_element_type=jnp.float32)  6.29 us
    concatenate x1, local copies, waits for them, and re-layouts, local(): jnp.concatenate([jnp.zeros_like(stream[:, :1]), stream[:, :length - 1]], 1)  5.46 us
  transfers between devices with their start and end apart: 6, of which 5 were waited for; matrix products, arithmetic and copies ran while one was open for 4% of the time, Pallas kernels for 23%

profile of v13, /device:TPU:0, one launch (start us, length us, event | category | flops | bytes accessed | tf_op | source)
XLA Modules:
  0.0 162.0 jit_solution(9639970317263484272)
XLA Ops:
  0.6 0.0 copy-start.3
  0.6 2.1 %slice.21 = bf16[64,15361]{1,0:T(8,128)(2,1)S(1)} slice(bf16[64,32768]{1,0:T(8,128)(2,1)} %param.3), slice={[0:64], [17407:32768]} | slice | bytes 3932416 | tf_op jit(solution)/shard_map/slice | solution.py:256
  2.8 2.5 %collective-permute-start = (bf16[64,15361]{1,0:T(8,128)(2,1)S(1)}, bf16[64,15361]{1,0:T(8,128)(2,1)S(1)}, u32[]{:S(2)}, u32[]{:S(2)}) collective-permute-start(bf16[64,15361]{1,0:T(8,128)(2,1)S(1)} %slice.21), channel_id=1, source_target_pairs={{0,1},{1,2},{2,3},{3,4},{4,5},{5,6},{6,7},{7,8},{8,9},{9,10},{10,1... | collective-permute-start | bytes 5898632 | tf_op jit(solution)/shard_map/ppermute | solution.py:16
  5.3 0.9 reshape.9.tgt_ref
  6.2 0.0 copy-start
  6.2 5.5 %concatenate.23.w_ref = bf16[64,32768]{1,0:T(8,128)(2,1)} pad(bf16[64,32767]{1,0:T(8,128)(2,1)} %bitcast.11, bf16[]{:T(256)} %constant.3.clone.1), padding=0_0x1_0 | pad | bytes 8388482 | tf_op jit(solution)/shard_map/concatenate | solution.py:267
  11.7 0.0 copy-done.3
  11.7 0.6 broadcast_in_dim.7.taps_ref
  12.3 37.2 %shard_map.51 = (bf16[256,16384]{1,0:T(8,128)(2,1)}, f32[256,256]{1,0:T(8,128)S(1)}, f32[1,256]{1,0:T(1,128)S(1)}) custom-call(bf16[64,32768]{1,0:T(8,128)(2,1)} %concatenate.23.w_ref, f32[64,64,128]{2,1,0:T(8,128)S(1)} %broadcast_in_dim.7.taps_ref, bf16[1,32768]{1,0:T(2,128)(2,1)S(1)} %reshape.9.tgt_ref), custom_call_target="tpu_custom_call" | custom-call | tf_op jit(solution)/shard_map/pallas_call | solution.py:98
  49.5 0.0 collective-permute-done
  49.5 0.0 copy-done
  49.5 2.6 %pad_maximum_fusion.w_ref = bf16[64,31744]{1,0:T(8,128)(2,1)} fusion(bf16[64,32768]{1,0:T(8,128)(2,1)S(1)} %copy-done, bf16[64,15361]{1,0:T(8,128)(2,1)S(1)} %collective-permute-done), kind=kLoop, calls=%fused_computation.1 | loop fusion | flops 8126464 | bytes 10223744 | tf_op jit(solution)/shard_map/concatenate | solution.py:262
  52.1 37.1 %shard_map.50 = (bf16[256,16384]{1,0:T(8,128)(2,1)}, f32[256,256]{1,0:T(8,128)S(1)}, f32[1,256]{1,0:T(1,128)S(1)}) custom-call(bf16[64,31744]{1,0:T(8,128)(2,1)} %pad_maximum_fusion.w_ref, f32[64,64,128]{2,1,0:T(8,128)S(1)} %broadcast_in_dim.7.taps_ref, bf16[1,32768]{1,0:T(2,128)(2,1)S(1)} %reshape.9.tgt_ref), custom_call_target="tpu_custom_call" | custom-call | tf_op jit(solution)/shard_map/pallas_call | solution.py:98
  89.3 1.2 gather_fusion
  90.6 2.6 %collective-permute-start.1 = (f32[130,256]{1,0:T(8,128)S(1)}, f32[130,256]{1,0:T(8,128)S(1)}, u32[]{:S(2)}, u32[]{:S(2)}) collective-permute-start(f32[130,256]{1,0:T(8,128)S(1)} %pad_maximum_fusion.1), channel_id=1, source_target_pairs={{0,1},{1,0},{2,3},{3,2},{4,5},{5,4},{6,7},{7,6},{8,9},{9,8},{10,11... | collective-permute-start | bytes 399368 | tf_op jit(solution)/shard_map/ppermute | solution.py:235
  93.2 1.0 collective-permute-done.1
  94.2 1.5 collective-permute-start.2
  95.7 4.5 %collective-permute-done.2 = f32[130,256]{1,0:T(8,128)S(1)} collective-permute-done((f32[130,256]{1,0:T(8,128)S(1)}, f32[130,256]{1,0:T(8,128)S(1)}, u32[]{:S(2)}, u32[]{:S(2)}) %collective-permute-start.2) | collective-permute-done | bytes 133152 | tf_op jit(solution)/shard_map/ppermute | solution.py:235
  100.2 1.6 collective-permute-start.3
  101.8 3.6 %collective-permute-done.3 = f32[130,256]{1,0:T(8,128)S(1)} collective-permute-done((f32[130,256]{1,0:T(8,128)S(1)}, f32[130,256]{1,0:T(8,128)S(1)}, u32[]{:S(2)}, u32[]{:S(2)}) %collective-permute-start.3) | collective-permute-done | bytes 133152 | tf_op jit(solution)/shard_map/ppermute | solution.py:235
  105.4 1.6 %collective-permute-start.4 = (f32[130,256]{1,0:T(8,128)S(1)}, f32[130,256]{1,0:T(8,128)S(1)}, u32[]{:S(2)}, u32[]{:S(2)}) collective-permute-start(f32[130,256]{1,0:T(8,128)S(1)} %add.33), channel_id=1, source_target_pairs={{0,8},{1,9},{2,10},{3,11},{4,12},{5,13},{6,14},{7,15},{8,0},{9,1},... | collective-permute-start | bytes 399368 | tf_op jit(solution)/shard_map/ppermute | solution.py:235
  107.0 3.5 %collective-permute-done.4 = f32[130,256]{1,0:T(8,128)S(1)} collective-permute-done((f32[130,256]{1,0:T(8,128)S(1)}, f32[130,256]{1,0:T(8,128)S(1)}, u32[]{:S(2)}, u32[]{:S(2)}) %collective-permute-start.4) | collective-permute-done | bytes 133152 | tf_op jit(solution)/shard_map/ppermute | solution.py:235
  110.5 2.6 %collective-permute-start.5 = (f32[130,256]{1,0:T(8,128)S(1)}, f32[130,256]{1,0:T(8,128)S(1)}, u32[]{:S(2)}, u32[]{:S(2)}) collective-permute-start(f32[130,256]{1,0:T(8,128)S(1)} %add.34), channel_id=1, source_target_pairs={{0,16},{1,17},{2,18},{3,19},{4,20},{5,21},{6,22},{7,23},{8,24},{9,... | collective-permute-start | bytes 399368 | tf_op jit(solution)/shard_map/ppermute | solution.py:235
  113.2 4.9 %collective-permute-done.5 = f32[130,256]{1,0:T(8,128)S(1)} collective-permute-done((f32[130,256]{1,0:T(8,128)S(1)}, f32[130,256]{1,0:T(8,128)S(1)}, u32[]{:S(2)}, u32[]{:S(2)}) %collective-permute-start.5) | collective-permute-done | bytes 133152 | tf_op jit(solution)/shard_map/ppermute | solution.py:235
  118.0 0.7 add.35.packed_ref
  118.7 35.1 %shard_map.52 = f32[256,128]{1,0:T(8,128)} custom-call(f32[130,256]{1,0:T(8,128)} %add.35.packed_ref), custom_call_target="tpu_custom_call" | custom-call | tf_op jit(solution)/shard_map/pallas_call | solution.py:208
  153.8 1.2 slice_reduce_fusion
  155.0 0.0 copy-start.4
  155.0 0.0 copy-start.2
  155.1 5.1 %fusion.2 = f32[1,16384]{1,0:T(1,128)S(1)} fusion(bf16[256,1]{0,1:T(2,128)(2,1)S(1)} %reshape.18, bf16[256,16384]{1,0:T(8,128)(2,1)} %get-tuple-element.13), kind=kOutput, calls=%fused_computation.10 | convolution fusion | flops 8388608 | bytes 8454656 | tf_op jit(solution)/shard_map/dot_general | solution.py:280
  160.2 1.2 fusion.1
  161.4 0.7 maximum_subtract_fusion
  (16 shorter events, 0.2 us)
Async XLA Ops:
  0.6 11.1 %copy-start.3 = (f32[4,16,64]{2,1,0:T(8,128)S(1)}, f32[4,16,64]{2,1,0:T(8,128)}, u32[]{:S(2)}) copy-start(f32[4,16,64]{2,1,0:T(8,128)} %param.5) | copy-start | bytes 49156
  2.8 46.7 %collective-permute-start = (bf16[64,15361]{1,0:T(8,128)(2,1)S(1)}, bf16[64,15361]{1,0:T(8,128)(2,1)S(1)}, u32[]{:S(2)}, u32[]{:S(2)}) collective-permute-start(bf16[64,15361]{1,0:T(8,128)(2,1)S(1)} %slice.21), channel_id=1, source_target_pairs={{0,1},{1,2},{2,3},{3,4},{4,5},{5,6},{6,7},{7,8},{8,9},{9,10},{10,1... | collective-permute-start | bytes 5898632 | tf_op jit(solution)/shard_map/ppermute | solution.py:16
  6.2 43.3 %copy-start = (bf16[64,32768]{1,0:T(8,128)(2,1)S(1)}, bf16[64,32768]{1,0:T(8,128)(2,1)}, u32[]{:S(2)}) copy-start(bf16[64,32768]{1,0:T(8,128)(2,1)} %param.3) | copy-start | bytes 12582916
  90.6 3.6 %collective-permute-start.1 = (f32[130,256]{1,0:T(8,128)S(1)}, f32[130,256]{1,0:T(8,128)S(1)}, u32[]{:S(2)}, u32[]{:S(2)}) collective-permute-start(f32[130,256]{1,0:T(8,128)S(1)} %pad_maximum_fusion.1), channel_id=1, source_target_pairs={{0,1},{1,0},{2,3},{3,2},{4,5},{5,4},{6,7},{7,6},{8,9},{9,8},{10,11... | collective-permute-start | bytes 399368 | tf_op jit(solution)/shard_map/ppermute | solution.py:235
  94.2 6.0 %collective-permute-start.2 = (f32[130,256]{1,0:T(8,128)S(1)}, f32[130,256]{1,0:T(8,128)S(1)}, u32[]{:S(2)}, u32[]{:S(2)}) collective-permute-start(f32[130,256]{1,0:T(8,128)S(1)} %fusion), channel_id=1, source_target_pairs={{0,2},{1,3},{2,0},{3,1},{4,6},{5,7},{6,4},{7,5},{8,10},{9,11},{10,... | collective-permute-start | bytes 399368 | tf_op jit(solution)/shard_map/ppermute | solution.py:235
  100.2 5.1 %collective-permute-start.3 = (f32[130,256]{1,0:T(8,128)S(1)}, f32[130,256]{1,0:T(8,128)S(1)}, u32[]{:S(2)}, u32[]{:S(2)}) collective-permute-start(f32[130,256]{1,0:T(8,128)S(1)} %add.32), channel_id=1, source_target_pairs={{0,4},{1,5},{2,6},{3,7},{4,0},{5,1},{6,2},{7,3},{8,12},{9,13},{10,... | collective-permute-start | bytes 399368 | tf_op jit(solution)/shard_map/ppermute | solution.py:235
  105.4 5.1 %collective-permute-start.4 = (f32[130,256]{1,0:T(8,128)S(1)}, f32[130,256]{1,0:T(8,128)S(1)}, u32[]{:S(2)}, u32[]{:S(2)}) collective-permute-start(f32[130,256]{1,0:T(8,128)S(1)} %add.33), channel_id=1, source_target_pairs={{0,8},{1,9},{2,10},{3,11},{4,12},{5,13},{6,14},{7,15},{8,0},{9,1},... | collective-permute-start | bytes 399368 | tf_op jit(solution)/shard_map/ppermute | solution.py:235
  110.5 7.5 %collective-permute-start.5 = (f32[130,256]{1,0:T(8,128)S(1)}, f32[130,256]{1,0:T(8,128)S(1)}, u32[]{:S(2)}, u32[]{:S(2)}) collective-permute-start(f32[130,256]{1,0:T(8,128)S(1)} %add.34), channel_id=1, source_target_pairs={{0,16},{1,17},{2,18},{3,19},{4,20},{5,21},{6,22},{7,23},{8,24},{9,... | collective-permute-start | bytes 399368 | tf_op jit(solution)/shard_map/ppermute | solution.py:235
  153.8 6.3 %copy-start.1 = (bf16[256,16384]{1,0:T(8,128)(2,1)S(1)}, bf16[256,16384]{1,0:T(8,128)(2,1)}, u32[]{:S(2)}) copy-start(bf16[256,16384]{1,0:T(8,128)(2,1)} %get-tuple-element.12) | copy-start | bytes 25165828
  155.0 6.3 %copy-start.4 = (f32[256]{0:T(256)}, f32[256]{0:T(256)S(1)}, u32[]{:S(2)}) copy-start(f32[256]{0:T(256)S(1)} %slice_reduce_fusion) | copy-start | bytes 3076
  155.0 6.3 %copy-start.2 = (bf16[32768]{0:T(1024)(128)(2,1)S(1)}, bf16[32768]{0:T(1024)(128)(2,1)}, u32[]{:S(2)}) copy-start(bf16[32768]{0:T(1024)(128)(2,1)} %param.4) | copy-start | bytes 196612

commit v14 on v13

--- a/solution.py
+++ b/solution.py
@@ -40,7 +40,7 @@
 WIDE_CHUNK = 4096
 
 
-def feature_kernel(dilations, span, base, first_block, taps_per_filter, w_ref, taps_ref, tgt_ref, f_ref, g_ref, c_ref):
+def feature_kernel(dilations, span, base, first_block, taps_per_filter, w_ref, taps_ref, tgt_ref, f_ref, g_ref, c_ref, *shifted_ref):
     block = pl.program_id(0)
     block_len = f_ref.shape[1]
     channels = w_ref.shape[0]
@@ -50,7 +50,21 @@
     def _():
         g_ref[...] = jnp.zeros_like(g_ref)
         c_ref[...] = jnp.zeros_like(c_ref)
-
+        if shifted_ref:
+            out = shifted_ref[0]
+            head = w_ref[:, 0:1024].astype(jnp.float32)
+            head = jnp.concatenate([jnp.zeros_like(head[:, :128]), head], 1)
+            out[:, 0:1024] = head[:, 127:1151].astype(out.dtype)
+
+            def delay(i, carry):
+                at = pl.multiple_of(i * 1024, 128)
+                slab = w_ref[:, pl.ds(at - 128, 1152)].astype(jnp.float32)
+                out[:, pl.ds(at, 1024)] = slab[:, 127:1151].astype(out.dtype)
+                return carry
+
+            lax.fori_loop(1, w_ref.shape[1] // 1024, delay, 0)
+
+    w_ref = shifted_ref[0] if shifted_ref else w_ref
     for j, d in enumerate(dilations):
         chunk = min(block_len, NARROW_CHUNK if d % 64 else WIDE_CHUNK)
         for g in range(channels // group):
@@ -83,7 +97,7 @@
     c_ref[...] += lax.dot_general(tgt_ref[...], feats, (((1,), (1,)), ((), ())), preferred_element_type=jnp.float32)
 
 
-def features_and_sums(window, base, first_block, n_blocks, depthwise_taps, target, top_dilation, length, interpret=False):
+def features_and_sums(window, base, first_block, n_blocks, depthwise_taps, target, top_dilation, length, interpret=False, delay=False):
     channels = window.shape[0]
     dilations = dilation_list(top_dilation)
     n_filters, taps_per_filter = len(dilations), depthwise_taps.shape[1]
@@ -113,6 +127,7 @@
             jax.ShapeDtypeStruct((rows, rows), jnp.float32),
             jax.ShapeDtypeStruct((1, rows), jnp.float32),
         ],
+        scratch_shapes=[pltpu.VMEM(window.shape, window.dtype)] if delay else [],
         compiler_params=pltpu.CompilerParams(
             dimension_semantics=("arbitrary",), vmem_limit_bytes=48 * 1024 * 1024
         ),
@@ -264,9 +279,8 @@
         window, 0, 0, split, depthwise_taps, target, top_dilation, length
     )
     if split < n_blocks:
-        delayed = jnp.concatenate([jnp.zeros_like(stream[:, :1]), stream[:, : length - 1]], 1)
         late_features, late_gram, late_cross = features_and_sums(
-            delayed, span, split, n_blocks - split, depthwise_taps, target, top_dilation, length
+            stream, span, split, n_blocks - split, depthwise_taps, target, top_dilation, length, delay=True
         )
         features = (features, late_features)
         gram_sum, cross_sum = gram_sum + late_gram, cross_sum + late_cross

time: 162 us -> 164 us (1.012)
  local copies, waits for them, and re-layouts: 11.5 us -> 6.83 us
  Pallas kernels: 109 us -> 113 us
  matrix products: 6.29 us -> 9.18 us
    concatenate x1 -> x0, local copies, waits for them, and re-layouts: 5.46 us -> none  [local(): jnp.concatenate([jnp.zeros_like(stream[:, :1]), stream[:, :length - 1]], 1)]
    pallas_call x2, Pallas kernels: 74.3 us -> 77.9 us  [features_and_sums(): pl.pallas_call(kernel, grid=(n_blocks,), in_specs=[pl.BlockSpec(memory_sp...]
    dot_general x2, matrix products: 6.29 us -> 9.18 us  [local(): jnp.dot(rounded, f, preferred_element_type=jnp.float32)]
  transfers between devices with their start and end apart: 6 -> 6, of which waited for: 5 -> 5; matrix products, arithmetic and copies ran while one was open for 4% -> 1% of each run, Pallas kernels for 23% -> 25%
where the time goes in v14:
time: 164 us
  Pallas kernels  113 us (69%)
  waiting for transfers between devices  17.4 us (11%)
  starting transfers between devices  12.4 us (8%)
  matrix products  9.18 us (6%)
  local copies, waits for them, and re-layouts  6.83 us (4%)
  other arithmetic  4.13 us (3%)
    pallas_call x2, Pallas kernels, features_and_sums(): pl.pallas_call(kernel, grid=(n_blocks,), in_specs=[pl.BlockSpec(memory_sp...  77.9 us
    pallas_call x1, Pallas kernels, ridge_solve_packed(): pl.pallas_call(functools.partial(jordan_kernel, ridge), in_specs=[pl.Bloc...  35.1 us
    ppermute x5, waiting for transfers between devices, butterfly_sum(): x = x + lax.ppermute(x, axes, [(i, i ^ step) for i in range(size)])  17.4 us
    ppermute x5, starting transfers between devices, butterfly_sum(): x = x + lax.ppermute(x, axes, [(i, i ^ step) for i in range(size)])  9.91 us
    dot_general x2, matrix products, local(): jnp.dot(rounded, f, preferred_element_type=jnp.float32)  9.18 us
  transfers between devices with their start and end apart: 6, of which 5 were waited for; matrix products, arithmetic and copies ran while one was open for 1% of the time, Pallas kernels for 25%

profile of v14, /device:TPU:0, one launch (start us, length us, event | category | flops | bytes accessed | tf_op | source)
XLA Modules:
  0.0 163.8 jit_solution(1236307211091473069)
XLA Ops:
  0.6 0.0 copy-start
  0.6 2.3 %slice.18 = bf16[64,15361]{1,0:T(8,128)(2,1)S(1)} slice(bf16[64,32768]{1,0:T(8,128)(2,1)} %w_ref.1), slice={[0:64], [17407:32768]} | slice | bytes 3932416 | tf_op jit(solution)/shard_map/slice | solution.py:271
  2.9 2.5 %collective-permute-start = (bf16[64,15361]{1,0:T(8,128)(2,1)S(1)}, bf16[64,15361]{1,0:T(8,128)(2,1)S(1)}, u32[]{:S(2)}, u32[]{:S(2)}) collective-permute-start(bf16[64,15361]{1,0:T(8,128)(2,1)S(1)} %slice.18), channel_id=1, source_target_pairs={{0,1},{1,2},{2,3},{3,4},{4,5},{5,6},{6,7},{7,8},{8,9},{9,10},{10,1... | collective-permute-start | bytes 5898632 | tf_op jit(solution)/shard_map/ppermute | solution.py:16
  5.5 0.9 reshape.9.tgt_ref
  6.4 1.4 broadcast_in_dim.7.taps_ref
  7.7 40.8 %shard_map.51 = (bf16[256,16384]{1,0:T(8,128)(2,1)}, f32[256,256]{1,0:T(8,128)S(1)}, f32[1,256]{1,0:T(1,128)S(1)}) custom-call(bf16[64,32768]{1,0:T(8,128)(2,1)} %w_ref.1, f32[64,64,128]{2,1,0:T(8,128)S(1)} %broadcast_in_dim.7.taps_ref, bf16[1,32768]{1,0:T(2,128)(2,1)S(1)} %reshape.9.tgt_ref), custom_call_target="tpu_custom_call" | custom-call | tf_op jit(solution)/shard_map/pallas_call | solution.py:112
  48.5 0.0 collective-permute-done
  48.5 0.0 copy-done
  48.5 2.6 %pad_maximum_fusion.w_ref = bf16[64,31744]{1,0:T(8,128)(2,1)} fusion(bf16[64,32768]{1,0:T(8,128)(2,1)S(1)} %copy-done, bf16[64,15361]{1,0:T(8,128)(2,1)S(1)} %collective-permute-done), kind=kLoop, calls=%fused_computation.1 | loop fusion | flops 8126464 | bytes 10223744 | tf_op jit(solution)/shard_map/concatenate | solution.py:277
  51.2 37.1 %shard_map.50 = (bf16[256,16384]{1,0:T(8,128)(2,1)}, f32[256,256]{1,0:T(8,128)S(1)}, f32[1,256]{1,0:T(1,128)S(1)}) custom-call(bf16[64,31744]{1,0:T(8,128)(2,1)} %pad_maximum_fusion.w_ref, f32[64,64,128]{2,1,0:T(8,128)S(1)} %broadcast_in_dim.7.taps_ref, bf16[1,32768]{1,0:T(2,128)(2,1)S(1)} %reshape.9.tgt_ref), custom_call_target="tpu_custom_call" | custom-call | tf_op jit(solution)/shard_map/pallas_call | solution.py:112
  88.3 1.2 gather_fusion
  89.6 2.6 %collective-permute-start.1 = (f32[130,256]{1,0:T(8,128)S(1)}, f32[130,256]{1,0:T(8,128)S(1)}, u32[]{:S(2)}, u32[]{:S(2)}) collective-permute-start(f32[130,256]{1,0:T(8,128)S(1)} %pad_maximum_fusion.1), channel_id=1, source_target_pairs={{0,1},{1,0},{2,3},{3,2},{4,5},{5,4},{6,7},{7,6},{8,9},{9,8},{10,11... | collective-permute-start | bytes 399368 | tf_op jit(solution)/shard_map/ppermute | solution.py:250
  92.2 1.0 collective-permute-done.1
  93.2 1.5 collective-permute-start.2
  94.7 4.5 %collective-permute-done.2 = f32[130,256]{1,0:T(8,128)S(1)} collective-permute-done((f32[130,256]{1,0:T(8,128)S(1)}, f32[130,256]{1,0:T(8,128)S(1)}, u32[]{:S(2)}, u32[]{:S(2)}) %collective-permute-start.2) | collective-permute-done | bytes 133152 | tf_op jit(solution)/shard_map/ppermute | solution.py:250
  99.3 1.6 collective-permute-start.3
  100.8 3.6 %collective-permute-done.3 = f32[130,256]{1,0:T(8,128)S(1)} collective-permute-done((f32[130,256]{1,0:T(8,128)S(1)}, f32[130,256]{1,0:T(8,128)S(1)}, u32[]{:S(2)}, u32[]{:S(2)}) %collective-permute-start.3) | collective-permute-done | bytes 133152 | tf_op jit(solution)/shard_map/ppermute | solution.py:250
  104.4 1.6 %collective-permute-start.4 = (f32[130,256]{1,0:T(8,128)S(1)}, f32[130,256]{1,0:T(8,128)S(1)}, u32[]{:S(2)}, u32[]{:S(2)}) collective-permute-start(f32[130,256]{1,0:T(8,128)S(1)} %add.31), channel_id=1, source_target_pairs={{0,8},{1,9},{2,10},{3,11},{4,12},{5,13},{6,14},{7,15},{8,0},{9,1},... | collective-permute-start | bytes 399368 | tf_op jit(solution)/shard_map/ppermute | solution.py:250
  106.1 3.5 %collective-permute-done.4 = f32[130,256]{1,0:T(8,128)S(1)} collective-permute-done((f32[130,256]{1,0:T(8,128)S(1)}, f32[130,256]{1,0:T(8,128)S(1)}, u32[]{:S(2)}, u32[]{:S(2)}) %collective-permute-start.4) | collective-permute-done | bytes 133152 | tf_op jit(solution)/shard_map/ppermute | solution.py:250
  109.6 2.7 %collective-permute-start.5 = (f32[130,256]{1,0:T(8,128)S(1)}, f32[130,256]{1,0:T(8,128)S(1)}, u32[]{:S(2)}, u32[]{:S(2)}) collective-permute-start(f32[130,256]{1,0:T(8,128)S(1)} %add.32), channel_id=1, source_target_pairs={{0,16},{1,17},{2,18},{3,19},{4,20},{5,21},{6,22},{7,23},{8,24},{9,... | collective-permute-start | bytes 399368 | tf_op jit(solution)/shard_map/ppermute | solution.py:250
  112.2 4.9 %collective-permute-done.5 = f32[130,256]{1,0:T(8,128)S(1)} collective-permute-done((f32[130,256]{1,0:T(8,128)S(1)}, f32[130,256]{1,0:T(8,128)S(1)}, u32[]{:S(2)}, u32[]{:S(2)}) %collective-permute-start.5) | collective-permute-done | bytes 133152 | tf_op jit(solution)/shard_map/ppermute | solution.py:250
  117.1 0.7 add.33.packed_ref
  117.8 35.1 %shard_map.52 = f32[256,128]{1,0:T(8,128)} custom-call(f32[130,256]{1,0:T(8,128)} %add.33.packed_ref), custom_call_target="tpu_custom_call" | custom-call | tf_op jit(solution)/shard_map/pallas_call | solution.py:223
  152.9 1.0 slice_reduce_fusion
  153.9 0.0 copy-start.2
  153.9 0.0 copy-start.1
  154.0 4.6 %fusion.1 = f32[1,16384]{1,0:T(1,128)S(1)} fusion(bf16[256,1]{0,1:T(2,128)(2,1)S(1)} %reshape.18, bf16[256,16384]{1,0:T(8,128)(2,1)} %get-tuple-element.12), kind=kOutput, calls=%fused_computation.9 | convolution fusion | flops 8388608 | bytes 8454656 | tf_op jit(solution)/shard_map/dot_general | solution.py:294
  158.6 4.6 %fusion.2 = f32[1,16384]{1,0:T(1,128)S(1)} fusion(bf16[256,1]{0,1:T(2,128)(2,1)S(1)} %reshape.18, bf16[256,16384]{1,0:T(8,128)(2,1)} %get-tuple-element.13), kind=kOutput, calls=%fused_computation.10 | convolution fusion | flops 8388608 | bytes 8454656 | tf_op jit(solution)/shard_map/dot_general | solution.py:294
  163.1 0.0 copy-done.2
  163.1 0.0 copy-done.1
  163.1 0.7 maximum_subtract_fusion
  (12 shorter events, 0.2 us)
Async XLA Ops:
  0.6 47.9 %copy-start = (bf16[64,32768]{1,0:T(8,128)(2,1)S(1)}, bf16[64,32768]{1,0:T(8,128)(2,1)}, u32[]{:S(2)}) copy-start(bf16[64,32768]{1,0:T(8,128)(2,1)} %w_ref.1) | copy-start | bytes 12582916
  2.9 45.6 %collective-permute-start = (bf16[64,15361]{1,0:T(8,128)(2,1)S(1)}, bf16[64,15361]{1,0:T(8,128)(2,1)S(1)}, u32[]{:S(2)}, u32[]{:S(2)}) collective-permute-start(bf16[64,15361]{1,0:T(8,128)(2,1)S(1)} %slice.18), channel_id=1, source_target_pairs={{0,1},{1,2},{2,3},{3,4},{4,5},{5,6},{6,7},{7,8},{8,9},{9,10},{10,1... | collective-permute-start | bytes 5898632 | tf_op jit(solution)/shard_map/ppermute | solution.py:16
  89.6 3.6 %collective-permute-start.1 = (f32[130,256]{1,0:T(8,128)S(1)}, f32[130,256]{1,0:T(8,128)S(1)}, u32[]{:S(2)}, u32[]{:S(2)}) collective-permute-start(f32[130,256]{1,0:T(8,128)S(1)} %pad_maximum_fusion.1), channel_id=1, source_target_pairs={{0,1},{1,0},{2,3},{3,2},{4,5},{5,4},{6,7},{7,6},{8,9},{9,8},{10,11... | collective-permute-start | bytes 399368 | tf_op jit(solution)/shard_map/ppermute | solution.py:250
  93.2 6.0 %collective-permute-start.2 = (f32[130,256]{1,0:T(8,128)S(1)}, f32[130,256]{1,0:T(8,128)S(1)}, u32[]{:S(2)}, u32[]{:S(2)}) collective-permute-start(f32[130,256]{1,0:T(8,128)S(1)} %fusion), channel_id=1, source_target_pairs={{0,2},{1,3},{2,0},{3,1},{4,6},{5,7},{6,4},{7,5},{8,10},{9,11},{10,... | collective-permute-start | bytes 399368 | tf_op jit(solution)/shard_map/ppermute | solution.py:250
  99.3 5.1 %collective-permute-start.3 = (f32[130,256]{1,0:T(8,128)S(1)}, f32[130,256]{1,0:T(8,128)S(1)}, u32[]{:S(2)}, u32[]{:S(2)}) collective-permute-start(f32[130,256]{1,0:T(8,128)S(1)} %add.30), channel_id=1, source_target_pairs={{0,4},{1,5},{2,6},{3,7},{4,0},{5,1},{6,2},{7,3},{8,12},{9,13},{10,... | collective-permute-start | bytes 399368 | tf_op jit(solution)/shard_map/ppermute | solution.py:250
  104.4 5.1 %collective-permute-start.4 = (f32[130,256]{1,0:T(8,128)S(1)}, f32[130,256]{1,0:T(8,128)S(1)}, u32[]{:S(2)}, u32[]{:S(2)}) collective-permute-start(f32[130,256]{1,0:T(8,128)S(1)} %add.31), channel_id=1, source_target_pairs={{0,8},{1,9},{2,10},{3,11},{4,12},{5,13},{6,14},{7,15},{8,0},{9,1},... | collective-permute-start | bytes 399368 | tf_op jit(solution)/shard_map/ppermute | solution.py:250
  109.6 7.5 %collective-permute-start.5 = (f32[130,256]{1,0:T(8,128)S(1)}, f32[130,256]{1,0:T(8,128)S(1)}, u32[]{:S(2)}, u32[]{:S(2)}) collective-permute-start(f32[130,256]{1,0:T(8,128)S(1)} %add.32), channel_id=1, source_target_pairs={{0,16},{1,17},{2,18},{3,19},{4,20},{5,21},{6,22},{7,23},{8,24},{9,... | collective-permute-start | bytes 399368 | tf_op jit(solution)/shard_map/ppermute | solution.py:250
  153.9 9.2 %copy-start.2 = (f32[256]{0:T(256)}, f32[256]{0:T(256)S(1)}, u32[]{:S(2)}) copy-start(f32[256]{0:T(256)S(1)} %slice_reduce_fusion) | copy-start | bytes 3076
  153.9 9.2 %copy-start.1 = (bf16[32768]{0:T(1024)(128)(2,1)S(1)}, bf16[32768]{0:T(1024)(128)(2,1)}, u32[]{:S(2)}) copy-start(bf16[32768]{0:T(1024)(128)(2,1)} %param.4) | copy-start | bytes 196612
